TPU v7x, 512 devices: a whole 4x8x8 slice. The times are simulated.
512 devices in a mesh: dp: 8 (over y), expert: 64 (over x, z, core).
Axes of the slice: x: 4, y: 8, z: 8, core: 2. Of those that a mesh axis runs over, the one named last changes fastest.
Arguments:
- tokens: bfloat16 [65536, 3584], P(('dp', 'expert')), may hold values from -6 to 6
- out_cotangent: bfloat16 [65536, 3584], P(('dp', 'expert')), may hold values from -6 to 6
- expert_ids: int32 [65536, 8], P(('dp', 'expert')), may hold values from 0 to 255, as said below
- gate_fixed: int32 [65536, 8], P(('dp', 'expert')), may hold values from 4096 to 65535
- w_gate: bfloat16 [64, 3584, 128], P('expert', 'dp'), may hold values from -0.09375 to 0.09375
- w_up: bfloat16 [64, 3584, 128], P('expert', 'dp'), may hold values from -0.09375 to 0.09375
- w_down: bfloat16 [64, 3584, 128], P('expert', 'dp'), may hold values from -0.125 to 0.125
Outputs:
- layer_out: bfloat16 [65536, 3584], P(('dp', 'expert'))
- token_grad: bfloat16 [65536, 3584], P(('dp', 'expert'))
- grad_gate: float32 [64, 3584, 128], P('expert', 'dp')
- grad_up: float32 [64, 3584, 128], P('expert', 'dp')
- grad_down: float32 [64, 3584, 128], P('expert', 'dp')
Inputs may be any that keep to these rules, and one draw needn't show every extreme that they name: `expert_ids`: each row names 8 different experts. Within the 128 rows of one device each expert below 4 is named by 1 to 4 rows; in every draw one expert below 4 is named by exactly 4 rows on every device.
All inputs are finite; a program needn't handle non-finite values.
Results may differ from a plain program's by a relative error of at most 0.014.
Values may be sent and summed in bfloat16 or wider, within the bound.
No kernel may reach another device: no remote copies, remote signals or barrier semaphores. Data moves between devices by JAX's collectives and lax.ppermute only.
A program may use at most 128 MiB of HBM per device.

v0:
```python
import jax
import jax.numpy as jnp
from jax import lax
from jax.sharding import PartitionSpec as P

SPLIT = 16
CAP = 4


SCALE = 2.0 ** (-16)
HIGH = lax.Precision.HIGHEST


def routing(ids, gates, window, capacity):
    wanted = jnp.arange(window, dtype=jnp.int32)
    hits = ids[:, :, None] == wanted[None, None, :]
    member = jnp.any(hits, axis=1)
    weight = jnp.sum(jnp.where(hits, gates[:, :, None], 0), axis=1).astype(jnp.float32) * SCALE
    rank = jnp.cumsum(member.astype(jnp.int32), axis=0) - 1
    slots = jnp.arange(capacity, dtype=jnp.int32)
    pick = jnp.logical_and(member[:, :, None], rank[:, :, None] == slots[None, None, :])
    select = jnp.where(pick, 1.0, 0.0).astype(jnp.float32)
    slot_gate = jnp.sum(select * weight[:, :, None], axis=0)
    return (select, slot_gate)


def expert_math(inputs, cotangents, gate_w, up_w, down_w):
    gate_pre = jnp.einsum("prf,pfh->rh", inputs, gate_w, preferred_element_type=jnp.float32)
    up_pre = jnp.einsum("prf,pfh->rh", inputs, up_w, preferred_element_type=jnp.float32)
    sig = jax.nn.sigmoid(gate_pre)
    act = gate_pre * sig
    hidden = (act * up_pre).astype(jnp.bfloat16)
    partial_out = jnp.einsum("rh,pfh->prf", hidden, down_w, preferred_element_type=jnp.float32)
    d_hidden = jnp.einsum("prf,pfh->rh", cotangents, down_w, preferred_element_type=jnp.float32)
    d_gate = (d_hidden * up_pre * sig * (1.0 + gate_pre * (1.0 - sig))).astype(jnp.bfloat16)
    d_up = (d_hidden * act).astype(jnp.bfloat16)
    partial_grad = jnp.einsum(
        "rh,pfh->prf", d_gate, gate_w, preferred_element_type=jnp.float32
    ) + jnp.einsum("rh,pfh->prf", d_up, up_w, preferred_element_type=jnp.float32)
    term = jnp.concatenate(
        [
            jnp.einsum("prf,rh->pfh", inputs, d_gate, preferred_element_type=jnp.float32),
            jnp.einsum("prf,rh->pfh", inputs, d_up, preferred_element_type=jnp.float32),
            jnp.einsum("prf,rh->pfh", cotangents, hidden, preferred_element_type=jnp.float32),
        ],
        axis=2,
    )
    return (partial_out, partial_grad, term.reshape(-1, term.shape[2]))


def per_device(tokens, out_cotangent, expert_ids, gate_fixed, w_gate, w_up, w_down):
    tok_rows, width = tokens.shape
    groups = lax.axis_size("expert")
    window = groups // SPLIT
    hid = w_gate.shape[2]
    parts = 1
    feat = width // parts
    select, slot_gate = routing(expert_ids, gate_fixed, window, CAP)
    select_b = select.astype(jnp.bfloat16)
    tok3 = tokens.reshape(tok_rows, parts, feat)
    cot3 = out_cotangent.reshape(tok_rows, parts, feat)
    slot_tokens = jnp.einsum(
        "tec,tsf->escf", select_b, tok3, preferred_element_type=jnp.float32
    ).astype(jnp.bfloat16)
    picked = jnp.einsum("tec,tsf->escf", select_b, cot3, preferred_element_type=jnp.float32)
    slot_cot = (picked * slot_gate[:, None, :, None]).astype(jnp.bfloat16)
    payload = jnp.stack([slot_tokens, slot_cot], axis=2)
    gate_full, up_full, down_full = (
        lax.all_gather(w_gate, "dp", axis=1, tiled=True),
        lax.all_gather(w_up, "dp", axis=1, tiled=True),
        lax.all_gather(w_down, "dp", axis=1, tiled=True),
    )
    outgoing = jnp.broadcast_to(payload, (window, SPLIT, 2, CAP, width)).reshape(
        groups, 2, CAP, width
    )
    arrived = lax.all_to_all(outgoing, "expert", split_axis=0, concat_axis=0, tiled=True)
    pieces = arrived[None]
    inputs = pieces[:, :, 0].reshape(parts, groups * CAP, feat)
    cotangents = pieces[:, :, 1].reshape(parts, groups * CAP, feat)
    partial_out, partial_grad, term = expert_math(inputs, cotangents, gate_full, up_full, down_full)
    summed = lax.psum_scatter(
        term.astype(jnp.bfloat16), "dp", scatter_dimension=0, tiled=True
    ).astype(jnp.float32)
    grad_gate = summed[:, :hid][None]
    grad_up = summed[:, hid : 2 * hid][None]
    grad_down = summed[:, 2 * hid :][None]
    results = jnp.stack(
        [
            partial_out.reshape(parts, groups, CAP, feat),
            partial_grad.reshape(parts, groups, CAP, feat),
        ],
        axis=2,
    )
    returned = lax.all_to_all(
        results[0].astype(jnp.bfloat16), "expert", split_axis=0, concat_axis=0, tiled=True
    ).astype(jnp.float32)
    combined = jnp.sum(
        returned.reshape(window, SPLIT, 2, CAP, width), axis=1, keepdims=True
    ).astype(jnp.bfloat16)
    weighted = select * slot_gate[None, :, :]
    layer_out = jnp.einsum(
        "tec,ehcf->thf", weighted, combined[:, :, 0].astype(jnp.float32), precision=HIGH
    )
    token_grad = jnp.einsum(
        "tec,ehcf->thf", select, combined[:, :, 1].astype(jnp.float32), precision=HIGH
    )
    return (
        layer_out.reshape(tok_rows, width).astype(jnp.bfloat16),
        token_grad.reshape(tok_rows, width).astype(jnp.bfloat16),
        grad_gate,
        grad_up,
        grad_down,
    )


def solution(mesh):
    return jax.shard_map(
        per_device,
        mesh=mesh,
        in_specs=(
            P(("dp", "expert"), None),
            P(("dp", "expert"), None),
            P(("dp", "expert"), None),
            P(("dp", "expert"), None),
            P("expert", "dp", None),
            P("expert", "dp", None),
            P("expert", "dp", None),
        ),
        out_specs=(
            P(("dp", "expert"), None),
            P(("dp", "expert"), None),
            P("expert", "dp", None),
            P("expert", "dp", None),
            P("expert", "dp", None),
        ),
        check_vma=False,
    )
```

profile of v0, /device:TPU:1, one launch (start us, length us, event | category | flops | bytes accessed | tf_op | source)
XLA Modules:
  0.0 262.6 jit_solution(5232182075128742454)
XLA Ops:
  7.2 0.8 fusion.25
  8.3 0.7 select_reduce_fusion
  9.5 1.4 fusion.11
  11.2 2.9 %broadcast_in_dim.54 = bf16[4,16,2,4,3584]{4,3,2,1,0:T(4,128)(2,1)} broadcast(bf16[4,2,4,3584]{3,2,1,0:T(4,128)(2,1)S(1)} %copy.43), dimensions={0,2,3,4} | broadcast | bytes 3899392 | tf_op jit(solution)/shard_map/broadcast_in_dim | solution.py:73
  14.1 15.1 %all-to-all-start = ((bf16[64,2,4,3584]{3,2,1,0:T(4,128)(2,1)}), bf16[64,2,4,3584]{3,2,1,0:T(4,128)(2,1)}, u32[]{:S(2)}, u32[]{:S(2)}) async-start(bf16[64,2,4,3584]{3,2,1,0:T(4,128)(2,1)} %bitcast.111), calls=%async_computation | async-start | bytes 7340032 | tf_op jit(solution)/shard_map/all_to_all | solution.py:76
  29.3 26.0 %all_gather.9 = bf16[1,3584,128]{2,1,0:T(8,128)(2,1)} all-gather(bf16[1,448,128]{2,1,0:T(8,128)(2,1)S(1)} %copy-done.6), channel_id=1, replica_groups=mesh['dp'=8,'expert'=64] {'dp'}, dimensions={1}, use_global_device_ids=true | all-gather | bytes 1032192 | tf_op jit(solution)/shard_map/all_gather | solution.py:69
  55.3 24.1 %all_gather.11 = bf16[1,3584,128]{2,1,0:T(8,128)(2,1)} all-gather(bf16[1,448,128]{2,1,0:T(8,128)(2,1)S(1)} %copy-done.7), channel_id=1, replica_groups=mesh['dp'=8,'expert'=64] {'dp'}, dimensions={1}, use_global_device_ids=true | all-gather | bytes 1032192 | tf_op jit(solution)/shard_map/all_gather | solution.py:71
  79.5 24.1 %all_gather.10 = bf16[1,3584,128]{2,1,0:T(8,128)(2,1)} all-gather(bf16[1,448,128]{2,1,0:T(8,128)(2,1)S(1)} %copy-done.8), channel_id=1, replica_groups=mesh['dp'=8,'expert'=64] {'dp'}, dimensions={1}, use_global_device_ids=true | all-gather | bytes 1032192 | tf_op jit(solution)/shard_map/all_gather | solution.py:70
  103.6 10.4 %all-to-all-done = bf16[64,2,4,3584]{3,2,1,0:T(4,128)(2,1)} async-done(((bf16[64,2,4,3584]{3,2,1,0:T(4,128)(2,1)}), bf16[64,2,4,3584]{3,2,1,0:T(4,128)(2,1)}, u32[]{:S(2)}, u32[]{:S(2)}) %all-to-all-start) | async-done | bytes 3670048 | tf_op jit(solution)/shard_map/all_to_all | solution.py:76
  113.9 5.1 %fusion.42 = (bf16[1,64,1,4,3584]{4,3,2,1,0:T(4,128)(2,1)}, bf16[1,64,1,4,3584]{4,3,2,1,0:T(4,128)(2,1)}) fusion(bf16[1,64,2,4,3584]{4,3,2,1,0:T(4,128)(2,1)} %bitcast.12), kind=kLoop, calls=%fused_computation.71 | loop fusion | bytes 7340032 | tf_op jit(solution)/shard_map/slice | solution.py:79
  119.1 2.9 %reshape.115 = bf16[256,3584]{1,0:T(8,128)(2,1)S(1)} reshape(bf16[1,64,1,4,3584]{4,3,2,1,0:T(4,128)(2,1)} %get-tuple-element.21) | data formatting | bytes 3670016 | tf_op jit(solution)/shard_map/reshape.5
  122.0 4.0 %reshape.119 = bf16[256,3584]{1,0:T(8,128)(2,1)} reshape(bf16[1,64,1,4,3584]{4,3,2,1,0:T(4,128)(2,1)} %get-tuple-element.20) | data formatting | bytes 3670016 | tf_op jit(solution)/shard_map/reshape.24
  126.0 2.0 fusion.20
  130.4 0.6 fusion.18
  131.0 1.9 fusion.2
  132.9 4.1 %stack_reshape.9 = bf16[1,64,1,4,3584]{4,3,1,2,0:T(4,128)(2,1)} reshape(bf16[1,256,3584]{2,1,0:T(8,128)(2,1)} %fusion.2) | data formatting | bytes 3670016 | tf_op jit(solution)/shard_map/stack;reshape | solution.py:87
  137.0 3.1 %fusion.1 = bf16[1,256,3584]{2,1,0:T(8,128)(2,1)} fusion(bf16[256,128]{1,0:T(8,128)(2,1)S(1)} %get-tuple-element.25, bf16[1,3584,128]{2,1,0:T(8,128)(2,1)} %all_gather.11), kind=kOutput, calls=%fused_computation.3 | convolution fusion | flops 235798528 | bytes 2818048 | tf_op jit(solution)/shard_map/rh,pfh->prf/dot_general | solution.py:33
  140.1 4.1 %stack_reshape.8 = bf16[1,64,1,4,3584]{4,3,1,2,0:T(4,128)(2,1)} reshape(bf16[1,256,3584]{2,1,0:T(8,128)(2,1)} %fusion.1) | data formatting | bytes 3670016 | tf_op jit(solution)/shard_map/stack;reshape | solution.py:87
  144.1 6.3 %maximum_bitcast_fusion = bf16[64,2,4,3584]{3,2,1,0:T(4,128)(2,1)} fusion(bf16[1,64,1,4,3584]{4,3,2,1,0:T(4,128)(2,1)} %bitcast.112, bf16[1,64,1,4,3584]{4,3,2,1,0:T(4,128)(2,1)} %bitcast.113), kind=kLoop, calls=%fused_computation.21 | loop fusion | flops 1835008 | bytes 7340032 | tf_op jit(solution)/shard_map/convert_element_type | solution.py:95
  150.4 13.0 %all-to-all-start.1 = ((bf16[64,2,4,3584]{3,2,1,0:T(4,128)(2,1)}), bf16[64,2,4,3584]{3,2,1,0:T(4,128)(2,1)}, u32[]{:S(2)}, u32[]{:S(2)}) async-start(bf16[64,2,4,3584]{3,2,1,0:T(4,128)(2,1)} %maximum_bitcast_fusion), calls=%async_computation.1 | async-start | bytes 7340032 | tf_op jit(solution)/shard_map/all_to_all | solution.py:94
  164.6 1.0 copy-done.2
  166.1 1.7 maximum_bitcast_fusion.1
  167.8 4.5 %copy.51 = bf16[3584,384]{1,0:T(8,128)(2,1)} copy(bf16[3584,384]{0,1:T(8,128)(2,1)} %maximum_bitcast_fusion.1) | data formatting | bytes 5505024
  172.3 42.9 %reduce-scatter.4.cloned.1.call-done = bf16[448,384]{1,0:T(8,128)(2,1)} async-done(((bf16[3584,384]{1,0:T(8,128)(2,1)}), bf16[448,384]{1,0:T(8,128)(2,1)}) %reduce-scatter.4.cloned.1.call-update) | async-done | bytes 344080
  215.3 1.1 copy.52
  216.6 0.8 copy.48
  217.4 0.8 copy.49
  218.2 0.8 copy.50
  219.0 29.1 %all-to-all-done.1 = bf16[64,2,4,3584]{3,2,1,0:T(4,128)(2,1)} async-done(((bf16[64,2,4,3584]{3,2,1,0:T(4,128)(2,1)}), bf16[64,2,4,3584]{3,2,1,0:T(4,128)(2,1)}, u32[]{:S(2)}, u32[]{:S(2)}) %all-to-all-start.1) | async-done | bytes 3670048 | tf_op jit(solution)/shard_map/all_to_all | solution.py:94
  248.1 3.6 %bitcast_reduce_fusion = bf16[4,2,4,3584]{3,2,1,0:T(4,128)(2,1)S(1)} fusion(bf16[64,2,4,3584]{3,2,1,0:T(4,128)(2,1)} %all-to-all-done.1), kind=kLoop, calls=%fused_computation.22 | loop fusion | flops 1720320 | bytes 3899392 | tf_op jit(solution)/shard_map/reduce_sum | solution.py:97
  251.9 1.9 fusion.4
  253.8 1.9 fusion.3
  (38 shorter events, 5.3 us)
Async XLA Ops:
  7.2 2.1 copy-start
  14.1 15.1 %copy-start.6 = (bf16[1,448,128]{2,1,0:T(8,128)(2,1)S(1)}, bf16[1,448,128]{2,1,0:T(8,128)(2,1)}, u32[]{:S(2)}) copy-start(bf16[1,448,128]{2,1,0:T(8,128)(2,1)} %param.11) | copy-start | bytes 344068
  14.1 41.2 %copy-start.7 = (bf16[1,448,128]{2,1,0:T(8,128)(2,1)S(1)}, bf16[1,448,128]{2,1,0:T(8,128)(2,1)}, u32[]{:S(2)}) copy-start(bf16[1,448,128]{2,1,0:T(8,128)(2,1)} %param.13) | copy-start | bytes 344068
  14.1 99.8 %all-to-all-start = ((bf16[64,2,4,3584]{3,2,1,0:T(4,128)(2,1)}), bf16[64,2,4,3584]{3,2,1,0:T(4,128)(2,1)}, u32[]{:S(2)}, u32[]{:S(2)}) async-start(bf16[64,2,4,3584]{3,2,1,0:T(4,128)(2,1)} %bitcast.111), calls=%async_computation | async-start | bytes 7340032 | tf_op jit(solution)/shard_map/all_to_all | solution.py:76
  29.3 50.2 %copy-start.8 = (bf16[1,448,128]{2,1,0:T(8,128)(2,1)S(1)}, bf16[1,448,128]{2,1,0:T(8,128)(2,1)}, u32[]{:S(2)}) copy-start(bf16[1,448,128]{2,1,0:T(8,128)(2,1)} %param.12) | copy-start | bytes 344068
  126.0 2.0 copy-start.1
  126.0 2.0 copy-start.3
  128.0 1.2 copy-start.5
  129.2 1.2 copy-start.4
  150.4 97.7 %all-to-all-start.1 = ((bf16[64,2,4,3584]{3,2,1,0:T(4,128)(2,1)}), bf16[64,2,4,3584]{3,2,1,0:T(4,128)(2,1)}, u32[]{:S(2)}, u32[]{:S(2)}) async-start(bf16[64,2,4,3584]{3,2,1,0:T(4,128)(2,1)} %maximum_bitcast_fusion), calls=%async_computation.1 | async-start | bytes 7340032 | tf_op jit(solution)/shard_map/all_to_all | solution.py:94
  163.4 51.8 %reduce-scatter.4.cloned.1.call-start = ((), (), s32[]{:S(2)}) async-start(), calls=%async_computation.3 | async-start | bytes 3096576
  164.2 1.5 copy-start.2
Sparse Core Ops, SparseCore 0:
  172.5 42.7 reduce-scatter.3
where the time goes:
time: 264 us; the launch traced here: 263 us
  waiting for transfers between devices  82.4 us (31%)
  blocking collectives  74.3 us (28%)
  local copies, waits for them, and re-layouts  34 us (13%)
  starting transfers between devices  28.4 us (11%)
  matrix products  15.7 us (6%)
  between operations  14.2 us (5%)
  other arithmetic  13.7 us (5%)
    unnamed x2, waiting for transfers between devices  42.9 us
    all_to_all x1, waiting for transfers between devices, per_device(): lax.all_to_all(results[0].astype(jnp.bfloat16), 'expert', split_axis=0, c...  29.1 us
    all_gather x1, blocking collectives, per_device(): lax.all_gather(w_gate, 'dp', axis=1, tiled=True)  26 us
    all_gather x1, blocking collectives, per_device(): lax.all_gather(w_down, 'dp', axis=1, tiled=True)  24.1 us
    all_gather x1, blocking collectives, per_device(): lax.all_gather(w_up, 'dp', axis=1, tiled=True)  24.1 us
    all_to_all x1, starting transfers between devices, per_device(): lax.all_to_all(outgoing, 'expert', split_axis=0, concat_axis=0, tiled=True)  15.1 us
    all_to_all x1, starting transfers between devices, per_device(): lax.all_to_all(results[0].astype(jnp.bfloat16), 'expert', split_axis=0, c...  13 us
    all_to_all x1, waiting for transfers between devices, per_device(): lax.all_to_all(outgoing, 'expert', split_axis=0, concat_axis=0, tiled=True)  10.4 us
  transfers between devices with their start and end apart: 3, of which 3 were waited for; matrix products, arithmetic and copies ran while one was open for 4% of the time, Pallas kernels for 0%

commit v1 on v0

v1 whole, which is shorter than its diff:
```python
import jax
import jax.numpy as jnp
from jax import lax
from jax.sharding import Mesh
from jax.sharding import PartitionSpec as P

SPLIT = 16
CAP = 4


SCALE = 2.0 ** (-16)
HIGH = lax.Precision.HIGHEST
TOK = ("dp", "ex", "eh")


def routing(ids, gates, window, capacity):
    wanted = jnp.arange(window, dtype=jnp.int32)
    hits = ids[:, :, None] == wanted[None, None, :]
    member = jnp.any(hits, axis=1)
    weight = jnp.sum(jnp.where(hits, gates[:, :, None], 0), axis=1).astype(jnp.float32) * SCALE
    rank = jnp.cumsum(member.astype(jnp.int32), axis=0) - 1
    slots = jnp.arange(capacity, dtype=jnp.int32)
    pick = jnp.logical_and(member[:, :, None], rank[:, :, None] == slots[None, None, :])
    select = jnp.where(pick, 1.0, 0.0).astype(jnp.float32)
    slot_gate = jnp.sum(select * weight[:, :, None], axis=0)
    return (select, slot_gate)


def expert_math(inputs, cotangents, w_all, hid):
    gate_w = w_all[:, :hid]
    up_w = w_all[:, hid : 2 * hid]
    down_w = w_all[:, 2 * hid :]
    f32 = jnp.float32
    gate_pre = jnp.dot(inputs, gate_w, preferred_element_type=f32)
    up_pre = jnp.dot(inputs, up_w, preferred_element_type=f32)
    sig = jax.nn.sigmoid(gate_pre)
    act = gate_pre * sig
    hidden = (act * up_pre).astype(jnp.bfloat16)
    partial_out = lax.dot_general(hidden, down_w, (((1,), (1,)), ((), ())), preferred_element_type=f32)
    d_hidden = jnp.dot(cotangents, down_w, preferred_element_type=f32)
    d_gate = (d_hidden * up_pre * sig * (1.0 + gate_pre * (1.0 - sig))).astype(jnp.bfloat16)
    d_up = (d_hidden * act).astype(jnp.bfloat16)
    partial_grad = lax.dot_general(
        d_gate, gate_w, (((1,), (1,)), ((), ())), preferred_element_type=f32
    ) + lax.dot_general(d_up, up_w, (((1,), (1,)), ((), ())), preferred_element_type=f32)
    tn = (((0,), (0,)), ((), ()))
    term = jnp.concatenate(
        [
            lax.dot_general(inputs, d_gate, tn, preferred_element_type=f32),
            lax.dot_general(inputs, d_up, tn, preferred_element_type=f32),
            lax.dot_general(cotangents, hidden, tn, preferred_element_type=f32),
        ],
        axis=1,
    )
    return (partial_out, partial_grad, term)


def per_device(tokens, out_cotangent, expert_ids, gate_fixed, w_gate, w_up, w_down):
    tok_rows, width = tokens.shape
    window = lax.axis_size("ex")
    hsplit = lax.axis_size("eh")
    hid = w_gate.shape[2]
    select, slot_gate = routing(expert_ids, gate_fixed, window, CAP)
    select_b = select.astype(jnp.bfloat16)
    slot_tokens = jnp.einsum(
        "tec,tf->ecf", select_b, tokens, preferred_element_type=jnp.float32
    ).astype(jnp.bfloat16)
    picked = jnp.einsum("tec,tf->ecf", select_b, out_cotangent, preferred_element_type=jnp.float32)
    slot_cot = (picked * slot_gate[:, :, None]).astype(jnp.bfloat16)
    payload = jnp.stack([slot_tokens, slot_cot], axis=1)
    w_loc = jnp.concatenate([w_gate[0], w_up[0], w_down[0]], axis=1)
    w_all = lax.all_gather(w_loc, "dp", axis=0, tiled=False)
    w_all = w_all.reshape(-1, 3 * hid)
    by_x = lax.all_to_all(payload, "ex", split_axis=0, concat_axis=0, tiled=True)
    arrived = lax.all_gather(by_x, "eh", axis=0, tiled=False)
    inputs = arrived[:, :, 0].reshape(hsplit * window * CAP, width)
    cotangents = arrived[:, :, 1].reshape(hsplit * window * CAP, width)
    partial_out, partial_grad, term = expert_math(inputs, cotangents, w_all, hid)
    summed = lax.psum_scatter(
        term.astype(jnp.bfloat16), "dp", scatter_dimension=0, tiled=True
    ).astype(jnp.float32)
    grad_gate = summed[:, :hid][None]
    grad_up = summed[:, hid : 2 * hid][None]
    grad_down = summed[:, 2 * hid :][None]
    results = jnp.stack(
        [
            partial_out.reshape(hsplit, window, CAP, width),
            partial_grad.reshape(hsplit, window, CAP, width),
        ],
        axis=2,
    ).astype(jnp.bfloat16)
    reduced = lax.psum_scatter(results, "eh", scatter_dimension=0, tiled=True)
    combined = lax.all_to_all(reduced[0], "ex", split_axis=0, concat_axis=0, tiled=True)
    combined = combined.astype(jnp.float32)
    weighted = select * slot_gate[None, :, :]
    layer_out = jnp.einsum("tec,ecf->tf", weighted, combined[:, 0], precision=HIGH)
    token_grad = jnp.einsum("tec,ecf->tf", select, combined[:, 1], precision=HIGH)
    return (
        layer_out.astype(jnp.bfloat16),
        token_grad.astype(jnp.bfloat16),
        grad_gate,
        grad_up,
        grad_down,
    )


def solution(mesh):
    n_dp = mesh.shape["dp"]
    n_exp = mesh.shape["expert"]
    devices = mesh.devices.reshape(n_dp, n_exp // SPLIT, SPLIT)
    grid = Mesh(devices, ("dp", "ex", "eh"))
    tok = P(TOK, None)
    wsp = P(("ex", "eh"), "dp", None)
    return jax.shard_map(
        per_device,
        mesh=grid,
        in_specs=(tok, tok, tok, tok, wsp, wsp, wsp),
        out_specs=(tok, tok, wsp, wsp, wsp),
        check_vma=False,
    )
```

time: 264 us -> 330 us (1.25)
  waiting for transfers between devices: 82.4 us -> 228 us
  blocking collectives: 74.3 us -> 19.2 us
  starting transfers between devices: 28.4 us -> 0.35 us
  other arithmetic: 13.7 us -> 8.88 us
  local copies, waits for them, and re-layouts: 34 us -> 38.4 us
    unnamed x2 -> x6, waiting for transfers between devices: 42.9 us -> 147 us
    all_gather x0 -> x2, waiting for transfers between devices: none -> 80 us  [the longest x1 48.8 us: per_device(): arrived = lax.all_gather(by_x, 'eh', axis=0, tiled=False)]
    all_gather x3 -> x0, blocking collectives: 74.3 us -> none  [the longest x1 26 us: per_device(): lax.all_gather(w_gate, 'dp', axis=1, tiled=True)]
    all_to_all x2 -> x0, waiting for transfers between devices: 39.4 us -> none  [the longest x1 29.1 us: per_device(): lax.all_to_all(results[0].astype(jnp.bfloat16), 'expert', split_axis=0, c...]
    all_to_all x2 -> x0, starting transfers between devices: 28.1 us -> none  [the longest x1 15.1 us: per_device(): lax.all_to_all(outgoing, 'expert', split_axis=0, concat_axis=0, tiled=True)]
    all_to_all x0 -> x2, blocking collectives: none -> 19.2 us  [the longest x1 10.1 us: per_device(): lax.all_to_all(payload, 'ex', split_axis=0, concat_axis=0, tiled=True)]
    convert_element_type x2 -> x0, other arithmetic: 7.98 us -> none  [the longest x1 6.27 us: per_device(): results[0].astype(jnp.bfloat16)]
    another operation x4 -> x7, local copies, waits for them, and re-layouts: 15 us -> 21.3 us  [the longest x4 14.3 us: per_device(): jnp.stack([partial_out.reshape(hsplit, window, CAP, width), partial_grad....]
  transfers between devices with their start and end apart: 3 -> 4, of which waited for: 3 -> 4; matrix products, arithmetic and copies ran while one was open for 4% -> 9% of each run, Pallas kernels for 0% -> 0%
where the time goes in v1:
time: 330 us; the launch traced here: 327 us
  waiting for transfers between devices  228 us (69%)
  local copies, waits for them, and re-layouts  38.4 us (12%)
  blocking collectives  19.2 us (6%)
  matrix products  18.4 us (6%)
  between operations  14 us (4%)
  other arithmetic  8.88 us (3%)
    unnamed x6, waiting for transfers between devices  147 us
    all_gather x1, waiting for transfers between devices, per_device(): arrived = lax.all_gather(by_x, 'eh', axis=0, tiled=False)  48.8 us
    all_gather x1, waiting for transfers between devices, per_device(): w_all = lax.all_gather(w_loc, 'dp', axis=0, tiled=False)  31.2 us
    another operation x4, local copies, waits for them, and re-layouts, per_device(): jnp.stack([partial_out.reshape(hsplit, window, CAP, width), partial_grad....  14.3 us
    all_to_all x1, blocking collectives, per_device(): lax.all_to_all(payload, 'ex', split_axis=0, concat_axis=0, tiled=True)  10.1 us
    unnamed x20, local copies, waits for them, and re-layouts  9.49 us
    all_to_all x1, blocking collectives, per_device(): lax.all_to_all(reduced[0], 'ex', split_axis=0, concat_axis=0, tiled=True)  9.12 us
  transfers between devices with their start and end apart: 4, of which 4 were waited for; matrix products, arithmetic and copies ran while one was open for 9% of the time, Pallas kernels for 0%

profile of v1, /device:TPU:1, one launch (start us, length us, event | category | flops | bytes accessed | tf_op | source)
XLA Modules:
  0.0 326.8 jit_solution(12019169510402515637)
XLA Ops:
  7.2 0.8 fusion.19
  9.5 1.4 fusion.5
  11.2 10.1 %all_to_all.10 = bf16[4,2,4,3584]{3,2,1,0:T(4,128)(2,1)} all-to-all(bf16[4,2,4,3584]{3,2,1,0:T(4,128)(2,1)S(1)} %copy.61), channel_id=1, replica_groups=mesh['dp'=8,'ex'=4,'eh'=16] {'ex'}, dimensions={0} | all-to-all | bytes 458752 | tf_op jit(solution)/shard_map/all_to_all | solution.py:74
  21.4 0.8 pad_maximum_fusion.2
  22.3 48.8 %all-gather.5.cloned.1.call-done = bf16[64,2,4,3584]{3,2,1,0:T(4,128)(2,1)} async-done(((bf16[4,2,4,3584]{3,2,1,0:T(4,128)(2,1)}), bf16[64,2,4,3584]{3,2,1,0:T(4,128)(2,1)}) %all-gather.5.cloned.1.call-update) | async-done | bytes 3670032 | tf_op jit(solution)/shard_map/all_gather | solution.py:75
  71.1 5.5 %fusion.36 = (bf16[16,4,1,4,3584]{4,3,2,1,0:T(4,128)(2,1)}, bf16[16,4,1,4,3584]{4,3,2,1,0:T(4,128)(2,1)}) fusion(bf16[16,4,2,4,3584]{4,3,2,1,0:T(4,128)(2,1)} %bitcast.50), kind=kLoop, calls=%fused_computation.65 | loop fusion | bytes 7340032 | tf_op jit(solution)/shard_map/slice | solution.py:77
  76.6 2.9 reshape_squeeze.6
  79.5 4.0 %reshape_squeeze.7 = bf16[256,3584]{1,0:T(8,128)(2,1)} reshape(bf16[16,4,1,4,3584]{4,3,2,1,0:T(4,128)(2,1)} %get-tuple-element.25) | data formatting | bytes 3670016 | tf_op jit(solution)/shard_map/reshape;squeeze | solution.py:77
  83.5 31.2 %all-gather.7.cloned.1.call-done = bf16[3584,384]{1,0:T(8,128)(2,1)} async-done(((bf16[448,384]{1,0:T(8,128)(2,1)}), bf16[3584,384]{1,0:T(8,128)(2,1)}) %all-gather.7.cloned.1.call-update) | async-done | bytes 2752528 | tf_op jit(solution)/shard_map/all_gather | solution.py:72
  114.7 1.9 fusion.16
  116.7 2.0 fusion.8
  120.0 1.9 fusion
  121.9 4.1 %stack_reshape.9 = bf16[16,4,1,4,3584]{4,3,1,0,2:T(4,128)(2,1)} reshape(bf16[256,3584]{1,0:T(8,128)(2,1)} %fusion) | data formatting | bytes 3670016 | tf_op jit(solution)/shard_map/stack;reshape | solution.py:85
  126.0 3.6 %copy.63 = bf16[16,4,1,4,3584]{4,1,3,2,0:T(4,128)(2,1)} copy(bf16[16,4,1,4,3584]{4,3,1,0,2:T(4,128)(2,1)} %stack_reshape.9) | data formatting | bytes 3670016 | tf_op jit(solution)/shard_map/stack;reshape | solution.py:85
  129.6 3.0 convolution_convert_fusion
  132.7 4.1 %stack_reshape.8 = bf16[16,4,1,4,3584]{4,3,1,0,2:T(4,128)(2,1)} reshape(bf16[256,3584]{1,0:T(8,128)(2,1)} %convolution_convert_fusion) | data formatting | bytes 3670016 | tf_op jit(solution)/shard_map/stack;reshape | solution.py:85
  136.7 2.5 copy.62
  139.3 4.3 %pad_maximum_fusion = bf16[16,4,2,4,3584]{4,1,3,2,0:T(4,128)(2,1)} fusion(bf16[16,4,1,4,3584]{4,1,3,2,0:T(4,128)(2,1)S(1)} %copy-done.1, bf16[16,4,1,4,3584]{4,1,3,2,0:T(4,128)(2,1)S(1)} %copy.62), kind=kLoop, calls=%fused_computation.15 | loop fusion | flops 1835008 | bytes 7340032 | tf_op jit(solution)/shard_map/stack | solution.py:85
  143.9 2.0 convolution_convert_fusion.1
  146.7 1.7 pad_maximum_fusion.1
  148.5 4.5 %copy.70 = bf16[3584,384]{1,0:T(8,128)(2,1)} copy(bf16[3584,384]{0,1:T(8,128)(2,1)} %pad_maximum_fusion.1) | data formatting | bytes 5505024
  153.0 1.3 dynamic-slice
  154.2 116.1 %all-reduce.3.cloned.1.call-done = bf16[16,4,2,4,3584]{4,1,3,2,0:T(4,128)(2,1)} async-done(((bf16[16,4,2,4,3584]{4,1,3,2,0:T(4,128)(2,1)}), bf16[16,4,2,4,3584]{4,1,3,2,0:T(4,128)(2,1)}) %all-reduce.3.cloned.1.call-update) | async-done | bytes 3670032
  270.4 1.7 dynamic-slice_bitcast_fusion
  272.2 9.1 %all_to_all.11 = bf16[4,2,4,3584]{3,2,1,0:T(4,128)(2,1)S(1)} all-to-all(bf16[4,2,4,3584]{3,2,1,0:T(4,128)(2,1)S(1)} %copy.64), channel_id=1, replica_groups=mesh['dp'=8,'ex'=4,'eh'=16] {'ex'}, dimensions={0} | all-to-all | bytes 458752 | tf_op jit(solution)/shard_map/all_to_all | solution.py:93
  281.4 1.9 fusion.2
  283.3 1.9 fusion.1
  285.2 31.3 %reduce-scatter.4.cloned.1.call-done = bf16[448,384]{1,0:T(8,128)(2,1)} async-done(((bf16[3584,384]{1,0:T(8,128)(2,1)}), bf16[448,384]{1,0:T(8,128)(2,1)}) %reduce-scatter.4.cloned.1.call-update) | async-done | bytes 344080
  316.5 1.1 copy.71
  317.8 0.8 copy.67
  318.6 0.8 copy.68
  319.4 0.8 copy.69
  (42 shorter events, 4.8 us)
Async XLA Ops:
  7.2 2.1 copy-start
  7.2 63.9 %all-gather.5.cloned.1.call-start = ((), (), s32[]{:S(2)}) async-start(), calls=%async_computation.3 | async-start | bytes 3899392 | tf_op jit(solution)/shard_map/all_gather | solution.py:75
  9.3 12.1 %copy-start.4 = (bf16[1,448,128]{2,1,0:T(8,128)(2,1)S(1)}, bf16[1,448,128]{2,1,0:T(8,128)(2,1)}, u32[]{:S(2)}) copy-start(bf16[1,448,128]{2,1,0:T(8,128)(2,1)} %param.13) | copy-start | bytes 344068
  9.3 12.1 %copy-start.5 = (bf16[1,448,128]{2,1,0:T(8,128)(2,1)S(1)}, bf16[1,448,128]{2,1,0:T(8,128)(2,1)}, u32[]{:S(2)}) copy-start(bf16[1,448,128]{2,1,0:T(8,128)(2,1)} %param.12) | copy-start | bytes 344068
  9.3 12.1 %copy-start.6 = (bf16[1,448,128]{2,1,0:T(8,128)(2,1)S(1)}, bf16[1,448,128]{2,1,0:T(8,128)(2,1)}, u32[]{:S(2)}) copy-start(bf16[1,448,128]{2,1,0:T(8,128)(2,1)} %param.11) | copy-start | bytes 344068
  21.4 93.4 %all-gather.7.cloned.1.call-start = ((), (), s32[]{:S(2)}) async-start(), calls=%async_computation.4 | async-start | bytes 3096576 | tf_op jit(solution)/shard_map/all_gather | solution.py:72
  22.2 248.2 %all-reduce.3.cloned.1.call-start = ((), (), s32[]{:S(2)}) async-start(), calls=%async_computation.6 | async-start | bytes 7340032
  114.7 1.9 copy-start.2
  116.7 2.1 copy-start.3
  136.7 2.5 copy-start.1
  143.6 172.8 %reduce-scatter.4.cloned.1.call-start = ((), (), s32[]{:S(2)}) async-start(), calls=%async_computation.5 | async-start | bytes 3096576
Sparse Core Ops, SparseCore 0:
  21.5 49.5 all-gather.4
  73.8 40.9 all-gather.6
  143.7 126.5 all-reduce.2
  273.1 43.3 reduce-scatter.3

commit v2 on v0

--- a/solution.py
+++ b/solution.py
@@ -65,11 +65,11 @@
     picked = jnp.einsum("tec,tsf->escf", select_b, cot3, preferred_element_type=jnp.float32)
     slot_cot = (picked * slot_gate[:, None, :, None]).astype(jnp.bfloat16)
     payload = jnp.stack([slot_tokens, slot_cot], axis=2)
-    gate_full, up_full, down_full = (
-        lax.all_gather(w_gate, "dp", axis=1, tiled=True),
-        lax.all_gather(w_up, "dp", axis=1, tiled=True),
-        lax.all_gather(w_down, "dp", axis=1, tiled=True),
-    )
+    w_loc = jnp.concatenate([w_gate[0], w_up[0], w_down[0]], axis=1)
+    w_all = lax.all_gather(w_loc, "dp", axis=0, tiled=False).reshape(-1, 3 * hid)
+    gate_full = w_all[None, :, :hid]
+    up_full = w_all[None, :, hid : 2 * hid]
+    down_full = w_all[None, :, 2 * hid :]
     outgoing = jnp.broadcast_to(payload, (window, SPLIT, 2, CAP, width)).reshape(
         groups, 2, CAP, width
     )

time: 264 us -> 256 us (0.970)
  blocking collectives: 74.3 us -> 0 us
  waiting for transfers between devices: 82.4 us -> 156 us
  starting transfers between devices: 28.4 us -> 21.5 us
    all_gather x3 -> x0, blocking collectives: 74.3 us -> none  [the longest x1 26 us: per_device(): lax.all_gather(w_gate, 'dp', axis=1, tiled=True)]
    all_to_all x1, waiting for transfers between devices: 10.4 us -> 83.6 us  [per_device(): lax.all_to_all(outgoing, 'expert', split_axis=0, concat_axis=0, tiled=True)]
    all_to_all x1, starting transfers between devices: 13 us -> 5.91 us  [per_device(): lax.all_to_all(results[0].astype(jnp.bfloat16), 'expert', split_axis=0, c...]
    unnamed x2 -> x3, waiting for transfers between devices: 42.9 us -> 44.7 us
    unnamed x23 -> x19, local copies, waits for them, and re-layouts: 10.3 us -> 8.7 us
  transfers between devices with their start and end apart: 3 -> 4, of which waited for: 3 -> 3; matrix products, arithmetic and copies ran while one was open for 4% -> 9% of each run, Pallas kernels for 0% -> 0%
where the time goes in v2:
time: 256 us; the launch traced here: 255 us
  waiting for transfers between devices  156 us (61%)
  local copies, waits for them, and re-layouts  32.3 us (13%)
  starting transfers between devices  21.5 us (8%)
  matrix products  16.8 us (7%)
  other arithmetic  14.5 us (6%)
  between operations  14.2 us (6%)
    all_to_all x1, waiting for transfers between devices, per_device(): lax.all_to_all(outgoing, 'expert', split_axis=0, concat_axis=0, tiled=True)  83.6 us
    unnamed x3, waiting for transfers between devices  44.7 us
    all_to_all x1, waiting for transfers between devices, per_device(): lax.all_to_all(results[0].astype(jnp.bfloat16), 'expert', split_axis=0, c...  27.8 us
    all_to_all x1, starting transfers between devices, per_device(): lax.all_to_all(outgoing, 'expert', split_axis=0, concat_axis=0, tiled=True)  15.1 us
    unnamed x19, local copies, waits for them, and re-layouts  8.7 us
    another operation x2, local copies, waits for them, and re-layouts, per_device(): jnp.stack([partial_out.reshape(parts, groups, CAP, feat), partial_grad.re...  8.15 us
    another operation x2, local copies, waits for them, and re-layouts  6.85 us
    convert_element_type x1, other arithmetic, per_device(): results[0].astype(jnp.bfloat16)  6.26 us
  transfers between devices with their start and end apart: 4, of which 3 were waited for; matrix products, arithmetic and copies ran while one was open for 9% of the time, Pallas kernels for 0%

profile of v2, /device:TPU:1, one launch (start us, length us, event | category | flops | bytes accessed | tf_op | source)
XLA Modules:
  0.0 255.5 jit_solution(6141263027511738063)
XLA Ops:
  7.2 0.8 fusion.25
  8.3 0.7 select_reduce_fusion
  9.5 1.4 fusion.11
  11.2 2.9 %broadcast_in_dim.57 = bf16[4,16,2,4,3584]{4,3,2,1,0:T(4,128)(2,1)} broadcast(bf16[4,2,4,3584]{3,2,1,0:T(4,128)(2,1)S(1)} %copy.43), dimensions={0,2,3,4} | broadcast | bytes 3899392 | tf_op jit(solution)/shard_map/broadcast_in_dim | solution.py:73
  14.1 15.1 %all-to-all-start = ((bf16[64,2,4,3584]{3,2,1,0:T(4,128)(2,1)}), bf16[64,2,4,3584]{3,2,1,0:T(4,128)(2,1)}, u32[]{:S(2)}, u32[]{:S(2)}) async-start(bf16[64,2,4,3584]{3,2,1,0:T(4,128)(2,1)} %bitcast.93), calls=%async_computation | async-start | bytes 7340032 | tf_op jit(solution)/shard_map/all_to_all | solution.py:76
  29.5 0.8 pad_maximum_fusion
  30.3 83.6 %all-to-all-done = bf16[64,2,4,3584]{3,2,1,0:T(4,128)(2,1)} async-done(((bf16[64,2,4,3584]{3,2,1,0:T(4,128)(2,1)}), bf16[64,2,4,3584]{3,2,1,0:T(4,128)(2,1)}, u32[]{:S(2)}, u32[]{:S(2)}) %all-to-all-start) | async-done | bytes 3670048 | tf_op jit(solution)/shard_map/all_to_all | solution.py:76
  113.9 5.1 %fusion.42 = (bf16[1,64,1,4,3584]{4,3,2,1,0:T(4,128)(2,1)}, bf16[1,64,1,4,3584]{4,3,2,1,0:T(4,128)(2,1)}) fusion(bf16[1,64,2,4,3584]{4,3,2,1,0:T(4,128)(2,1)} %bitcast.15), kind=kLoop, calls=%fused_computation.72 | loop fusion | bytes 7340032 | tf_op jit(solution)/shard_map/slice | solution.py:79
  119.1 2.9 %reshape.119 = bf16[256,3584]{1,0:T(8,128)(2,1)S(1)} reshape(bf16[1,64,1,4,3584]{4,3,2,1,0:T(4,128)(2,1)} %get-tuple-element.21) | data formatting | bytes 3670016 | tf_op jit(solution)/shard_map/reshape.5
  122.0 3.9 %reshape.120 = bf16[256,3584]{1,0:T(8,128)(2,1)} reshape(bf16[1,64,1,4,3584]{4,3,2,1,0:T(4,128)(2,1)} %get-tuple-element.20) | data formatting | bytes 3670016 | tf_op jit(solution)/shard_map/reshape.26
  126.0 2.0 fusion.19
  127.9 1.8 fusion.21
  129.7 0.6 multiply_convert_fusion.2
  130.4 0.6 fusion.17
  131.0 1.9 fusion.2
  132.9 4.1 %stack_reshape.9 = bf16[1,64,1,4,3584]{4,3,1,2,0:T(4,128)(2,1)} reshape(bf16[1,256,3584]{2,1,0:T(8,128)(2,1)} %fusion.2) | data formatting | bytes 3670016 | tf_op jit(solution)/shard_map/stack;reshape | solution.py:87
  137.0 3.1 %fusion.1 = bf16[1,256,3584]{2,1,0:T(8,128)(2,1)} fusion(bf16[256,128]{1,0:T(8,128)(2,1)S(1)} %get-tuple-element.25, bf16[3584,384]{1,0:T(8,128)(2,1)} %all-gather.3.cloned.1.call-done), kind=kOutput, calls=%fused_computation.3 | convolution fusion | flops 235798528 | bytes 2818048 | tf_op jit(solution)/shard_map/rh,pfh->prf/dot_general | solution.py:33
  140.1 4.1 %stack_reshape.8 = bf16[1,64,1,4,3584]{4,3,1,2,0:T(4,128)(2,1)} reshape(bf16[1,256,3584]{2,1,0:T(8,128)(2,1)} %fusion.1) | data formatting | bytes 3670016 | tf_op jit(solution)/shard_map/stack;reshape | solution.py:87
  144.2 6.3 %maximum_bitcast_fusion = bf16[64,2,4,3584]{3,2,1,0:T(4,128)(2,1)} fusion(bf16[1,64,1,4,3584]{4,3,2,1,0:T(4,128)(2,1)} %bitcast.94, bf16[1,64,1,4,3584]{4,3,2,1,0:T(4,128)(2,1)} %bitcast.95), kind=kLoop, calls=%fused_computation.21 | loop fusion | flops 1835008 | bytes 7340032 | tf_op jit(solution)/shard_map/convert_element_type | solution.py:95
  150.4 5.9 %all-to-all-start.1 = ((bf16[64,2,4,3584]{3,2,1,0:T(4,128)(2,1)}), bf16[64,2,4,3584]{3,2,1,0:T(4,128)(2,1)}, u32[]{:S(2)}, u32[]{:S(2)}) async-start(bf16[64,2,4,3584]{3,2,1,0:T(4,128)(2,1)} %maximum_bitcast_fusion), calls=%async_computation.1 | async-start | bytes 7340032 | tf_op jit(solution)/shard_map/all_to_all | solution.py:94
  157.5 0.6 copy-done.2
  158.6 1.7 maximum_bitcast_fusion.1
  160.3 4.5 %copy.51 = bf16[3584,384]{1,0:T(8,128)(2,1)} copy(bf16[3584,384]{0,1:T(8,128)(2,1)} %maximum_bitcast_fusion.1) | data formatting | bytes 5505024
  164.8 44.6 %reduce-scatter.4.cloned.1.call-done = bf16[448,384]{1,0:T(8,128)(2,1)} async-done(((bf16[3584,384]{1,0:T(8,128)(2,1)}), bf16[448,384]{1,0:T(8,128)(2,1)}) %reduce-scatter.4.cloned.1.call-update) | async-done | bytes 344080
  209.4 1.1 copy.52
  210.7 0.8 copy.48
  211.6 0.8 copy.49
  212.4 0.8 copy.50
  213.2 27.8 %all-to-all-done.1 = bf16[64,2,4,3584]{3,2,1,0:T(4,128)(2,1)} async-done(((bf16[64,2,4,3584]{3,2,1,0:T(4,128)(2,1)}), bf16[64,2,4,3584]{3,2,1,0:T(4,128)(2,1)}, u32[]{:S(2)}, u32[]{:S(2)}) %all-to-all-start.1) | async-done | bytes 3670048 | tf_op jit(solution)/shard_map/all_to_all | solution.py:94
  241.0 3.6 %bitcast_reduce_fusion = bf16[4,2,4,3584]{3,2,1,0:T(4,128)(2,1)S(1)} fusion(bf16[64,2,4,3584]{3,2,1,0:T(4,128)(2,1)} %all-to-all-done.1), kind=kLoop, calls=%fused_computation.22 | loop fusion | flops 1720320 | bytes 3899392 | tf_op jit(solution)/shard_map/reduce_sum | solution.py:97
  244.8 1.9 fusion.4
  246.7 1.9 fusion.3
  (35 shorter events, 3.2 us)
Async XLA Ops:
  7.2 2.1 copy-start
  14.1 15.4 %copy-start.4 = (bf16[1,448,128]{2,1,0:T(8,128)(2,1)S(1)}, bf16[1,448,128]{2,1,0:T(8,128)(2,1)}, u32[]{:S(2)}) copy-start(bf16[1,448,128]{2,1,0:T(8,128)(2,1)} %param.13) | copy-start | bytes 344068
  14.1 15.4 %copy-start.5 = (bf16[1,448,128]{2,1,0:T(8,128)(2,1)S(1)}, bf16[1,448,128]{2,1,0:T(8,128)(2,1)}, u32[]{:S(2)}) copy-start(bf16[1,448,128]{2,1,0:T(8,128)(2,1)} %param.12) | copy-start | bytes 344068
  14.1 15.4 %copy-start.6 = (bf16[1,448,128]{2,1,0:T(8,128)(2,1)S(1)}, bf16[1,448,128]{2,1,0:T(8,128)(2,1)}, u32[]{:S(2)}) copy-start(bf16[1,448,128]{2,1,0:T(8,128)(2,1)} %param.11) | copy-start | bytes 344068
  14.1 99.8 %all-to-all-start = ((bf16[64,2,4,3584]{3,2,1,0:T(4,128)(2,1)}), bf16[64,2,4,3584]{3,2,1,0:T(4,128)(2,1)}, u32[]{:S(2)}, u32[]{:S(2)}) async-start(bf16[64,2,4,3584]{3,2,1,0:T(4,128)(2,1)} %bitcast.93), calls=%async_computation | async-start | bytes 7340032 | tf_op jit(solution)/shard_map/all_to_all | solution.py:76
  29.3 96.7 %all-gather.3.cloned.1.call-start = ((), (), s32[]{:S(2)}) async-start(), calls=%async_computation.3 | async-start | bytes 3096576 | tf_op jit(solution)/shard_map/all_gather | solution.py:69
  125.9 2.0 copy-start.1
  125.9 3.8 %copy-start.3 = (bf16[3584,384]{1,0:T(8,128)(2,1)S(1)}, bf16[3584,384]{1,0:T(8,128)(2,1)}, u32[]{:S(2)}) copy-start(bf16[3584,384]{1,0:T(8,128)(2,1)} %all-gather.3.cloned.1.call-done) | copy-start | bytes 8257540
  150.4 90.6 %all-to-all-start.1 = ((bf16[64,2,4,3584]{3,2,1,0:T(4,128)(2,1)}), bf16[64,2,4,3584]{3,2,1,0:T(4,128)(2,1)}, u32[]{:S(2)}, u32[]{:S(2)}) async-start(bf16[64,2,4,3584]{3,2,1,0:T(4,128)(2,1)} %maximum_bitcast_fusion), calls=%async_computation.1 | async-start | bytes 7340032 | tf_op jit(solution)/shard_map/all_to_all | solution.py:94
  156.3 53.1 %reduce-scatter.4.cloned.1.call-start = ((), (), s32[]{:S(2)}) async-start(), calls=%async_computation.4 | async-start | bytes 3096576
  156.6 1.5 copy-start.2
Sparse Core Ops, SparseCore 0:
  32.8 44.1 all-gather.2
  164.9 44.4 reduce-scatter.3

commit v3 on v1

--- a/solution.py
+++ b/solution.py
@@ -10,7 +10,7 @@
 
 SCALE = 2.0 ** (-16)
 HIGH = lax.Precision.HIGHEST
-TOK = ("dp", "ex", "eh")
+TOK = ("dp", "ex", "ez", "ec")
 
 
 def routing(ids, gates, window, capacity):
@@ -58,7 +58,7 @@
 def per_device(tokens, out_cotangent, expert_ids, gate_fixed, w_gate, w_up, w_down):
     tok_rows, width = tokens.shape
     window = lax.axis_size("ex")
-    hsplit = lax.axis_size("eh")
+    hsplit = lax.axis_size("ez") * lax.axis_size("ec")
     hid = w_gate.shape[2]
     select, slot_gate = routing(expert_ids, gate_fixed, window, CAP)
     select_b = select.astype(jnp.bfloat16)
@@ -72,7 +72,7 @@
     w_all = lax.all_gather(w_loc, "dp", axis=0, tiled=False)
     w_all = w_all.reshape(-1, 3 * hid)
     by_x = lax.all_to_all(payload, "ex", split_axis=0, concat_axis=0, tiled=True)
-    arrived = lax.all_gather(by_x, "eh", axis=0, tiled=False)
+    arrived = lax.all_gather(by_x, ("ez", "ec"), axis=0, tiled=False)
     inputs = arrived[:, :, 0].reshape(hsplit * window * CAP, width)
     cotangents = arrived[:, :, 1].reshape(hsplit * window * CAP, width)
     partial_out, partial_grad, term = expert_math(inputs, cotangents, w_all, hid)
@@ -89,8 +89,11 @@
         ],
         axis=2,
     ).astype(jnp.bfloat16)
-    reduced = lax.psum_scatter(results, "eh", scatter_dimension=0, tiled=True)
-    combined = lax.all_to_all(reduced[0], "ex", split_axis=0, concat_axis=0, tiled=True)
+    r2 = results.reshape(-1, 2, window * 2 * CAP * width)
+    half = lax.psum_scatter(r2, "ec", scatter_dimension=1, tiled=True)
+    reduced = lax.psum_scatter(half.reshape(-1, 256), "ez", scatter_dimension=0, tiled=True)
+    reduced = reduced.reshape(window, 2, CAP, width)
+    combined = lax.all_to_all(reduced, "ex", split_axis=0, concat_axis=0, tiled=True)
     combined = combined.astype(jnp.float32)
     weighted = select * slot_gate[None, :, :]
     layer_out = jnp.einsum("tec,ecf->tf", weighted, combined[:, 0], precision=HIGH)
@@ -107,10 +110,10 @@
 def solution(mesh):
     n_dp = mesh.shape["dp"]
     n_exp = mesh.shape["expert"]
-    devices = mesh.devices.reshape(n_dp, n_exp // SPLIT, SPLIT)
-    grid = Mesh(devices, ("dp", "ex", "eh"))
+    devices = mesh.devices.reshape(n_dp, n_exp // SPLIT, SPLIT // 2, 2)
+    grid = Mesh(devices, ("dp", "ex", "ez", "ec"))
     tok = P(TOK, None)
-    wsp = P(("ex", "eh"), "dp", None)
+    wsp = P(("ex", "ez", "ec"), "dp", None)
     return jax.shard_map(
         per_device,
         mesh=grid,

time: 330 us -> 295 us (0.89)
  waiting for transfers between devices: 228 us -> 184 us
  blocking collectives: 19.2 us -> 10.1 us
  local copies, waits for them, and re-layouts: 38.4 us -> 47.3 us
  starting transfers between devices: 0.35 us -> 4.32 us
    unnamed x6, waiting for transfers between devices: 147 us -> 43 us
    reduce_scatter x0 -> x2, waiting for transfers between devices: none -> 58.5 us  [the longest x1 45.9 us: per_device(): lax.psum_scatter(half.reshape(-1, 256), 'ez', scatter_dimension=0, tiled=...]
    convert_element_type x0 -> x2, local copies, waits for them, and re-layouts: none -> 12.7 us  [per_device(): results = jnp.stack([partial_out.reshape(hsplit, window, CAP, width), par...]
    all_to_all x1 -> x0, blocking collectives: 9.12 us -> none  [per_device(): lax.all_to_all(reduced[0], 'ex', split_axis=0, concat_axis=0, tiled=True)]
    another operation x4 -> x2, local copies, waits for them, and re-layouts: 14.3 us -> 8.16 us  [per_device(): jnp.stack([partial_out.reshape(hsplit, window, CAP, width), partial_grad....]
    reshape x0 -> x2, local copies, waits for them, and re-layouts: none -> 5.31 us  [the longest x1 3.59 us: per_device(): half.reshape(-1, 256)]
    all_to_all x0 -> x1, starting transfers between devices: none -> 3.93 us  [per_device(): lax.all_to_all(reduced, 'ex', split_axis=0, concat_axis=0, tiled=True)]
    unnamed x20 -> x17, local copies, waits for them, and re-layouts: 9.49 us -> 8.22 us
  transfers between devices with their start and end apart: 4 -> 6, of which waited for: 4 -> 6; matrix products, arithmetic and copies ran while one was open for 9% -> 10% of each run, Pallas kernels for 0% -> 0%
where the time goes in v3:
time: 295 us; the launch traced here: 289 us
  waiting for transfers between devices  184 us (62%)
  local copies, waits for them, and re-layouts  47.3 us (16%)
  matrix products  18.4 us (6%)
  between operations  13.9 us (5%)
  other arithmetic  10.8 us (4%)
  blocking collectives  10.1 us (3%)
  starting transfers between devices  4.32 us (1%)
    all_gather x1, waiting for transfers between devices, per_device(): arrived = lax.all_gather(by_x, ('ez', 'ec'), axis=0, tiled=False)  48.8 us
    reduce_scatter x1, waiting for transfers between devices, per_device(): lax.psum_scatter(half.reshape(-1, 256), 'ez', scatter_dimension=0, tiled=...  45.9 us
    unnamed x6, waiting for transfers between devices  43 us
    all_gather x1, waiting for transfers between devices, per_device(): w_all = lax.all_gather(w_loc, 'dp', axis=0, tiled=False)  31.2 us
    convert_element_type x2, local copies, waits for them, and re-layouts, per_device(): results = jnp.stack([partial_out.reshape(hsplit, window, CAP, width), par...  12.7 us
    reduce_scatter x1, waiting for transfers between devices, per_device(): half = lax.psum_scatter(r2, 'ec', scatter_dimension=1, tiled=True)  12.5 us
    all_to_all x1, blocking collectives, per_device(): lax.all_to_all(payload, 'ex', split_axis=0, concat_axis=0, tiled=True)  10.1 us
    unnamed x17, local copies, waits for them, and re-layouts  8.22 us
  transfers between devices with their start and end apart: 6, of which 6 were waited for; matrix products, arithmetic and copies ran while one was open for 10% of the time, Pallas kernels for 0%

profile of v3, /device:TPU:1, one launch (start us, length us, event | category | flops | bytes accessed | tf_op | source)
XLA Modules:
  0.0 289.2 jit_solution(2326334516755320837)
XLA Ops:
  9.5 1.4 fusion.5
  11.2 10.1 %all_to_all.10 = bf16[4,2,4,3584]{3,2,1,0:T(4,128)(2,1)} all-to-all(bf16[4,2,4,3584]{3,2,1,0:T(4,128)(2,1)S(1)} %copy.72), channel_id=1, replica_groups=mesh['dp'=8,'ex'=4,'ez'=8,'ec'=2] {'ex'}, dimensions={0} | all-to-all | bytes 458752 | tf_op jit(solution)/shard_map/all_to_all | solution.py:74
  22.3 48.8 %all-gather.5.cloned.1.call-done = bf16[64,2,4,3584]{3,2,1,0:T(4,128)(2,1)} async-done(((bf16[4,2,4,3584]{3,2,1,0:T(4,128)(2,1)}), bf16[64,2,4,3584]{3,2,1,0:T(4,128)(2,1)}) %all-gather.5.cloned.1.call-update) | async-done | bytes 3670032 | tf_op jit(solution)/shard_map/all_gather | solution.py:75
  71.1 5.5 %fusion.36 = (bf16[16,4,1,4,3584]{4,3,2,1,0:T(4,128)(2,1)}, bf16[16,4,1,4,3584]{4,3,2,1,0:T(4,128)(2,1)}) fusion(bf16[16,4,2,4,3584]{4,3,2,1,0:T(4,128)(2,1)} %bitcast.53), kind=kLoop, calls=%fused_computation.64 | loop fusion | bytes 7340032 | tf_op jit(solution)/shard_map/slice | solution.py:77
  76.6 2.9 %reshape_squeeze.6 = bf16[256,3584]{1,0:T(8,128)(2,1)S(1)} reshape(bf16[16,4,1,4,3584]{4,3,2,1,0:T(4,128)(2,1)} %get-tuple-element.31) | data formatting | bytes 3670016 | tf_op jit(solution)/shard_map/reshape;squeeze | solution.py:76
  79.5 4.0 %reshape_squeeze.7 = bf16[256,3584]{1,0:T(8,128)(2,1)} reshape(bf16[16,4,1,4,3584]{4,3,2,1,0:T(4,128)(2,1)} %get-tuple-element.30) | data formatting | bytes 3670016 | tf_op jit(solution)/shard_map/reshape;squeeze | solution.py:77
  83.5 31.2 %all-gather.7.cloned.1.call-done = bf16[3584,384]{1,0:T(8,128)(2,1)} async-done(((bf16[448,384]{1,0:T(8,128)(2,1)}), bf16[3584,384]{1,0:T(8,128)(2,1)}) %all-gather.7.cloned.1.call-update) | async-done | bytes 2752528 | tf_op jit(solution)/shard_map/all_gather | solution.py:72
  114.7 1.9 fusion.16
  116.7 2.0 fusion.8
  120.0 1.9 fusion
  121.9 4.1 %stack_reshape.9 = bf16[16,4,1,4,3584]{4,3,1,0,2:T(4,128)(2,1)} reshape(bf16[256,3584]{1,0:T(8,128)(2,1)} %fusion) | data formatting | bytes 3670016 | tf_op jit(solution)/shard_map/stack;reshape | solution.py:85
  126.0 3.1 %convolution_convert_fusion = bf16[256,3584]{1,0:T(8,128)(2,1)} fusion(bf16[256,128]{1,0:T(8,128)(2,1)S(1)} %get-tuple-element.35, bf16[3584,384]{1,0:T(8,128)(2,1)} %all-gather.7.cloned.1.call-done), kind=kOutput, calls=%fused_computation.2 | convolution fusion | flops 235798528 | bytes 2818048 | tf_op jit(solution)/shard_map/dot_general | solution.py:39
  129.1 4.1 %stack_reshape.8 = bf16[16,4,1,4,3584]{4,3,1,0,2:T(4,128)(2,1)} reshape(bf16[256,3584]{1,0:T(8,128)(2,1)} %convolution_convert_fusion) | data formatting | bytes 3670016 | tf_op jit(solution)/shard_map/stack;reshape | solution.py:85
  133.1 6.3 %pad_maximum_fusion = bf16[16,4,2,4,3584]{4,3,2,1,0:T(4,128)(2,1)} fusion(bf16[16,4,1,4,3584]{4,3,2,1,0:T(4,128)(2,1)} %bitcast.51, bf16[16,4,1,4,3584]{4,3,2,1,0:T(4,128)(2,1)} %bitcast.52), kind=kLoop, calls=%fused_computation.15 | loop fusion | flops 1835008 | bytes 7340032 | tf_op jit(solution)/shard_map/stack | solution.py:85
  139.4 6.9 %convert_element_type.56 = bf16[8,2,114688]{2,1,0:T(2,128)(2,1)} reshape(bf16[16,4,2,4,3584]{4,3,2,1,0:T(4,128)(2,1)} %pad_maximum_fusion) | data formatting | bytes 7340032 | tf_op jit(solution)/shard_map/convert_element_type | solution.py:91
  146.3 5.8 %copy.75 = bf16[8,2,114688]{2,0,1:T(8,128)(2,1)} copy(bf16[8,2,114688]{2,1,0:T(2,128)(2,1)} %convert_element_type.56) | data formatting | bytes 7340032 | tf_op jit(solution)/shard_map/convert_element_type | solution.py:91
  152.4 2.0 convolution_convert_fusion.1
  155.2 1.8 pad_maximum_fusion.1
  157.0 4.5 %copy.81 = bf16[3584,384]{1,0:T(8,128)(2,1)} copy(bf16[3584,384]{0,1:T(8,128)(2,1)} %pad_maximum_fusion.1) | data formatting | bytes 5505024
  161.6 12.5 %reduce-scatter.6.cloned.1.call-done = bf16[8,1,114688]{2,0,1:T(8,128)(2,1)} async-done(((bf16[8,2,114688]{2,0,1:T(8,128)(2,1)}), bf16[8,1,114688]{2,0,1:T(8,128)(2,1)}) %reduce-scatter.6.cloned.1.call-update) | async-done | bytes 1835024 | tf_op jit(solution)/shard_map/reduce_scatter | solution.py:93
  174.1 3.6 %reshape.41 = bf16[3584,256]{1,0:T(8,128)(2,1)} reshape(bf16[8,1,114688]{2,0,1:T(8,128)(2,1)} %reduce-scatter.6.cloned.1.call-done) | data formatting | bytes 3670016 | tf_op jit(solution)/shard_map/reshape | solution.py:94
  177.7 42.9 %reduce-scatter.10.cloned.1.call-done = bf16[448,384]{1,0:T(8,128)(2,1)} async-done(((bf16[3584,384]{1,0:T(8,128)(2,1)}), bf16[448,384]{1,0:T(8,128)(2,1)}) %reduce-scatter.10.cloned.1.call-update) | async-done | bytes 344080
  220.6 1.1 copy.82
  221.8 45.9 %reduce-scatter.8.cloned.1.call-done = bf16[448,256]{1,0:T(8,128)(2,1)} async-done(((bf16[3584,256]{1,0:T(8,128)(2,1)}), bf16[448,256]{1,0:T(8,128)(2,1)}) %reduce-scatter.8.cloned.1.call-update) | async-done | bytes 229392 | tf_op jit(solution)/shard_map/reduce_scatter | solution.py:94
  267.8 1.7 reshape.42
  269.5 3.9 %all-to-all-start.1 = ((bf16[4,2,4,3584]{3,2,1,0:T(4,128)(2,1)}), bf16[4,2,4,3584]{3,2,1,0:T(4,128)(2,1)S(1)}, u32[]{:S(2)}, u32[]{:S(2)}) async-start(bf16[4,2,4,3584]{3,2,1,0:T(4,128)(2,1)} %reshape.42), calls=%async_computation.3 | async-start | bytes 458752 | tf_op jit(solution)/shard_map/all_to_all | solution.py:96
  273.5 0.8 copy.78
  274.3 0.8 copy.79
  275.1 0.8 copy.80
  275.9 2.8 all-to-all-done.1
  278.8 1.9 fusion.2
  280.7 1.9 fusion.1
  (43 shorter events, 6.3 us)
Async XLA Ops:
  7.2 2.1 copy-start
  7.2 63.9 %all-gather.5.cloned.1.call-start = ((), (), s32[]{:S(2)}) async-start(), calls=%async_computation.7 | async-start | bytes 3899392 | tf_op jit(solution)/shard_map/all_gather | solution.py:75
  9.3 12.1 %copy-start.3 = (bf16[1,448,128]{2,1,0:T(8,128)(2,1)S(1)}, bf16[1,448,128]{2,1,0:T(8,128)(2,1)}, u32[]{:S(2)}) copy-start(bf16[1,448,128]{2,1,0:T(8,128)(2,1)} %param.13) | copy-start | bytes 344068
  9.3 12.1 %copy-start.4 = (bf16[1,448,128]{2,1,0:T(8,128)(2,1)S(1)}, bf16[1,448,128]{2,1,0:T(8,128)(2,1)}, u32[]{:S(2)}) copy-start(bf16[1,448,128]{2,1,0:T(8,128)(2,1)} %param.12) | copy-start | bytes 344068
  9.3 12.1 %copy-start.5 = (bf16[1,448,128]{2,1,0:T(8,128)(2,1)S(1)}, bf16[1,448,128]{2,1,0:T(8,128)(2,1)}, u32[]{:S(2)}) copy-start(bf16[1,448,128]{2,1,0:T(8,128)(2,1)} %param.11) | copy-start | bytes 344068
  21.4 93.4 %all-gather.7.cloned.1.call-start = ((), (), s32[]{:S(2)}) async-start(), calls=%async_computation.8 | async-start | bytes 3096576 | tf_op jit(solution)/shard_map/all_gather | solution.py:72
  22.2 151.9 %reduce-scatter.6.cloned.1.call-start = ((), (), s32[]{:S(2)}) async-start(), calls=%async_computation.5 | async-start | bytes 5505024 | tf_op jit(solution)/shard_map/reduce_scatter | solution.py:93
  114.7 1.9 copy-start.1
  116.7 2.1 copy-start.2
  152.1 68.5 %reduce-scatter.10.cloned.1.call-start = ((), (), s32[]{:S(2)}) async-start(), calls=%async_computation.9 | async-start | bytes 3096576
  161.5 106.2 %reduce-scatter.8.cloned.1.call-start = ((), (), s32[]{:S(2)}) async-start(), calls=%async_computation.6 | async-start | bytes 2064384 | tf_op jit(solution)/shard_map/reduce_scatter | solution.py:94
  269.5 9.3 %all-to-all-start.1 = ((bf16[4,2,4,3584]{3,2,1,0:T(4,128)(2,1)}), bf16[4,2,4,3584]{3,2,1,0:T(4,128)(2,1)S(1)}, u32[]{:S(2)}, u32[]{:S(2)}) async-start(bf16[4,2,4,3584]{3,2,1,0:T(4,128)(2,1)} %reshape.42), calls=%async_computation.3 | async-start | bytes 458752 | tf_op jit(solution)/shard_map/all_to_all | solution.py:96
Sparse Core Ops, SparseCore 0:
  21.5 49.5 all-gather.4
  73.8 40.9 all-gather.6
  152.3 21.8 reduce-scatter.5
  177.1 43.4 reduce-scatter.9
  223.3 44.4 reduce-scatter.7

commit v4 on v3

--- a/solution.py
+++ b/solution.py
@@ -24,6 +24,51 @@
     select = jnp.where(pick, 1.0, 0.0).astype(jnp.float32)
     slot_gate = jnp.sum(select * weight[:, :, None], axis=0)
     return (select, slot_gate)
+
+
+def _shift(n, k):
+    return [(i, (i + k) % n) for i in range(n)]
+
+
+def ring_gather(piece, axis):
+    n = lax.axis_size(axis)
+    me = lax.axis_index(axis)
+    fw = piece
+    bw = piece
+    ahead = []
+    behind = []
+    for step in range(n // 2):
+        fw = lax.ppermute(fw, axis, _shift(n, 1))
+        ahead.append(fw)
+        if step < (n - 1) // 2:
+            bw = lax.ppermute(bw, axis, _shift(n, -1))
+            behind.append(bw)
+    rot = jnp.stack([piece] + ahead + behind[::-1], axis=0)
+    rev = rot[::-1]
+    doubled = jnp.concatenate([rev, rev], axis=0)
+    return lax.dynamic_slice_in_dim(doubled, (n - 1 - me) % n, n, axis=0)
+
+
+def ring_reduce_scatter(full, axis):
+    n = lax.axis_size(axis)
+    me = lax.axis_index(axis)
+    rows = full.shape[0] // n
+    cols = full.shape[1] // 2
+    chunks = full.reshape(n, rows, full.shape[1])
+    left = chunks[:, :, :cols]
+    right = chunks[:, :, cols:]
+
+    def pick(part, k):
+        return lax.dynamic_index_in_dim(part, k % n, axis=0, keepdims=False).astype(jnp.float32)
+
+    acc_f = pick(left, me - 1)
+    acc_b = pick(right, me + 1)
+    for step in range(n - 1):
+        got_f = lax.ppermute(acc_f.astype(jnp.bfloat16), axis, _shift(n, 1))
+        got_b = lax.ppermute(acc_b.astype(jnp.bfloat16), axis, _shift(n, -1))
+        acc_f = got_f.astype(jnp.float32) + pick(left, me - 2 - step)
+        acc_b = got_b.astype(jnp.float32) + pick(right, me + 2 + step)
+    return jnp.concatenate([acc_f, acc_b], axis=1)
 
 
 def expert_math(inputs, cotangents, w_all, hid):
@@ -69,16 +114,13 @@
     slot_cot = (picked * slot_gate[:, :, None]).astype(jnp.bfloat16)
     payload = jnp.stack([slot_tokens, slot_cot], axis=1)
     w_loc = jnp.concatenate([w_gate[0], w_up[0], w_down[0]], axis=1)
-    w_all = lax.all_gather(w_loc, "dp", axis=0, tiled=False)
-    w_all = w_all.reshape(-1, 3 * hid)
+    w_all = ring_gather(w_loc, "dp").reshape(-1, 3 * hid)
     by_x = lax.all_to_all(payload, "ex", split_axis=0, concat_axis=0, tiled=True)
     arrived = lax.all_gather(by_x, ("ez", "ec"), axis=0, tiled=False)
     inputs = arrived[:, :, 0].reshape(hsplit * window * CAP, width)
     cotangents = arrived[:, :, 1].reshape(hsplit * window * CAP, width)
     partial_out, partial_grad, term = expert_math(inputs, cotangents, w_all, hid)
-    summed = lax.psum_scatter(
-        term.astype(jnp.bfloat16), "dp", scatter_dimension=0, tiled=True
-    ).astype(jnp.float32)
+    summed = ring_reduce_scatter(term.astype(jnp.bfloat16), "dp")
     grad_gate = summed[:, :hid][None]
     grad_up = summed[:, hid : 2 * hid][None]
     grad_down = summed[:, 2 * hid :][None]

time: 295 us -> 298 us (1.010)
  the two profiles are of different devices: /device:TPU:1 before, /device:TPU:2 now
where the time goes in v4:
time: 298 us; the launch traced here: 296 us
  waiting for transfers between devices  94.6 us (32%)
  starting transfers between devices  80.8 us (27%)
  local copies, waits for them, and re-layouts  53.6 us (18%)
  matrix products  21.2 us (7%)
  other arithmetic  17.4 us (6%)
  between operations  14.5 us (5%)
  blocking collectives  14 us (5%)
    ppermute x7, waiting for transfers between devices, ring_reduce_scatter(): got_f = lax.ppermute(acc_f.astype(jnp.bfloat16), axis, _shift(n, 1))  49.5 us
    ppermute x7, starting transfers between devices, ring_reduce_scatter(): got_b = lax.ppermute(acc_b.astype(jnp.bfloat16), axis, _shift(n, -1))  39.6 us
    ppermute x7, waiting for transfers between devices, ring_reduce_scatter(): got_b = lax.ppermute(acc_b.astype(jnp.bfloat16), axis, _shift(n, -1))  20 us
    ppermute x4, waiting for transfers between devices, ring_gather(): fw = lax.ppermute(fw, axis, _shift(n, 1))  19.2 us
    ppermute x3, starting transfers between devices, ring_gather(): bw = lax.ppermute(bw, axis, _shift(n, -1))  15.7 us
    all_to_all x1, blocking collectives, per_device(): lax.all_to_all(payload, 'ex', split_axis=0, concat_axis=0, tiled=True)  14 us
    ppermute x7, starting transfers between devices, ring_reduce_scatter(): got_f = lax.ppermute(acc_f.astype(jnp.bfloat16), axis, _shift(n, 1))  13.4 us
    convert_element_type x2, local copies, waits for them, and re-layouts, per_device(): results = jnp.stack([partial_out.reshape(hsplit, window, CAP, width), par...  12.7 us
  transfers between devices with their start and end apart: 25, of which 20 were waited for; matrix products, arithmetic and copies ran while one was open for 11% of the time, Pallas kernels for 0%

profile of v4, /device:TPU:2, one launch (start us, length us, event | category | flops | bytes accessed | tf_op | source)
XLA Modules:
  0.0 296.0 jit_solution(4379658094487490686)
XLA Ops:
  11.2 14.0 %all_to_all.10 = bf16[4,2,4,3584]{3,2,1,0:T(4,128)(2,1)} all-to-all(bf16[4,2,4,3584]{3,2,1,0:T(4,128)(2,1)S(1)} %copy.87), channel_id=1, replica_groups=mesh['dp'=8,'ex'=4,'ez'=8,'ec'=2] {'ex'}, dimensions={0} | all-to-all | bytes 458752 | tf_op jit(solution)/shard_map/all_to_all | solution.py:118
  27.3 8.8 %collective-permute-done = bf16[448,384]{1,0:T(8,128)(2,1)S(1)} collective-permute-done((bf16[448,384]{1,0:T(8,128)(2,1)S(1)}, bf16[448,384]{1,0:T(8,128)(2,1)S(1)}, u32[]{:S(2)}, u32[]{:S(2)}) %collective-permute-start) | collective-permute-done | bytes 344096 | tf_op jit(solution)/shard_map/ppermute | solution.py:41
  38.0 5.1 %collective-permute-start.4 = (bf16[448,384]{1,0:T(8,128)(2,1)S(1)}, bf16[448,384]{1,0:T(8,128)(2,1)S(1)}, u32[]{:S(2)}, u32[]{:S(2)}) collective-permute-start(bf16[448,384]{1,0:T(8,128)(2,1)S(1)} %pad_maximum_fusion.1), channel_id=1, source_target_pairs={{0,448},{64,0},{128,64},{192,128},{256,192},{320,256},{384,320},{4... | collective-permute-start | bytes 1032200 | tf_op jit(solution)/shard_map/ppermute | solution.py:44
  43.2 4.7 %collective-permute-done.1 = bf16[448,384]{1,0:T(8,128)(2,1)S(1)} collective-permute-done((bf16[448,384]{1,0:T(8,128)(2,1)S(1)}, bf16[448,384]{1,0:T(8,128)(2,1)S(1)}, u32[]{:S(2)}, u32[]{:S(2)}) %collective-permute-start.1) | collective-permute-done | bytes 344096 | tf_op jit(solution)/shard_map/ppermute | solution.py:41
  50.6 5.1 %collective-permute-start.5 = (bf16[448,384]{1,0:T(8,128)(2,1)S(1)}, bf16[448,384]{1,0:T(8,128)(2,1)S(1)}, u32[]{:S(2)}, u32[]{:S(2)}) collective-permute-start(bf16[448,384]{1,0:T(8,128)(2,1)S(1)} %collective-permute-done.4), channel_id=1, source_target_pairs={{0,448},{64,0},{128,64},{192,128},{256,192},{320,256},{384,320},{4... | collective-permute-start | bytes 1032200 | tf_op jit(solution)/shard_map/ppermute | solution.py:44
  56.5 4.3 %collective-permute-done.2 = bf16[448,384]{1,0:T(8,128)(2,1)S(1)} collective-permute-done((bf16[448,384]{1,0:T(8,128)(2,1)S(1)}, bf16[448,384]{1,0:T(8,128)(2,1)S(1)}, u32[]{:S(2)}, u32[]{:S(2)}) %collective-permute-start.2) | collective-permute-done | bytes 344096 | tf_op jit(solution)/shard_map/ppermute | solution.py:41
  63.5 5.4 %collective-permute-start.6 = (bf16[448,384]{1,0:T(8,128)(2,1)S(1)}, bf16[448,384]{1,0:T(8,128)(2,1)S(1)}, u32[]{:S(2)}, u32[]{:S(2)}) collective-permute-start(bf16[448,384]{1,0:T(8,128)(2,1)S(1)} %collective-permute-done.5), channel_id=1, source_target_pairs={{0,448},{64,0},{128,64},{192,128},{256,192},{320,256},{384,320},{4... | collective-permute-start | bytes 1032200 | tf_op jit(solution)/shard_map/ppermute | solution.py:44
  76.0 3.6 %rev.3 = bf16[8,448,384]{2,1,0:T(8,128)(2,1)} reverse(bf16[8,448,384]{2,1,0:T(8,128)(2,1)} %bitcast_dynamic-update-slice_fusion), dimensions={0} | reverse | bytes 5505024 | tf_op jit(solution)/shard_map/rev | solution.py:47
  79.7 4.5 %fusion.6 = bf16[8,448,384]{2,1,0:T(8,128)(2,1)} fusion(s32[]{:T(128)S(6)} %select_n.134, bf16[8,448,384]{2,1,0:T(8,128)(2,1)} %rev.3), kind=kLoop, calls=%fused_computation.47 | loop fusion | flops 1376256 | bytes 5505028 | tf_op jit(solution)/shard_map/concatenate | solution.py:48
  84.2 4.9 %slice_bitcast_fusion = (bf16[16,4,1,4,3584]{4,3,1,0,2:T(4,128)(2,1)}, bf16[16,4,1,4,3584]{4,3,1,0,2:T(4,128)(2,1)S(1)}) fusion(bf16[16,4,2,4,3584]{4,3,2,1,0:T(4,128)(2,1)} %bitcast.144), kind=kLoop, calls=%fused_computation.48 | loop fusion | bytes 7340032
  89.1 3.9 %reshape_squeeze.7 = bf16[256,3584]{1,0:T(8,128)(2,1)} reshape(bf16[16,4,1,4,3584]{4,3,1,0,2:T(4,128)(2,1)} %get-tuple-element.5) | data formatting | bytes 3670016 | tf_op jit(solution)/shard_map/reshape;squeeze | solution.py:121
  110.1 4.1 %stack_reshape.9 = bf16[16,4,1,4,3584]{4,3,1,0,2:T(4,128)(2,1)} reshape(bf16[256,3584]{1,0:T(8,128)(2,1)} %fusion) | data formatting | bytes 3670016 | tf_op jit(solution)/shard_map/stack;reshape | solution.py:127
  114.2 5.7 %pad_maximum_fusion = bf16[16,4,2,4,3584]{4,3,2,1,0:T(4,128)(2,1)} fusion(bf16[16,4,1,4,3584]{4,3,2,1,0:T(4,128)(2,1)} %bitcast.140, bf16[16,4,1,4,3584]{4,3,2,1,0:T(4,128)(2,1)S(1)} %bitcast.139), kind=kLoop, calls=%fused_computation.14 | loop fusion | flops 1835008 | bytes 7340032 | tf_op jit(solution)/shard_map/stack | solution.py:127
  119.8 6.9 %convert_element_type.220 = bf16[8,2,114688]{2,1,0:T(2,128)(2,1)} reshape(bf16[16,4,2,4,3584]{4,3,2,1,0:T(4,128)(2,1)} %pad_maximum_fusion) | data formatting | bytes 7340032 | tf_op jit(solution)/shard_map/convert_element_type | solution.py:133
  126.7 5.8 %copy.92 = bf16[8,2,114688]{2,0,1:T(8,128)(2,1)} copy(bf16[8,2,114688]{2,1,0:T(2,128)(2,1)} %convert_element_type.220) | data formatting | bytes 7340032 | tf_op jit(solution)/shard_map/convert_element_type | solution.py:133
  136.3 3.8 %copy.95 = bf16[3584,256]{1,0:T(8,128)(2,1)} copy(bf16[3584,256]{0,1:T(8,128)(2,1)} %bitcast.142) | data formatting | bytes 3670016 | tf_op jit(solution)/shard_map/dot_general | solution.py:94
  144.7 6.0 %collective-permute-start.14 = (bf16[448,192]{1,0:T(8,128)(2,1)S(1)}, bf16[448,192]{1,0:T(8,128)(2,1)S(1)}, u32[]{:S(2)}, u32[]{:S(2)}) collective-permute-start(bf16[448,192]{1,0:T(8,128)(2,1)S(1)} %get-tuple-element.9), channel_id=1, source_target_pairs={{0,448},{64,0},{128,64},{192,128},{256,192},{320,256},{384,320},{4... | collective-permute-start | bytes 516104 | tf_op jit(solution)/shard_map/ppermute | solution.py:68
  154.4 5.6 %collective-permute-start.15 = (bf16[448,192]{1,0:T(8,128)(2,1)S(1)}, bf16[448,192]{1,0:T(8,128)(2,1)S(1)}, u32[]{:S(2)}, u32[]{:S(2)}) collective-permute-start(bf16[448,192]{1,0:T(8,128)(2,1)S(1)} %fusion.24), channel_id=1, source_target_pairs={{0,448},{64,0},{128,64},{192,128},{256,192},{320,256},{384,320},{4... | collective-permute-start | bytes 516104 | tf_op jit(solution)/shard_map/ppermute | solution.py:68
  163.7 5.6 %collective-permute-start.16 = (bf16[448,192]{1,0:T(8,128)(2,1)S(1)}, bf16[448,192]{1,0:T(8,128)(2,1)S(1)}, u32[]{:S(2)}, u32[]{:S(2)}) collective-permute-start(bf16[448,192]{1,0:T(8,128)(2,1)S(1)} %fusion.23), channel_id=1, source_target_pairs={{0,448},{64,0},{128,64},{192,128},{256,192},{320,256},{384,320},{4... | collective-permute-start | bytes 516104 | tf_op jit(solution)/shard_map/ppermute | solution.py:68
  173.0 5.6 %collective-permute-start.17 = (bf16[448,192]{1,0:T(8,128)(2,1)S(1)}, bf16[448,192]{1,0:T(8,128)(2,1)S(1)}, u32[]{:S(2)}, u32[]{:S(2)}) collective-permute-start(bf16[448,192]{1,0:T(8,128)(2,1)S(1)} %fusion.22), channel_id=1, source_target_pairs={{0,448},{64,0},{128,64},{192,128},{256,192},{320,256},{384,320},{4... | collective-permute-start | bytes 516104 | tf_op jit(solution)/shard_map/ppermute | solution.py:68
  178.6 3.8 %collective-permute-done.17 = bf16[448,192]{1,0:T(8,128)(2,1)S(1)} collective-permute-done((bf16[448,192]{1,0:T(8,128)(2,1)S(1)}, bf16[448,192]{1,0:T(8,128)(2,1)S(1)}, u32[]{:S(2)}, u32[]{:S(2)}) %collective-permute-start.17) | collective-permute-done | bytes 172064 | tf_op jit(solution)/shard_map/ppermute | solution.py:68
  182.6 5.6 %collective-permute-start.18 = (bf16[448,192]{1,0:T(8,128)(2,1)S(1)}, bf16[448,192]{1,0:T(8,128)(2,1)S(1)}, u32[]{:S(2)}, u32[]{:S(2)}) collective-permute-start(bf16[448,192]{1,0:T(8,128)(2,1)S(1)} %fusion.21), channel_id=1, source_target_pairs={{0,448},{64,0},{128,64},{192,128},{256,192},{320,256},{384,320},{4... | collective-permute-start | bytes 516104 | tf_op jit(solution)/shard_map/ppermute | solution.py:68
  193.3 5.6 %collective-permute-start.19 = (bf16[448,192]{1,0:T(8,128)(2,1)S(1)}, bf16[448,192]{1,0:T(8,128)(2,1)S(1)}, u32[]{:S(2)}, u32[]{:S(2)}) collective-permute-start(bf16[448,192]{1,0:T(8,128)(2,1)S(1)} %fusion.20), channel_id=1, source_target_pairs={{0,448},{64,0},{128,64},{192,128},{256,192},{320,256},{384,320},{4... | collective-permute-start | bytes 516104 | tf_op jit(solution)/shard_map/ppermute | solution.py:68
  202.6 5.6 %collective-permute-start.20 = (bf16[448,192]{1,0:T(8,128)(2,1)S(1)}, bf16[448,192]{1,0:T(8,128)(2,1)S(1)}, u32[]{:S(2)}, u32[]{:S(2)}) collective-permute-start(bf16[448,192]{1,0:T(8,128)(2,1)S(1)} %fusion.19), channel_id=1, source_target_pairs={{0,448},{64,0},{128,64},{192,128},{256,192},{320,256},{384,320},{4... | collective-permute-start | bytes 516104 | tf_op jit(solution)/shard_map/ppermute | solution.py:68
  215.5 10.2 %collective-permute-done.8 = bf16[448,192]{1,0:T(8,128)(2,1)S(1)} collective-permute-done((bf16[448,192]{1,0:T(8,128)(2,1)}, bf16[448,192]{1,0:T(8,128)(2,1)S(1)}, u32[]{:S(2)}, u32[]{:S(2)}) %collective-permute-start.8) | collective-permute-done | bytes 172064 | tf_op jit(solution)/shard_map/ppermute | solution.py:67
  227.7 8.9 %collective-permute-done.9 = bf16[448,192]{1,0:T(8,128)(2,1)S(1)} collective-permute-done((bf16[448,192]{1,0:T(8,128)(2,1)S(1)}, bf16[448,192]{1,0:T(8,128)(2,1)S(1)}, u32[]{:S(2)}, u32[]{:S(2)}) %collective-permute-start.9) | collective-permute-done | bytes 172064 | tf_op jit(solution)/shard_map/ppermute | solution.py:67
  238.7 8.1 %collective-permute-done.10 = bf16[448,192]{1,0:T(8,128)(2,1)S(1)} collective-permute-done((bf16[448,192]{1,0:T(8,128)(2,1)S(1)}, bf16[448,192]{1,0:T(8,128)(2,1)S(1)}, u32[]{:S(2)}, u32[]{:S(2)}) %collective-permute-start.10) | collective-permute-done | bytes 172064 | tf_op jit(solution)/shard_map/ppermute | solution.py:67
  248.8 7.2 %collective-permute-done.11 = bf16[448,192]{1,0:T(8,128)(2,1)S(1)} collective-permute-done((bf16[448,192]{1,0:T(8,128)(2,1)S(1)}, bf16[448,192]{1,0:T(8,128)(2,1)S(1)}, u32[]{:S(2)}, u32[]{:S(2)}) %collective-permute-start.11) | collective-permute-done | bytes 172064 | tf_op jit(solution)/shard_map/ppermute | solution.py:67
  258.1 7.2 %collective-permute-done.12 = bf16[448,192]{1,0:T(8,128)(2,1)S(1)} collective-permute-done((bf16[448,192]{1,0:T(8,128)(2,1)S(1)}, bf16[448,192]{1,0:T(8,128)(2,1)S(1)}, u32[]{:S(2)}, u32[]{:S(2)}) %collective-permute-start.12) | collective-permute-done | bytes 172064 | tf_op jit(solution)/shard_map/ppermute | solution.py:67
  267.2 7.2 %collective-permute-done.13 = bf16[448,192]{1,0:T(8,128)(2,1)S(1)} collective-permute-done((bf16[448,192]{1,0:T(8,128)(2,1)S(1)}, bf16[448,192]{1,0:T(8,128)(2,1)S(1)}, u32[]{:S(2)}, u32[]{:S(2)}) %collective-permute-start.13) | collective-permute-done | bytes 172064 | tf_op jit(solution)/shard_map/ppermute | solution.py:67
  276.2 4.3 %all-to-all-start.1 = ((bf16[4,2,4,3584]{3,2,1,0:T(4,128)(2,1)}), bf16[4,2,4,3584]{3,2,1,0:T(4,128)(2,1)S(1)}, u32[]{:S(2)}, u32[]{:S(2)}) async-start(bf16[4,2,4,3584]{3,2,1,0:T(4,128)(2,1)} %reshape.77), calls=%async_computation.3 | async-start | bytes 458752 | tf_op jit(solution)/shard_map/all_to_all | solution.py:138
  281.5 4.0 %all-to-all-done.1 = bf16[4,2,4,3584]{3,2,1,0:T(4,128)(2,1)S(1)} async-done(((bf16[4,2,4,3584]{3,2,1,0:T(4,128)(2,1)}), bf16[4,2,4,3584]{3,2,1,0:T(4,128)(2,1)S(1)}, u32[]{:S(2)}, u32[]{:S(2)}) %all-to-all-start.1) | async-done | bytes 229408 | tf_op jit(solution)/shard_map/all_to_all | solution.py:138
  (106 shorter events, 90.2 us)
Async XLA Ops:
  7.2 77.0 %all-gather.3.cloned.1.call-start = ((), (), s32[]{:S(2)}) async-start(), calls=%async_computation.6 | async-start | bytes 3899392 | tf_op jit(solution)/shard_map/all_gather | solution.py:119
  9.3 16.0 %copy-start.7 = (bf16[1,448,128]{2,1,0:T(8,128)(2,1)S(1)}, bf16[1,448,128]{2,1,0:T(8,128)(2,1)}, u32[]{:S(2)}) copy-start(bf16[1,448,128]{2,1,0:T(8,128)(2,1)} %param.13) | copy-start | bytes 344068
  9.3 16.0 %copy-start.8 = (bf16[1,448,128]{2,1,0:T(8,128)(2,1)S(1)}, bf16[1,448,128]{2,1,0:T(8,128)(2,1)}, u32[]{:S(2)}) copy-start(bf16[1,448,128]{2,1,0:T(8,128)(2,1)} %param.12) | copy-start | bytes 344068
  9.3 16.0 %copy-start.9 = (bf16[1,448,128]{2,1,0:T(8,128)(2,1)S(1)}, bf16[1,448,128]{2,1,0:T(8,128)(2,1)}, u32[]{:S(2)}) copy-start(bf16[1,448,128]{2,1,0:T(8,128)(2,1)} %param.11) | copy-start | bytes 344068
  25.3 162.9 %reduce-scatter.3.cloned.1.call-start = ((), (), s32[]{:S(2)}) async-start(), calls=%async_computation.4 | async-start | bytes 5505024 | tf_op jit(solution)/shard_map/reduce_scatter | solution.py:135
  25.4 10.7 %collective-permute-start = (bf16[448,384]{1,0:T(8,128)(2,1)S(1)}, bf16[448,384]{1,0:T(8,128)(2,1)S(1)}, u32[]{:S(2)}, u32[]{:S(2)}) collective-permute-start(bf16[448,384]{1,0:T(8,128)(2,1)S(1)} %pad_maximum_fusion.1), channel_id=1, source_target_pairs={{0,64},{64,128},{128,192},{192,256},{256,320},{320,384},{384,448},... | collective-permute-start | bytes 1032200 | tf_op jit(solution)/shard_map/ppermute | solution.py:41
  36.1 11.8 %collective-permute-start.1 = (bf16[448,384]{1,0:T(8,128)(2,1)S(1)}, bf16[448,384]{1,0:T(8,128)(2,1)S(1)}, u32[]{:S(2)}, u32[]{:S(2)}) collective-permute-start(bf16[448,384]{1,0:T(8,128)(2,1)S(1)} %collective-permute-done), channel_id=1, source_target_pairs={{0,64},{64,128},{128,192},{192,256},{256,320},{320,384},{384,448},... | collective-permute-start | bytes 1032200 | tf_op jit(solution)/shard_map/ppermute | solution.py:41
  38.0 12.6 %collective-permute-start.4 = (bf16[448,384]{1,0:T(8,128)(2,1)S(1)}, bf16[448,384]{1,0:T(8,128)(2,1)S(1)}, u32[]{:S(2)}, u32[]{:S(2)}) collective-permute-start(bf16[448,384]{1,0:T(8,128)(2,1)S(1)} %pad_maximum_fusion.1), channel_id=1, source_target_pairs={{0,448},{64,0},{128,64},{192,128},{256,192},{320,256},{384,320},{4... | collective-permute-start | bytes 1032200 | tf_op jit(solution)/shard_map/ppermute | solution.py:44
  47.9 12.9 %collective-permute-start.2 = (bf16[448,384]{1,0:T(8,128)(2,1)S(1)}, bf16[448,384]{1,0:T(8,128)(2,1)S(1)}, u32[]{:S(2)}, u32[]{:S(2)}) collective-permute-start(bf16[448,384]{1,0:T(8,128)(2,1)S(1)} %collective-permute-done.1), channel_id=1, source_target_pairs={{0,64},{64,128},{128,192},{192,256},{256,320},{320,384},{384,448},... | collective-permute-start | bytes 1032200 | tf_op jit(solution)/shard_map/ppermute | solution.py:41
  50.6 12.9 %collective-permute-start.5 = (bf16[448,384]{1,0:T(8,128)(2,1)S(1)}, bf16[448,384]{1,0:T(8,128)(2,1)S(1)}, u32[]{:S(2)}, u32[]{:S(2)}) collective-permute-start(bf16[448,384]{1,0:T(8,128)(2,1)S(1)} %collective-permute-done.4), channel_id=1, source_target_pairs={{0,448},{64,0},{128,64},{192,128},{256,192},{320,256},{384,320},{4... | collective-permute-start | bytes 1032200 | tf_op jit(solution)/shard_map/ppermute | solution.py:44
  60.8 10.3 %collective-permute-start.3 = (bf16[448,384]{1,0:T(8,128)(2,1)S(1)}, bf16[448,384]{1,0:T(8,128)(2,1)S(1)}, u32[]{:S(2)}, u32[]{:S(2)}) collective-permute-start(bf16[448,384]{1,0:T(8,128)(2,1)S(1)} %collective-permute-done.2), channel_id=1, source_target_pairs={{0,64},{64,128},{128,192},{192,256},{256,320},{320,384},{384,448},... | collective-permute-start | bytes 1032200 | tf_op jit(solution)/shard_map/ppermute | solution.py:41
  63.5 10.2 %collective-permute-start.6 = (bf16[448,384]{1,0:T(8,128)(2,1)S(1)}, bf16[448,384]{1,0:T(8,128)(2,1)S(1)}, u32[]{:S(2)}, u32[]{:S(2)}) collective-permute-start(bf16[448,384]{1,0:T(8,128)(2,1)S(1)} %collective-permute-done.5), channel_id=1, source_target_pairs={{0,448},{64,0},{128,64},{192,128},{256,192},{320,256},{384,320},{4... | collective-permute-start | bytes 1032200 | tf_op jit(solution)/shard_map/ppermute | solution.py:44
  94.5 2.6 copy-start.3
  97.2 2.3 copy-start.5
  132.5 142.0 %reduce-scatter.5.cloned.1.call-start = ((), (), s32[]{:S(2)}) async-start(), calls=%async_computation.5 | async-start | bytes 2064384 | tf_op jit(solution)/shard_map/reduce_scatter | solution.py:136
  140.1 2.3 copy-start.2
  144.7 9.6 %collective-permute-start.14 = (bf16[448,192]{1,0:T(8,128)(2,1)S(1)}, bf16[448,192]{1,0:T(8,128)(2,1)S(1)}, u32[]{:S(2)}, u32[]{:S(2)}) collective-permute-start(bf16[448,192]{1,0:T(8,128)(2,1)S(1)} %get-tuple-element.9), channel_id=1, source_target_pairs={{0,448},{64,0},{128,64},{192,128},{256,192},{320,256},{384,320},{4... | collective-permute-start | bytes 516104 | tf_op jit(solution)/shard_map/ppermute | solution.py:68
  154.4 9.1 %collective-permute-start.15 = (bf16[448,192]{1,0:T(8,128)(2,1)S(1)}, bf16[448,192]{1,0:T(8,128)(2,1)S(1)}, u32[]{:S(2)}, u32[]{:S(2)}) collective-permute-start(bf16[448,192]{1,0:T(8,128)(2,1)S(1)} %fusion.24), channel_id=1, source_target_pairs={{0,448},{64,0},{128,64},{192,128},{256,192},{320,256},{384,320},{4... | collective-permute-start | bytes 516104 | tf_op jit(solution)/shard_map/ppermute | solution.py:68
  163.7 9.1 %collective-permute-start.16 = (bf16[448,192]{1,0:T(8,128)(2,1)S(1)}, bf16[448,192]{1,0:T(8,128)(2,1)S(1)}, u32[]{:S(2)}, u32[]{:S(2)}) collective-permute-start(bf16[448,192]{1,0:T(8,128)(2,1)S(1)} %fusion.23), channel_id=1, source_target_pairs={{0,448},{64,0},{128,64},{192,128},{256,192},{320,256},{384,320},{4... | collective-permute-start | bytes 516104 | tf_op jit(solution)/shard_map/ppermute | solution.py:68
  173.0 9.4 %collective-permute-start.17 = (bf16[448,192]{1,0:T(8,128)(2,1)S(1)}, bf16[448,192]{1,0:T(8,128)(2,1)S(1)}, u32[]{:S(2)}, u32[]{:S(2)}) collective-permute-start(bf16[448,192]{1,0:T(8,128)(2,1)S(1)} %fusion.22), channel_id=1, source_target_pairs={{0,448},{64,0},{128,64},{192,128},{256,192},{320,256},{384,320},{4... | collective-permute-start | bytes 516104 | tf_op jit(solution)/shard_map/ppermute | solution.py:68
  182.6 10.5 %collective-permute-start.18 = (bf16[448,192]{1,0:T(8,128)(2,1)S(1)}, bf16[448,192]{1,0:T(8,128)(2,1)S(1)}, u32[]{:S(2)}, u32[]{:S(2)}) collective-permute-start(bf16[448,192]{1,0:T(8,128)(2,1)S(1)} %fusion.21), channel_id=1, source_target_pairs={{0,448},{64,0},{128,64},{192,128},{256,192},{320,256},{384,320},{4... | collective-permute-start | bytes 516104 | tf_op jit(solution)/shard_map/ppermute | solution.py:68
  193.3 9.1 %collective-permute-start.19 = (bf16[448,192]{1,0:T(8,128)(2,1)S(1)}, bf16[448,192]{1,0:T(8,128)(2,1)S(1)}, u32[]{:S(2)}, u32[]{:S(2)}) collective-permute-start(bf16[448,192]{1,0:T(8,128)(2,1)S(1)} %fusion.20), channel_id=1, source_target_pairs={{0,448},{64,0},{128,64},{192,128},{256,192},{320,256},{384,320},{4... | collective-permute-start | bytes 516104 | tf_op jit(solution)/shard_map/ppermute | solution.py:68
  198.9 9.9 %collective-permute-start.7 = (bf16[448,192]{1,0:T(8,128)(2,1)S(1)}, bf16[448,192]{1,0:T(8,128)(2,1)}, u32[]{:S(2)}, u32[]{:S(2)}) collective-permute-start(bf16[448,192]{1,0:T(8,128)(2,1)S(1)} %get-tuple-element.10), channel_id=1, source_target_pairs={{0,64},{64,128},{128,192},{192,256},{256,320},{320,384},{384,448},... | collective-permute-start | bytes 516104 | tf_op jit(solution)/shard_map/ppermute | solution.py:67
  202.6 9.1 %collective-permute-start.20 = (bf16[448,192]{1,0:T(8,128)(2,1)S(1)}, bf16[448,192]{1,0:T(8,128)(2,1)S(1)}, u32[]{:S(2)}, u32[]{:S(2)}) collective-permute-start(bf16[448,192]{1,0:T(8,128)(2,1)S(1)} %fusion.19), channel_id=1, source_target_pairs={{0,448},{64,0},{128,64},{192,128},{256,192},{320,256},{384,320},{4... | collective-permute-start | bytes 516104 | tf_op jit(solution)/shard_map/ppermute | solution.py:68
  213.5 12.2 %collective-permute-start.8 = (bf16[448,192]{1,0:T(8,128)(2,1)}, bf16[448,192]{1,0:T(8,128)(2,1)S(1)}, u32[]{:S(2)}, u32[]{:S(2)}) collective-permute-start(bf16[448,192]{1,0:T(8,128)(2,1)} %get-tuple-element.8), channel_id=1, source_target_pairs={{0,64},{64,128},{128,192},{192,256},{256,320},{320,384},{384,448},... | collective-permute-start | bytes 516104 | tf_op jit(solution)/shard_map/ppermute | solution.py:67
  225.8 10.9 %collective-permute-start.9 = (bf16[448,192]{1,0:T(8,128)(2,1)S(1)}, bf16[448,192]{1,0:T(8,128)(2,1)S(1)}, u32[]{:S(2)}, u32[]{:S(2)}) collective-permute-start(bf16[448,192]{1,0:T(8,128)(2,1)S(1)} %fusion.29), channel_id=1, source_target_pairs={{0,64},{64,128},{128,192},{192,256},{256,320},{320,384},{384,448},... | collective-permute-start | bytes 516104 | tf_op jit(solution)/shard_map/ppermute | solution.py:67
  236.7 10.1 %collective-permute-start.10 = (bf16[448,192]{1,0:T(8,128)(2,1)S(1)}, bf16[448,192]{1,0:T(8,128)(2,1)S(1)}, u32[]{:S(2)}, u32[]{:S(2)}) collective-permute-start(bf16[448,192]{1,0:T(8,128)(2,1)S(1)} %fusion.28), channel_id=1, source_target_pairs={{0,64},{64,128},{128,192},{192,256},{256,320},{320,384},{384,448},... | collective-permute-start | bytes 516104 | tf_op jit(solution)/shard_map/ppermute | solution.py:67
  246.9 9.2 %collective-permute-start.11 = (bf16[448,192]{1,0:T(8,128)(2,1)S(1)}, bf16[448,192]{1,0:T(8,128)(2,1)S(1)}, u32[]{:S(2)}, u32[]{:S(2)}) collective-permute-start(bf16[448,192]{1,0:T(8,128)(2,1)S(1)} %fusion.27), channel_id=1, source_target_pairs={{0,64},{64,128},{128,192},{192,256},{256,320},{320,384},{384,448},... | collective-permute-start | bytes 516104 | tf_op jit(solution)/shard_map/ppermute | solution.py:67
  256.1 9.1 %collective-permute-start.12 = (bf16[448,192]{1,0:T(8,128)(2,1)S(1)}, bf16[448,192]{1,0:T(8,128)(2,1)S(1)}, u32[]{:S(2)}, u32[]{:S(2)}) collective-permute-start(bf16[448,192]{1,0:T(8,128)(2,1)S(1)} %fusion.26), channel_id=1, source_target_pairs={{0,64},{64,128},{128,192},{192,256},{256,320},{320,384},{384,448},... | collective-permute-start | bytes 516104 | tf_op jit(solution)/shard_map/ppermute | solution.py:67
  265.3 9.1 %collective-permute-start.13 = (bf16[448,192]{1,0:T(8,128)(2,1)S(1)}, bf16[448,192]{1,0:T(8,128)(2,1)S(1)}, u32[]{:S(2)}, u32[]{:S(2)}) collective-permute-start(bf16[448,192]{1,0:T(8,128)(2,1)S(1)} %fusion.25), channel_id=1, source_target_pairs={{0,64},{64,128},{128,192},{192,256},{256,320},{320,384},{384,448},... | collective-permute-start | bytes 516104 | tf_op jit(solution)/shard_map/ppermute | solution.py:67
  276.2 9.3 %all-to-all-start.1 = ((bf16[4,2,4,3584]{3,2,1,0:T(4,128)(2,1)}), bf16[4,2,4,3584]{3,2,1,0:T(4,128)(2,1)S(1)}, u32[]{:S(2)}, u32[]{:S(2)}) async-start(bf16[4,2,4,3584]{3,2,1,0:T(4,128)(2,1)} %reshape.77), calls=%async_computation.3 | async-start | bytes 458752 | tf_op jit(solution)/shard_map/all_to_all | solution.py:138
  285.6 3.8 %copy-start.1 = (bf16[128,3584]{1,0:T(8,128)(2,1)S(1)}, bf16[128,3584]{1,0:T(8,128)(2,1)}, u32[]{:S(2)}) copy-start(bf16[128,3584]{1,0:T(8,128)(2,1)} %param.7) | copy-start | bytes 2752516
  (3 other events, 5.1 us)
Sparse Core Ops, SparseCore 0:
  25.4 44.4 all-gather.2
  132.7 17.0 reduce-scatter.2
  191.9 46.1 reduce-scatter.4

commit v5 on v3

v5 whole, which is shorter than its diff:
```python
import jax
import jax.numpy as jnp
from jax import lax
from jax.sharding import Mesh
from jax.sharding import PartitionSpec as P

SPLIT = 16
CAP = 4


SCALE = 2.0 ** (-16)
HIGH = lax.Precision.HIGHEST


def routing(ids, gates, window, capacity):
    wanted = jnp.arange(window, dtype=jnp.int32)
    hits = ids[:, :, None] == wanted[None, None, :]
    member = jnp.any(hits, axis=1)
    weight = jnp.sum(jnp.where(hits, gates[:, :, None], 0), axis=1).astype(jnp.float32) * SCALE
    rank = jnp.cumsum(member.astype(jnp.int32), axis=0) - 1
    slots = jnp.arange(capacity, dtype=jnp.int32)
    pick = jnp.logical_and(member[:, :, None], rank[:, :, None] == slots[None, None, :])
    select = jnp.where(pick, 1.0, 0.0).astype(jnp.float32)
    slot_gate = jnp.sum(select * weight[:, :, None], axis=0)
    return (select, slot_gate)


def expert_math(inputs, cotangents, gate_w, up_w, down_w):
    gate_pre = jnp.einsum("prf,pfh->rh", inputs, gate_w, preferred_element_type=jnp.float32)
    up_pre = jnp.einsum("prf,pfh->rh", inputs, up_w, preferred_element_type=jnp.float32)
    sig = jax.nn.sigmoid(gate_pre)
    act = gate_pre * sig
    hidden = (act * up_pre).astype(jnp.bfloat16)
    partial_out = jnp.einsum("rh,pfh->prf", hidden, down_w, preferred_element_type=jnp.float32)
    d_hidden = jnp.einsum("prf,pfh->rh", cotangents, down_w, preferred_element_type=jnp.float32)
    d_gate = (d_hidden * up_pre * sig * (1.0 + gate_pre * (1.0 - sig))).astype(jnp.bfloat16)
    d_up = (d_hidden * act).astype(jnp.bfloat16)
    partial_grad = jnp.einsum(
        "rh,pfh->prf", d_gate, gate_w, preferred_element_type=jnp.float32
    ) + jnp.einsum("rh,pfh->prf", d_up, up_w, preferred_element_type=jnp.float32)
    term = jnp.concatenate(
        [
            jnp.einsum("prf,rh->pfh", inputs, d_gate, preferred_element_type=jnp.float32),
            jnp.einsum("prf,rh->pfh", inputs, d_up, preferred_element_type=jnp.float32),
            jnp.einsum("prf,rh->pfh", cotangents, hidden, preferred_element_type=jnp.float32),
        ],
        axis=2,
    )
    return (partial_out, partial_grad, term.reshape(-1, term.shape[2]))


def per_device(tokens, out_cotangent, expert_ids, gate_fixed, w_gate, w_up, w_down):
    tok_rows, width = tokens.shape
    window = lax.axis_size("ex")
    zsize = lax.axis_size("ez")
    hid = w_gate.shape[2]
    f32 = jnp.float32
    select, slot_gate = routing(expert_ids, gate_fixed, window, CAP)
    select_b = select.astype(jnp.bfloat16)
    slot_tokens = jnp.einsum("tec,tf->ecf", select_b, tokens, preferred_element_type=f32).astype(
        jnp.bfloat16
    )
    picked = jnp.einsum("tec,tf->ecf", select_b, out_cotangent, preferred_element_type=f32)
    slot_cot = (picked * slot_gate[:, :, None]).astype(jnp.bfloat16)
    payload = jnp.stack([slot_tokens, slot_cot], axis=1)
    w_loc = jnp.concatenate([w_gate[0], w_up[0], w_down[0]], axis=1)
    w_all = lax.all_gather(w_loc, "dp", axis=0, tiled=False).reshape(-1, 3 * hid)
    gate_full = w_all[None, :, :hid]
    up_full = w_all[None, :, hid : 2 * hid]
    down_full = w_all[None, :, 2 * hid :]
    outgoing = jnp.broadcast_to(payload[:, None], (window, zsize, 2, CAP, width)).reshape(
        window * zsize, 2, CAP, width
    )
    mine = lax.all_to_all(outgoing, ("ex", "ez"), split_axis=0, concat_axis=0, tiled=True)
    partner = lax.ppermute(mine, "ec", [(0, 1), (1, 0)])
    arrived = jnp.stack([mine, partner], axis=0)
    inputs = arrived[:, :, 0].reshape(1, -1, width)
    cotangents = arrived[:, :, 1].reshape(1, -1, width)
    partial_out, partial_grad, term = expert_math(inputs, cotangents, gate_full, up_full, down_full)
    summed = lax.psum_scatter(
        term.astype(jnp.bfloat16), "dp", scatter_dimension=0, tiled=True
    ).astype(f32)
    grad_gate = summed[:, :hid][None]
    grad_up = summed[:, hid : 2 * hid][None]
    grad_down = summed[:, 2 * hid :][None]
    results = jnp.stack(
        [
            partial_out.reshape(2, window * zsize, CAP, width),
            partial_grad.reshape(2, window * zsize, CAP, width),
        ],
        axis=2,
    )
    back = lax.ppermute(results[1].astype(jnp.bfloat16), "ec", [(0, 1), (1, 0)])
    pair = (results[0] + back.astype(f32)).astype(jnp.bfloat16)
    returned = lax.all_to_all(pair, ("ex", "ez"), split_axis=0, concat_axis=0, tiled=True)
    combined = jnp.sum(
        returned.reshape(window, zsize, 2, CAP, width).astype(f32), axis=1
    ).astype(jnp.bfloat16).astype(f32)
    weighted = select * slot_gate[None, :, :]
    layer_out = jnp.einsum("tec,ecf->tf", weighted, combined[:, 0], precision=HIGH)
    token_grad = jnp.einsum("tec,ecf->tf", select, combined[:, 1], precision=HIGH)
    return (
        layer_out.astype(jnp.bfloat16),
        token_grad.astype(jnp.bfloat16),
        grad_gate,
        grad_up,
        grad_down,
    )


def solution(mesh):
    n_dp = mesh.shape["dp"]
    n_exp = mesh.shape["expert"]
    devices = mesh.devices.reshape(n_dp, n_exp // SPLIT, SPLIT // 2, 2)
    grid = Mesh(devices, ("dp", "ex", "ez", "ec"))
    tok = P(("dp", "ex", "ez", "ec"), None)
    wsp = P(("ex", "ez", "ec"), "dp", None)
    return jax.shard_map(
        per_device,
        mesh=grid,
        in_specs=(tok, tok, tok, tok, wsp, wsp, wsp),
        out_specs=(tok, tok, wsp, wsp, wsp),
        check_vma=False,
    )
```

time: 295 us -> 194 us (0.66)
  waiting for transfers between devices: 184 us -> 45.9 us
  blocking collectives: 10.1 us -> 47.8 us
  local copies, waits for them, and re-layouts: 47.3 us -> 28.7 us
  starting transfers between devices: 4.32 us -> 20.5 us
  other arithmetic: 10.8 us -> 16.9 us
    all_gather x2 -> x1, waiting for transfers between devices: 80 us -> 0.02 us  [per_device(): lax.all_gather(w_loc, 'dp', axis=0, tiled=False).reshape(-1, 3 * hid)]
    reduce_scatter x2 -> x0, waiting for transfers between devices: 58.5 us -> none  [the longest x1 45.9 us: per_device(): lax.psum_scatter(half.reshape(-1, 256), 'ez', scatter_dimension=0, tiled=...]
    unnamed x6 -> x3, waiting for transfers between devices: 43 us -> 0.03 us
    all_to_all x1, waiting for transfers between devices: 2.83 us -> 42.5 us  [per_device(): lax.all_to_all(outgoing, ('ex', 'ez'), split_axis=0, concat_axis=0, tiled...]
    all_to_all x1, blocking collectives: 10.1 us -> 47.8 us  [per_device(): lax.all_to_all(pair, ('ex', 'ez'), split_axis=0, concat_axis=0, tiled=True)]
    convert_element_type x2 -> x0, local copies, waits for them, and re-layouts: 12.7 us -> none  [per_device(): results = jnp.stack([partial_out.reshape(hsplit, window, CAP, width), par...]
    all_to_all x1, starting transfers between devices: 3.93 us -> 13.8 us  [per_device(): lax.all_to_all(outgoing, ('ex', 'ez'), split_axis=0, concat_axis=0, tiled...]
    convert_element_type x0 -> x3, other arithmetic: none -> 9.26 us  [the longest x1 4.41 us: per_device(): back = lax.ppermute(results[1].astype(jnp.bfloat16), 'ec', [(0, 1), (1, 0)])]
  transfers between devices with their start and end apart: 6 -> 5, of which waited for: 6 -> 2; matrix products, arithmetic and copies ran while one was open for 10% -> 14% of each run, Pallas kernels for 0% -> 0%
where the time goes in v5:
time: 194 us; the launch traced here: 191 us
  blocking collectives  47.8 us (25%)
  waiting for transfers between devices  45.9 us (24%)
  local copies, waits for them, and re-layouts  28.7 us (15%)
  starting transfers between devices  20.5 us (11%)
  other arithmetic  16.9 us (9%)
  matrix products  16.9 us (9%)
  between operations  14.3 us (7%)
    all_to_all x1, blocking collectives, per_device(): lax.all_to_all(pair, ('ex', 'ez'), split_axis=0, concat_axis=0, tiled=True)  47.8 us
    all_to_all x1, waiting for transfers between devices, per_device(): lax.all_to_all(outgoing, ('ex', 'ez'), split_axis=0, concat_axis=0, tiled...  42.5 us
    all_to_all x1, starting transfers between devices, per_device(): lax.all_to_all(outgoing, ('ex', 'ez'), split_axis=0, concat_axis=0, tiled...  13.8 us
    another operation x2, local copies, waits for them, and re-layouts, per_device(): jnp.stack([partial_out.reshape(2, window * zsize, CAP, width), partial_gr...  10.4 us
    unnamed x20, local copies, waits for them, and re-layouts  9.22 us
    convert_element_type x1, other arithmetic, per_device(): back = lax.ppermute(results[1].astype(jnp.bfloat16), 'ec', [(0, 1), (1, 0)])  4.41 us
    ppermute x1, starting transfers between devices, per_device(): partner = lax.ppermute(mine, 'ec', [(0, 1), (1, 0)])  4.14 us
    another operation x1, other arithmetic, per_device(): arrived = jnp.stack([mine, partner], axis=0)  4 us
  transfers between devices with their start and end apart: 5, of which 2 were waited for; matrix products, arithmetic and copies ran while one was open for 14% of the time, Pallas kernels for 0%

profile of v5, /device:TPU:1, one launch (start us, length us, event | category | flops | bytes accessed | tf_op | source)
XLA Modules:
  0.0 191.0 jit_solution(7848320404933630441)
XLA Ops:
  7.2 0.8 fusion.29
  8.0 0.7 select_reduce_fusion
  9.5 1.4 fusion.8
  11.2 1.8 broadcast_in_dim.51
  13.0 13.8 %all-to-all-start = ((bf16[32,2,4,3584]{3,2,1,0:T(4,128)(2,1)}), bf16[32,2,4,3584]{3,2,1,0:T(4,128)(2,1)S(1)}, u32[]{:S(2)}, u32[]{:S(2)}) async-start(bf16[32,2,4,3584]{3,2,1,0:T(4,128)(2,1)} %bitcast.86), calls=%async_computation | async-start | bytes 3670016 | tf_op jit(solution)/shard_map/all_to_all | solution.py:74
  26.9 0.8 pad_maximum_fusion.2
  27.8 42.5 %all-to-all-done = bf16[32,2,4,3584]{3,2,1,0:T(4,128)(2,1)S(1)} async-done(((bf16[32,2,4,3584]{3,2,1,0:T(4,128)(2,1)}), bf16[32,2,4,3584]{3,2,1,0:T(4,128)(2,1)S(1)}, u32[]{:S(2)}, u32[]{:S(2)}) %all-to-all-start) | async-done | bytes 1835040 | tf_op jit(solution)/shard_map/all_to_all | solution.py:74
  70.2 4.1 %collective-permute-start = (bf16[32,2,4,3584]{3,2,1,0:T(4,128)(2,1)S(1)}, bf16[32,2,4,3584]{3,2,1,0:T(4,128)(2,1)S(1)}, u32[]{:S(2)}, u32[]{:S(2)}) collective-permute-start(bf16[32,2,4,3584]{3,2,1,0:T(4,128)(2,1)S(1)} %all-to-all-done), channel_id=1, source_target_pairs={{0,1},{1,0},{2,3},{3,2},{4,5},{5,4},{6,7},{7,6},{8,9},{9,8},{10,11... | collective-permute-start | bytes 5505032 | tf_op jit(solution)/shard_map/ppermute | solution.py:75
  74.4 3.4 %collective-permute-done = bf16[32,2,4,3584]{3,2,1,0:T(4,128)(2,1)S(1)} collective-permute-done((bf16[32,2,4,3584]{3,2,1,0:T(4,128)(2,1)S(1)}, bf16[32,2,4,3584]{3,2,1,0:T(4,128)(2,1)S(1)}, u32[]{:S(2)}, u32[]{:S(2)}) %collective-permute-start) | collective-permute-done | bytes 1835040 | tf_op jit(solution)/shard_map/ppermute | solution.py:75
  77.8 4.0 %pad_maximum_fusion.1 = (bf16[2,32,1,4,3584]{4,3,2,1,0:T(4,128)(2,1)}, bf16[2,32,1,4,3584]{4,3,2,1,0:T(4,128)(2,1)}) fusion(bf16[1,32,2,4,3584]{4,3,2,1,0:T(4,128)(2,1)S(1)} %bitcast.87, bf16[1,32,2,4,3584]{4,3,2,1,0:T(4,128)(2,1)S(1)} %bitcast.85), kind=kLoop, calls=%fused_computation.31 | loop fusion | flops 1835008 | bytes 7340032 | tf_op jit(solution)/shard_map/stack | solution.py:76
  81.8 3.9 %reshape.82 = bf16[256,3584]{1,0:T(8,128)(2,1)} reshape(bf16[2,32,1,4,3584]{4,3,2,1,0:T(4,128)(2,1)} %get-tuple-element.20) | data formatting | bytes 3670016 | tf_op jit(solution)/shard_map/reshape.12
  85.7 2.9 %reshape.81 = bf16[256,3584]{1,0:T(8,128)(2,1)S(1)} reshape(bf16[2,32,1,4,3584]{4,3,2,1,0:T(4,128)(2,1)} %get-tuple-element.21) | data formatting | bytes 3670016 | tf_op jit(solution)/shard_map/reshape
  88.7 2.0 %fusion.19 = f32[256,128]{1,0:T(8,128)S(1)} fusion(bf16[256,3584]{1,0:T(8,128)(2,1)S(1)} %reshape.81, bf16[3584,384]{1,0:T(8,128)(2,1)} %all-gather.3.cloned.1.call-done), kind=kOutput, calls=%fused_computation.36 | convolution fusion | flops 234881024 | bytes 2883584 | tf_op jit(solution)/shard_map/prf,pfh->rh/dot_general | solution.py:30
  91.4 0.8 copy-done.1
  92.2 0.7 multiply_convert_fusion
  93.5 2.5 %fusion = f32[1,256,3584]{2,1,0:T(8,128)} fusion(f32[3584,256]{0,1:T(8,128)S(1)} %fusion.21, bf16[256,128]{1,0:T(8,128)(2,1)S(1)} %get-tuple-element.25, bf16[3584,384]{1,0:T(8,128)(2,1)S(1)} %copy-done.3), kind=kOutput, calls=%fused_computation.3 | convolution fusion | flops 235798528 | bytes 8323072 | tf_op jit(solution)/shard_map/rh,pfh->prf/dot_general | solution.py:40
  96.1 5.2 %stack_reshape.7 = f32[2,32,1,4,3584]{4,3,1,0,2:T(4,128)} reshape(f32[1,256,3584]{2,1,0:T(8,128)} %fusion) | data formatting | bytes 7340032 | tf_op jit(solution)/shard_map/stack;reshape | solution.py:86
  101.2 3.6 %convolution_bitcast_fusion = f32[1,256,3584]{2,1,0:T(8,128)} fusion(bf16[256,128]{1,0:T(8,128)(2,1)S(1)} %get-tuple-element.27, bf16[3584,384]{1,0:T(8,128)(2,1)} %all-gather.3.cloned.1.call-done), kind=kOutput, calls=%fused_computation.4 | convolution fusion | flops 234881024 | bytes 4653056 | tf_op jit(solution)/shard_map/rh,pfh->prf/dot_general | solution.py:34
  104.9 5.2 %stack_reshape.6 = f32[2,32,1,4,3584]{4,3,1,0,2:T(4,128)} reshape(f32[1,256,3584]{2,1,0:T(8,128)} %convolution_bitcast_fusion) | data formatting | bytes 7340032 | tf_op jit(solution)/shard_map/stack;reshape | solution.py:86
  110.1 4.4 %fusion.15 = bf16[32,2,4,3584]{3,2,1,0:T(4,128)(2,1)} fusion(f32[2,32,1,4,3584]{4,3,2,1,0:T(4,128)} %bitcast.81, f32[2,32,1,4,3584]{4,3,2,1,0:T(4,128)} %bitcast.83), kind=kLoop, calls=%fused_computation.30 | loop fusion | flops 917504 | bytes 9175040 | tf_op jit(solution)/shard_map/convert_element_type | solution.py:93
  114.5 2.4 %collective-permute-start.1 = (bf16[32,2,4,3584]{3,2,1,0:T(4,128)(2,1)}, bf16[32,2,4,3584]{3,2,1,0:T(4,128)(2,1)}, u32[]{:S(2)}, u32[]{:S(2)}) collective-permute-start(bf16[32,2,4,3584]{3,2,1,0:T(4,128)(2,1)} %fusion.15), channel_id=1, source_target_pairs={{0,1},{1,0},{2,3},{3,2},{4,5},{5,4},{6,7},{7,6},{8,9},{9,8},{10,11... | collective-permute-start | bytes 5505032 | tf_op jit(solution)/shard_map/ppermute | solution.py:93
  118.4 1.7 maximum_bitcast_fusion
  120.1 4.6 %copy.54 = bf16[3584,384]{1,0:T(8,128)(2,1)} copy(bf16[3584,384]{0,1:T(8,128)(2,1)} %maximum_bitcast_fusion) | data formatting | bytes 5505024
  124.7 3.1 %fusion.12 = bf16[32,2,4,3584]{3,2,1,0:T(4,128)(2,1)S(1)} fusion(f32[2,32,1,4,3584]{4,3,2,1,0:T(4,128)} %bitcast.84, f32[2,32,1,4,3584]{4,3,2,1,0:T(4,128)} %bitcast.82, bf16[32,2,4,3584]{3,2,1,0:T(4,128)(2,1)} %collective-permute-done.1), kind=kLoop, calls=%fused_computation.23 | loop fusion | flops 3670016 | bytes 11010048 | tf_op jit(solution)/shard_map/convert_element_type | solution.py:94
  127.8 47.8 %all_to_all.10 = bf16[32,2,4,3584]{3,2,1,0:T(4,128)(2,1)S(1)} all-to-all(bf16[32,2,4,3584]{3,2,1,0:T(4,128)(2,1)S(1)} %fusion.12), channel_id=1, replica_groups=mesh['dp'=8,'ex'=4,'ez'=8,'ec'=2] {'ex','ez'}, dimensions={0} | all-to-all | bytes 3670016 | tf_op jit(solution)/shard_map/all_to_all | solution.py:95
  175.6 0.8 bitcast_reduce_fusion
  176.5 1.9 fusion.2
  178.4 1.9 %fusion.1 = bf16[128,3584]{1,0:T(8,128)(2,1)} fusion(bf16[4,1,4,3584]{3,2,0,1:T(4,128)(2,1)S(1)} %get-tuple-element.29, f32[4,4]{0,1:T(4,128)S(1)} %get-tuple-element.31, s32[128,4]{0,1:T(4,128)S(1)} %copy.41, pred[128,4]{0,1:T(4,128)(4,1)S(1)} %fusion.29), kind=kOutput, calls=%fused_computation.7 | convolution fusion | flops 88547328 | bytes 1034816 | tf_op jit(solution)/shard_map/tec,ecf->tf/dot_general | solution.py:100
  180.4 1.1 copy.55
  181.7 0.8 copy.53
  182.5 0.8 copy.52
  183.3 0.8 copy.51
  (39 shorter events, 4.2 us)
Async XLA Ops:
  7.2 2.1 %copy-start = (bf16[128,3584]{1,0:T(8,128)(2,1)S(1)}, bf16[128,3584]{1,0:T(8,128)(2,1)}, u32[]{:S(2)}) copy-start(bf16[128,3584]{1,0:T(8,128)(2,1)} %param.7) | copy-start | bytes 2752516
  13.0 13.9 %copy-start.4 = (bf16[1,448,128]{2,1,0:T(8,128)(2,1)S(1)}, bf16[1,448,128]{2,1,0:T(8,128)(2,1)}, u32[]{:S(2)}) copy-start(bf16[1,448,128]{2,1,0:T(8,128)(2,1)} %param.13) | copy-start | bytes 344068
  13.0 13.9 %copy-start.5 = (bf16[1,448,128]{2,1,0:T(8,128)(2,1)S(1)}, bf16[1,448,128]{2,1,0:T(8,128)(2,1)}, u32[]{:S(2)}) copy-start(bf16[1,448,128]{2,1,0:T(8,128)(2,1)} %param.12) | copy-start | bytes 344068
  13.0 13.9 %copy-start.6 = (bf16[1,448,128]{2,1,0:T(8,128)(2,1)S(1)}, bf16[1,448,128]{2,1,0:T(8,128)(2,1)}, u32[]{:S(2)}) copy-start(bf16[1,448,128]{2,1,0:T(8,128)(2,1)} %param.11) | copy-start | bytes 344068
  13.0 57.3 %all-to-all-start = ((bf16[32,2,4,3584]{3,2,1,0:T(4,128)(2,1)}), bf16[32,2,4,3584]{3,2,1,0:T(4,128)(2,1)S(1)}, u32[]{:S(2)}, u32[]{:S(2)}) async-start(bf16[32,2,4,3584]{3,2,1,0:T(4,128)(2,1)} %bitcast.86), calls=%async_computation | async-start | bytes 3670016 | tf_op jit(solution)/shard_map/all_to_all | solution.py:74
  26.8 61.8 %all-gather.3.cloned.1.call-start = ((), (), s32[]{:S(2)}) async-start(), calls=%async_computation.3 | async-start | bytes 3096576 | tf_op jit(solution)/shard_map/all_gather | solution.py:67
  27.7 152.7 %reduce-scatter.4.cloned.1.call-start = ((), (), s32[]{:S(2)}) async-start(), calls=%async_computation.4 | async-start | bytes 3096576
  70.2 7.5 %collective-permute-start = (bf16[32,2,4,3584]{3,2,1,0:T(4,128)(2,1)S(1)}, bf16[32,2,4,3584]{3,2,1,0:T(4,128)(2,1)S(1)}, u32[]{:S(2)}, u32[]{:S(2)}) collective-permute-start(bf16[32,2,4,3584]{3,2,1,0:T(4,128)(2,1)S(1)} %all-to-all-done), channel_id=1, source_target_pairs={{0,1},{1,0},{2,3},{3,2},{4,5},{5,4},{6,7},{7,6},{8,9},{9,8},{10,11... | collective-permute-start | bytes 5505032 | tf_op jit(solution)/shard_map/ppermute | solution.py:75
  88.7 2.1 %copy-start.3 = (bf16[3584,384]{1,0:T(8,128)(2,1)S(1)}, bf16[3584,384]{1,0:T(8,128)(2,1)}, u32[]{:S(2)}) copy-start(bf16[3584,384]{1,0:T(8,128)(2,1)} %all-gather.3.cloned.1.call-done) | copy-start | bytes 8257540
  90.7 1.5 copy-start.1
  110.1 6.9 %copy-start.2 = (bf16[256,3584]{1,0:T(8,128)(2,1)S(1)}, bf16[256,3584]{1,0:T(8,128)(2,1)}, u32[]{:S(2)}) copy-start(bf16[256,3584]{1,0:T(8,128)(2,1)} %reshape.82) | copy-start | bytes 5505028
  114.5 10.1 %collective-permute-start.1 = (bf16[32,2,4,3584]{3,2,1,0:T(4,128)(2,1)}, bf16[32,2,4,3584]{3,2,1,0:T(4,128)(2,1)}, u32[]{:S(2)}, u32[]{:S(2)}) collective-permute-start(bf16[32,2,4,3584]{3,2,1,0:T(4,128)(2,1)} %fusion.15), channel_id=1, source_target_pairs={{0,1},{1,0},{2,3},{3,2},{4,5},{5,4},{6,7},{7,6},{8,9},{9,8},{10,11... | collective-permute-start | bytes 5505032 | tf_op jit(solution)/shard_map/ppermute | solution.py:93
Sparse Core Ops, SparseCore 0:
  30.3 44.7 all-gather.2
  124.8 40.2 reduce-scatter.3

commit v6 on v5

v6 whole, which is shorter than its diff:
```python
import jax
import jax.numpy as jnp
from jax import lax
from jax.sharding import Mesh
from jax.sharding import PartitionSpec as P

SPLIT = 16
CAP = 4


SCALE = 2.0 ** (-16)
HIGH = lax.Precision.HIGHEST


def routing(ids, gates, window, capacity):
    wanted = jnp.arange(window, dtype=jnp.int32)
    hits = ids[:, :, None] == wanted[None, None, :]
    member = jnp.any(hits, axis=1)
    weight = jnp.sum(jnp.where(hits, gates[:, :, None], 0), axis=1).astype(jnp.float32) * SCALE
    rank = jnp.cumsum(member.astype(jnp.int32), axis=0) - 1
    slots = jnp.arange(capacity, dtype=jnp.int32)
    pick = jnp.logical_and(member[:, :, None], rank[:, :, None] == slots[None, None, :])
    select = jnp.where(pick, 1.0, 0.0).astype(jnp.float32)
    slot_gate = jnp.sum(select * weight[:, :, None], axis=0)
    return (select, slot_gate)


def expert_math(inputs, cotangents, gate_w, up_w, down_w):
    f32 = jnp.float32
    nt = (((1,), (1,)), ((), ()))
    tn = (((0,), (0,)), ((), ()))
    gate_pre = jnp.dot(inputs, gate_w, preferred_element_type=f32)
    up_pre = jnp.dot(inputs, up_w, preferred_element_type=f32)
    sig = jax.nn.sigmoid(gate_pre)
    act = gate_pre * sig
    hidden = (act * up_pre).astype(jnp.bfloat16)
    partial_out = lax.dot_general(hidden, down_w, nt, preferred_element_type=f32)
    d_hidden = jnp.dot(cotangents, down_w, preferred_element_type=f32)
    d_gate = (d_hidden * up_pre * sig * (1.0 + gate_pre * (1.0 - sig))).astype(jnp.bfloat16)
    d_up = (d_hidden * act).astype(jnp.bfloat16)
    partial_grad = lax.dot_general(d_gate, gate_w, nt, preferred_element_type=f32) + lax.dot_general(
        d_up, up_w, nt, preferred_element_type=f32
    )
    term = jnp.concatenate(
        [
            lax.dot_general(inputs, d_gate, tn, preferred_element_type=f32),
            lax.dot_general(inputs, d_up, tn, preferred_element_type=f32),
            lax.dot_general(cotangents, hidden, tn, preferred_element_type=f32),
        ],
        axis=1,
    )
    return (partial_out, partial_grad, term)


def dispatch(slots, window, zsize):
    cap, width = slots.shape[1], slots.shape[2]
    outgoing = jnp.broadcast_to(slots[:, None], (window, zsize, cap, width)).reshape(
        window * zsize, cap, width
    )
    mine = lax.all_to_all(outgoing, ("ex", "ez"), split_axis=0, concat_axis=0, tiled=True)
    partner = lax.ppermute(mine, "ec", [(0, 1), (1, 0)])
    return jnp.concatenate([mine, partner], axis=0).reshape(-1, width)


def give_back(partial, window, zsize, cap):
    width = partial.shape[1]
    halves = partial.reshape(2, window * zsize, cap, width)
    back = lax.ppermute(halves[1].astype(jnp.bfloat16), "ec", [(0, 1), (1, 0)])
    pair = (halves[0] + back.astype(jnp.float32)).astype(jnp.bfloat16)
    returned = lax.all_to_all(pair, ("ex", "ez"), split_axis=0, concat_axis=0, tiled=True)
    total = jnp.sum(returned.reshape(window, zsize, cap, width).astype(jnp.float32), axis=1)
    return total.astype(jnp.bfloat16).astype(jnp.float32)


def per_device(tokens, out_cotangent, expert_ids, gate_fixed, w_gate, w_up, w_down):
    window = lax.axis_size("ex")
    zsize = lax.axis_size("ez")
    hid = w_gate.shape[2]
    f32 = jnp.float32
    select, slot_gate = routing(expert_ids, gate_fixed, window, CAP)
    select_b = select.astype(jnp.bfloat16)
    slot_tokens = jnp.einsum("tec,tf->ecf", select_b, tokens, preferred_element_type=f32).astype(
        jnp.bfloat16
    )
    picked = jnp.einsum("tec,tf->ecf", select_b, out_cotangent, preferred_element_type=f32)
    slot_cot = (picked * slot_gate[:, :, None]).astype(jnp.bfloat16)
    w_loc = jnp.concatenate([w_gate[0], w_up[0], w_down[0]], axis=1)
    w_all = lax.all_gather(w_loc, "dp", axis=0, tiled=False).reshape(-1, 3 * hid)
    inputs = dispatch(slot_tokens, window, zsize)
    cotangents = dispatch(slot_cot, window, zsize)
    partial_out, partial_grad, term = expert_math(
        inputs, cotangents, w_all[:, :hid], w_all[:, hid : 2 * hid], w_all[:, 2 * hid :]
    )
    summed = lax.psum_scatter(
        term.astype(jnp.bfloat16), "dp", scatter_dimension=0, tiled=True
    ).astype(f32)
    grad_gate = summed[:, :hid][None]
    grad_up = summed[:, hid : 2 * hid][None]
    grad_down = summed[:, 2 * hid :][None]
    out_slots = give_back(partial_out, window, zsize, CAP)
    grad_slots = give_back(partial_grad, window, zsize, CAP)
    weighted = select * slot_gate[None, :, :]
    layer_out = jnp.einsum("tec,ecf->tf", weighted, out_slots, precision=HIGH)
    token_grad = jnp.einsum("tec,ecf->tf", select, grad_slots, precision=HIGH)
    return (
        layer_out.astype(jnp.bfloat16),
        token_grad.astype(jnp.bfloat16),
        grad_gate,
        grad_up,
        grad_down,
    )


def solution(mesh):
    n_dp = mesh.shape["dp"]
    n_exp = mesh.shape["expert"]
    devices = mesh.devices.reshape(n_dp, n_exp // SPLIT, SPLIT // 2, 2)
    grid = Mesh(devices, ("dp", "ex", "ez", "ec"))
    tok = P(("dp", "ex", "ez", "ec"), None)
    wsp = P(("ex", "ez", "ec"), "dp", None)
    return jax.shard_map(
        per_device,
        mesh=grid,
        in_specs=(tok, tok, tok, tok, wsp, wsp, wsp),
        out_specs=(tok, tok, wsp, wsp, wsp),
        check_vma=False,
    )
```

time: 194 us -> 212 us (1.093)
  the two profiles are of different devices: /device:TPU:1 before, /device:TPU:32 now
where the time goes in v6:
time: 212 us; the launch traced here: 210 us
  waiting for transfers between devices  92.4 us (44%)
  starting transfers between devices  36.8 us (17%)
  local copies, waits for them, and re-layouts  33.5 us (16%)
  other arithmetic  19.3 us (9%)
  between operations  14.4 us (7%)
  matrix products  13.9 us (7%)
    all_to_all x2, waiting for transfers between devices, dispatch(): lax.all_to_all(outgoing, ('ex', 'ez'), split_axis=0, concat_axis=0, tiled...  48.6 us
    all_to_all x2, waiting for transfers between devices, give_back(): lax.all_to_all(pair, ('ex', 'ez'), split_axis=0, concat_axis=0, tiled=True)  43.8 us
    all_to_all x2, starting transfers between devices, dispatch(): lax.all_to_all(outgoing, ('ex', 'ez'), split_axis=0, concat_axis=0, tiled...  18.1 us
    unnamed x31, local copies, waits for them, and re-layouts  14.2 us
    all_to_all x2, starting transfers between devices, give_back(): lax.all_to_all(pair, ('ex', 'ez'), split_axis=0, concat_axis=0, tiled=True)  10.3 us
    concatenate x2, other arithmetic, dispatch(): return jnp.concatenate([mine, partner], axis=0).reshape(-1, width)  6.55 us
    convert_element_type x2, other arithmetic, give_back(): pair = (halves[0] + back.astype(jnp.float32)).astype(jnp.bfloat16)  6.3 us
    convert_element_type x2, local copies, waits for them, and re-layouts, give_back(): back = lax.ppermute(halves[1].astype(jnp.bfloat16), 'ec', [(0, 1), (1, 0)])  5.04 us
  transfers between devices with their start and end apart: 10, of which 4 were waited for; matrix products, arithmetic and copies ran while one was open for 20% of the time, Pallas kernels for 0%

profile of v6, /device:TPU:32, one launch (start us, length us, event | category | flops | bytes accessed | tf_op | source)
XLA Modules:
  0.0 210.3 jit_solution(3895081545367737432)
XLA Ops:
  10.7 13.2 %all-to-all-start.2 = ((bf16[32,4,3584]{2,1,0:T(4,128)(2,1)}), bf16[32,4,3584]{2,1,0:T(4,128)(2,1)S(1)}, u32[]{:S(2)}, u32[]{:S(2)}) async-start(bf16[32,4,3584]{2,1,0:T(4,128)(2,1)} %bitcast.8), calls=%async_computation.2 | async-start | bytes 1835008 | tf_op jit(solution)/shard_map/all_to_all | solution.py:60
  25.0 24.9 %all-to-all-done.2 = bf16[32,4,3584]{2,1,0:T(4,128)(2,1)S(1)} async-done(((bf16[32,4,3584]{2,1,0:T(4,128)(2,1)}), bf16[32,4,3584]{2,1,0:T(4,128)(2,1)S(1)}, u32[]{:S(2)}, u32[]{:S(2)}) %all-to-all-start.2) | async-done | bytes 917536 | tf_op jit(solution)/shard_map/all_to_all | solution.py:60
  51.1 5.0 %all-to-all-start = ((bf16[32,4,3584]{2,1,0:T(4,128)(2,1)}), bf16[32,4,3584]{2,1,0:T(4,128)(2,1)}, u32[]{:S(2)}, u32[]{:S(2)}) async-start(bf16[32,4,3584]{2,1,0:T(4,128)(2,1)} %bitcast.1), calls=%async_computation | async-start | bytes 1835008 | tf_op jit(solution)/shard_map/all_to_all | solution.py:60
  56.2 1.9 collective-permute-start.2
  58.1 23.7 %all-to-all-done = bf16[32,4,3584]{2,1,0:T(4,128)(2,1)} async-done(((bf16[32,4,3584]{2,1,0:T(4,128)(2,1)}), bf16[32,4,3584]{2,1,0:T(4,128)(2,1)}, u32[]{:S(2)}, u32[]{:S(2)}) %all-to-all-start) | async-done | bytes 917536 | tf_op jit(solution)/shard_map/all_to_all | solution.py:60
  81.8 1.9 collective-permute-start
  83.7 2.6 %pad_maximum_fusion.2 = bf16[64,4,3584]{2,1,0:T(4,128)(2,1)S(1)} fusion(bf16[32,4,3584]{2,1,0:T(4,128)(2,1)} %collective-permute-done.2, bf16[32,4,3584]{2,1,0:T(4,128)(2,1)} %copy-done.5), kind=kLoop, calls=%fused_computation.15 | loop fusion | flops 917504 | bytes 3670016 | tf_op jit(solution)/shard_map/concatenate | solution.py:62
  86.3 1.5 reshape.68
  87.8 3.9 %pad_maximum_fusion.1 = bf16[64,4,3584]{2,1,0:T(4,128)(2,1)} fusion(bf16[32,4,3584]{2,1,0:T(4,128)(2,1)} %collective-permute-done, bf16[32,4,3584]{2,1,0:T(4,128)(2,1)} %all-to-all-done), kind=kLoop, calls=%fused_computation.14 | loop fusion | flops 917504 | bytes 3670016 | tf_op jit(solution)/shard_map/concatenate | solution.py:62
  91.7 2.9 %reshape.64 = bf16[256,3584]{1,0:T(8,128)(2,1)S(1)} reshape(bf16[64,4,3584]{2,1,0:T(4,128)(2,1)} %pad_maximum_fusion.1) | data formatting | bytes 3670016 | tf_op jit(solution)/shard_map/reshape | solution.py:62
  94.7 2.0 fusion.10
  103.0 1.8 copy-done.2
  105.8 2.5 %convert_element_type.80 = bf16[32,4,3584]{2,1,0:T(4,128)(2,1)} reshape(bf16[128,3584]{1,0:T(8,128)(2,1)} %slice.73) | data formatting | bytes 1835008 | tf_op jit(solution)/shard_map/convert_element_type | solution.py:68
  108.4 2.6 %collective-permute-start.3 = (bf16[32,4,3584]{2,1,0:T(4,128)(2,1)}, bf16[32,4,3584]{2,1,0:T(4,128)(2,1)}, u32[]{:S(2)}, u32[]{:S(2)}) collective-permute-start(bf16[32,4,3584]{2,1,0:T(4,128)(2,1)} %convert_element_type.80), channel_id=1, source_target_pairs={{0,1},{1,0},{2,3},{3,2},{4,5},{5,4},{6,7},{7,6},{8,9},{9,8},{10,11... | collective-permute-start | bytes 2752520 | tf_op jit(solution)/shard_map/ppermute | solution.py:68
  112.9 1.7 pad_maximum_fusion
  114.6 4.5 %copy.44 = bf16[3584,384]{1,0:T(8,128)(2,1)} copy(bf16[3584,384]{0,1:T(8,128)(2,1)} %pad_maximum_fusion) | data formatting | bytes 5505024
  119.1 1.8 fusion.7
  121.0 1.8 copy-done.1
  123.8 2.5 %convert_element_type.73 = bf16[32,4,3584]{2,1,0:T(4,128)(2,1)} reshape(bf16[128,3584]{1,0:T(8,128)(2,1)} %slice.74) | data formatting | bytes 1835008 | tf_op jit(solution)/shard_map/convert_element_type | solution.py:68
  126.3 1.8 squeeze.21
  128.1 1.9 collective-permute-start.1
  130.1 3.1 %add_convert_fusion = bf16[32,4,3584]{2,1,0:T(4,128)(2,1)} fusion(f32[32,4,3584]{2,1,0:T(4,128)} %squeeze.21, bf16[32,4,3584]{2,1,0:T(4,128)(2,1)} %collective-permute-done.3), kind=kLoop, calls=%fused_computation.16 | loop fusion | flops 1376256 | bytes 3670016 | tf_op jit(solution)/shard_map/convert_element_type | solution.py:69
  133.2 4.9 %all-to-all-start.3 = ((bf16[32,4,3584]{2,1,0:T(4,128)(2,1)}), bf16[32,4,3584]{2,1,0:T(4,128)(2,1)}, u32[]{:S(2)}, u32[]{:S(2)}) async-start(bf16[32,4,3584]{2,1,0:T(4,128)(2,1)} %add_convert_fusion), calls=%async_computation.3 | async-start | bytes 1835008 | tf_op jit(solution)/shard_map/all_to_all | solution.py:70
  138.1 1.5 slice-done
  139.6 1.8 squeeze.20
  141.4 3.2 %add_convert_fusion.1 = bf16[32,4,3584]{2,1,0:T(4,128)(2,1)} fusion(f32[32,4,3584]{2,1,0:T(4,128)} %squeeze.20, bf16[32,4,3584]{2,1,0:T(4,128)(2,1)} %collective-permute-done.1), kind=kLoop, calls=%fused_computation.17 | loop fusion | flops 1376256 | bytes 3670016 | tf_op jit(solution)/shard_map/convert_element_type | solution.py:69
  144.6 19.7 %all-to-all-done.3 = bf16[32,4,3584]{2,1,0:T(4,128)(2,1)} async-done(((bf16[32,4,3584]{2,1,0:T(4,128)(2,1)}), bf16[32,4,3584]{2,1,0:T(4,128)(2,1)}, u32[]{:S(2)}, u32[]{:S(2)}) %all-to-all-start.3) | async-done | bytes 917536 | tf_op jit(solution)/shard_map/all_to_all | solution.py:70
  164.3 5.4 %all-to-all-start.1 = ((bf16[32,4,3584]{2,1,0:T(4,128)(2,1)}), bf16[32,4,3584]{2,1,0:T(4,128)(2,1)S(1)}, u32[]{:S(2)}, u32[]{:S(2)}) async-start(bf16[32,4,3584]{2,1,0:T(4,128)(2,1)} %add_convert_fusion.1), calls=%async_computation.1 | async-start | bytes 1835008 | tf_op jit(solution)/shard_map/all_to_all | solution.py:70
  169.7 1.6 bitcast_reduce_fusion
  171.3 24.1 %all-to-all-done.1 = bf16[32,4,3584]{2,1,0:T(4,128)(2,1)S(1)} async-done(((bf16[32,4,3584]{2,1,0:T(4,128)(2,1)}), bf16[32,4,3584]{2,1,0:T(4,128)(2,1)S(1)}, u32[]{:S(2)}, u32[]{:S(2)}) %all-to-all-start.1) | async-done | bytes 917536 | tf_op jit(solution)/shard_map/all_to_all | solution.py:70
  195.9 1.9 fusion.1
  197.8 1.9 fusion
  (68 shorter events, 20.3 us)
Async XLA Ops:
  7.2 2.1 copy-start
  9.3 14.7 %copy-start.10 = (bf16[1,448,128]{2,1,0:T(8,128)(2,1)S(1)}, bf16[1,448,128]{2,1,0:T(8,128)(2,1)}, u32[]{:S(2)}) copy-start(bf16[1,448,128]{2,1,0:T(8,128)(2,1)} %param.13) | copy-start | bytes 344068
  9.3 14.7 %copy-start.11 = (bf16[1,448,128]{2,1,0:T(8,128)(2,1)S(1)}, bf16[1,448,128]{2,1,0:T(8,128)(2,1)}, u32[]{:S(2)}) copy-start(bf16[1,448,128]{2,1,0:T(8,128)(2,1)} %param.12) | copy-start | bytes 344068
  9.3 14.7 %copy-start.12 = (bf16[1,448,128]{2,1,0:T(8,128)(2,1)S(1)}, bf16[1,448,128]{2,1,0:T(8,128)(2,1)}, u32[]{:S(2)}) copy-start(bf16[1,448,128]{2,1,0:T(8,128)(2,1)} %param.11) | copy-start | bytes 344068
  9.5 15.3 %copy-start.9 = (bf16[128,3584]{1,0:T(8,128)(2,1)S(1)}, bf16[128,3584]{1,0:T(8,128)(2,1)}, u32[]{:S(2)}) copy-start(bf16[128,3584]{1,0:T(8,128)(2,1)} %param.7) | copy-start | bytes 2752516
  10.7 39.2 %all-to-all-start.2 = ((bf16[32,4,3584]{2,1,0:T(4,128)(2,1)}), bf16[32,4,3584]{2,1,0:T(4,128)(2,1)S(1)}, u32[]{:S(2)}, u32[]{:S(2)}) async-start(bf16[32,4,3584]{2,1,0:T(4,128)(2,1)} %bitcast.8), calls=%async_computation.2 | async-start | bytes 1835008 | tf_op jit(solution)/shard_map/all_to_all | solution.py:60
  23.9 70.8 %all-gather.3.cloned.1.call-start = ((), (), s32[]{:S(2)}) async-start(), calls=%async_computation.5 | async-start | bytes 3096576 | tf_op jit(solution)/shard_map/all_gather | solution.py:88
  49.9 33.8 %copy-start.5 = (bf16[32,4,3584]{2,1,0:T(4,128)(2,1)}, bf16[32,4,3584]{2,1,0:T(4,128)(2,1)S(1)}, u32[]{:S(2)}) copy-start(bf16[32,4,3584]{2,1,0:T(4,128)(2,1)S(1)} %all-to-all-done.2) | copy-start | bytes 2752516
  51.1 30.6 %all-to-all-start = ((bf16[32,4,3584]{2,1,0:T(4,128)(2,1)}), bf16[32,4,3584]{2,1,0:T(4,128)(2,1)}, u32[]{:S(2)}, u32[]{:S(2)}) async-start(bf16[32,4,3584]{2,1,0:T(4,128)(2,1)} %bitcast.1), calls=%async_computation | async-start | bytes 1835008 | tf_op jit(solution)/shard_map/all_to_all | solution.py:60
  56.1 143.6 %reduce-scatter.4.cloned.1.call-start = ((), (), s32[]{:S(2)}) async-start(), calls=%async_computation.6 | async-start | bytes 3096576
  56.2 27.5 %collective-permute-start.2 = (bf16[32,4,3584]{2,1,0:T(4,128)(2,1)S(1)}, bf16[32,4,3584]{2,1,0:T(4,128)(2,1)}, u32[]{:S(2)}, u32[]{:S(2)}) collective-permute-start(bf16[32,4,3584]{2,1,0:T(4,128)(2,1)S(1)} %all-to-all-done.2), channel_id=1, source_target_pairs={{0,1},{1,0},{2,3},{3,2},{4,5},{5,4},{6,7},{7,6},{8,9},{9,8},{10,11... | collective-permute-start | bytes 2752520 | tf_op jit(solution)/shard_map/ppermute | solution.py:61
  81.8 6.1 %collective-permute-start = (bf16[32,4,3584]{2,1,0:T(4,128)(2,1)}, bf16[32,4,3584]{2,1,0:T(4,128)(2,1)}, u32[]{:S(2)}, u32[]{:S(2)}) collective-permute-start(bf16[32,4,3584]{2,1,0:T(4,128)(2,1)} %all-to-all-done), channel_id=1, source_target_pairs={{0,1},{1,0},{2,3},{3,2},{4,5},{5,4},{6,7},{7,6},{8,9},{9,8},{10,11... | collective-permute-start | bytes 2752520 | tf_op jit(solution)/shard_map/ppermute | solution.py:61
  94.7 2.1 copy-start.8
  96.8 1.5 copy-start.3
  103.0 1.8 copy-start.2
  104.8 6.1 %copy-start.4 = (bf16[256,3584]{1,0:T(8,128)(2,1)S(1)}, bf16[256,3584]{1,0:T(8,128)(2,1)}, u32[]{:S(2)}) copy-start(bf16[256,3584]{1,0:T(8,128)(2,1)} %reshape.68) | copy-start | bytes 5505028
  108.4 21.7 %collective-permute-start.3 = (bf16[32,4,3584]{2,1,0:T(4,128)(2,1)}, bf16[32,4,3584]{2,1,0:T(4,128)(2,1)}, u32[]{:S(2)}, u32[]{:S(2)}) collective-permute-start(bf16[32,4,3584]{2,1,0:T(4,128)(2,1)} %convert_element_type.80), channel_id=1, source_target_pairs={{0,1},{1,0},{2,3},{3,2},{4,5},{5,4},{6,7},{7,6},{8,9},{9,8},{10,11... | collective-permute-start | bytes 2752520 | tf_op jit(solution)/shard_map/ppermute | solution.py:68
  111.4 1.2 copy-start.6
  111.4 1.4 copy-start.7
  121.0 1.9 copy-start.1
  122.8 3.5 %slice-start.1 = ((f32[256,3584]{1,0:T(8,128)}), f32[128,3584]{1,0:T(8,128)S(1)}, s32[]{:S(2)}) async-start(f32[256,3584]{1,0:T(8,128)} %copy-done.2), calls=%async_computation.8 | async-start | bytes 3670016 | tf_op jit(solution)/shard_map/slice | solution.py:69
  128.1 13.3 %collective-permute-start.1 = (bf16[32,4,3584]{2,1,0:T(4,128)(2,1)}, bf16[32,4,3584]{2,1,0:T(4,128)(2,1)}, u32[]{:S(2)}, u32[]{:S(2)}) collective-permute-start(bf16[32,4,3584]{2,1,0:T(4,128)(2,1)} %convert_element_type.73), channel_id=1, source_target_pairs={{0,1},{1,0},{2,3},{3,2},{4,5},{5,4},{6,7},{7,6},{8,9},{9,8},{10,11... | collective-permute-start | bytes 2752520 | tf_op jit(solution)/shard_map/ppermute | solution.py:68
  133.2 31.1 %all-to-all-start.3 = ((bf16[32,4,3584]{2,1,0:T(4,128)(2,1)}), bf16[32,4,3584]{2,1,0:T(4,128)(2,1)}, u32[]{:S(2)}, u32[]{:S(2)}) async-start(bf16[32,4,3584]{2,1,0:T(4,128)(2,1)} %add_convert_fusion), calls=%async_computation.3 | async-start | bytes 1835008 | tf_op jit(solution)/shard_map/all_to_all | solution.py:70
  138.1 1.5 slice-start
  164.3 31.2 %all-to-all-start.1 = ((bf16[32,4,3584]{2,1,0:T(4,128)(2,1)}), bf16[32,4,3584]{2,1,0:T(4,128)(2,1)S(1)}, u32[]{:S(2)}, u32[]{:S(2)}) async-start(bf16[32,4,3584]{2,1,0:T(4,128)(2,1)} %add_convert_fusion.1), calls=%async_computation.1 | async-start | bytes 1835008 | tf_op jit(solution)/shard_map/all_to_all | solution.py:70
Sparse Core Ops, SparseCore 0:
  26.8 43.9 all-gather.2
  119.3 41.2 reduce-scatter.3

commit v7 on v5

--- a/solution.py
+++ b/solution.py
@@ -25,28 +25,34 @@
     return (select, slot_gate)
 
 
-def expert_math(inputs, cotangents, gate_w, up_w, down_w):
-    gate_pre = jnp.einsum("prf,pfh->rh", inputs, gate_w, preferred_element_type=jnp.float32)
-    up_pre = jnp.einsum("prf,pfh->rh", inputs, up_w, preferred_element_type=jnp.float32)
+def expert_math(rows, w_all, hid):
+    f32 = jnp.float32
+    bf16 = jnp.bfloat16
+    nt = (((1,), (1,)), ((), ()))
+    tn = (((0,), (0,)), ((), ()))
+    n = rows.shape[0]
+    pre = jnp.dot(rows.reshape(-1, rows.shape[-1]), w_all, preferred_element_type=f32)
+    pre = pre.reshape(n, 2, -1, 3 * hid)
+    gate_pre = pre[:, 0, :, :hid]
+    up_pre = pre[:, 0, :, hid : 2 * hid]
+    d_hidden = pre[:, 1, :, 2 * hid :]
     sig = jax.nn.sigmoid(gate_pre)
     act = gate_pre * sig
-    hidden = (act * up_pre).astype(jnp.bfloat16)
-    partial_out = jnp.einsum("rh,pfh->prf", hidden, down_w, preferred_element_type=jnp.float32)
-    d_hidden = jnp.einsum("prf,pfh->rh", cotangents, down_w, preferred_element_type=jnp.float32)
-    d_gate = (d_hidden * up_pre * sig * (1.0 + gate_pre * (1.0 - sig))).astype(jnp.bfloat16)
-    d_up = (d_hidden * act).astype(jnp.bfloat16)
-    partial_grad = jnp.einsum(
-        "rh,pfh->prf", d_gate, gate_w, preferred_element_type=jnp.float32
-    ) + jnp.einsum("rh,pfh->prf", d_up, up_w, preferred_element_type=jnp.float32)
-    term = jnp.concatenate(
-        [
-            jnp.einsum("prf,rh->pfh", inputs, d_gate, preferred_element_type=jnp.float32),
-            jnp.einsum("prf,rh->pfh", inputs, d_up, preferred_element_type=jnp.float32),
-            jnp.einsum("prf,rh->pfh", cotangents, hidden, preferred_element_type=jnp.float32),
-        ],
-        axis=2,
-    )
-    return (partial_out, partial_grad, term.reshape(-1, term.shape[2]))
+    hidden = (act * up_pre).astype(bf16)
+    d_gate = (d_hidden * up_pre * sig * (1.0 + gate_pre * (1.0 - sig))).astype(bf16)
+    d_up = (d_hidden * act).astype(bf16)
+    zero = jnp.zeros_like(hidden)
+    tok_side = jnp.concatenate([d_gate, d_up, zero], axis=-1)
+    cot_side = jnp.concatenate([zero, zero, hidden], axis=-1)
+    grad_side = jnp.stack([tok_side, cot_side], axis=1).reshape(-1, 3 * hid)
+    out_side = jnp.stack(
+        [jnp.concatenate([zero, zero, hidden], axis=-1), jnp.concatenate([d_gate, d_up, zero], axis=-1)],
+        axis=1,
+    ).reshape(-1, 3 * hid)
+    flat = rows.reshape(-1, rows.shape[-1])
+    term = lax.dot_general(flat, grad_side, tn, preferred_element_type=f32)
+    results = lax.dot_general(out_side, w_all, nt, preferred_element_type=f32)
+    return results.reshape(rows.shape), term
 
 
 def per_device(tokens, out_cotangent, expert_ids, gate_fixed, w_gate, w_up, w_down):
@@ -65,33 +71,22 @@
     payload = jnp.stack([slot_tokens, slot_cot], axis=1)
     w_loc = jnp.concatenate([w_gate[0], w_up[0], w_down[0]], axis=1)
     w_all = lax.all_gather(w_loc, "dp", axis=0, tiled=False).reshape(-1, 3 * hid)
-    gate_full = w_all[None, :, :hid]
-    up_full = w_all[None, :, hid : 2 * hid]
-    down_full = w_all[None, :, 2 * hid :]
     outgoing = jnp.broadcast_to(payload[:, None], (window, zsize, 2, CAP, width)).reshape(
         window * zsize, 2, CAP, width
     )
     mine = lax.all_to_all(outgoing, ("ex", "ez"), split_axis=0, concat_axis=0, tiled=True)
     partner = lax.ppermute(mine, "ec", [(0, 1), (1, 0)])
-    arrived = jnp.stack([mine, partner], axis=0)
-    inputs = arrived[:, :, 0].reshape(1, -1, width)
-    cotangents = arrived[:, :, 1].reshape(1, -1, width)
-    partial_out, partial_grad, term = expert_math(inputs, cotangents, gate_full, up_full, down_full)
+    arrived = jnp.concatenate([mine, partner], axis=0)
+    results, term = expert_math(arrived, w_all, hid)
     summed = lax.psum_scatter(
         term.astype(jnp.bfloat16), "dp", scatter_dimension=0, tiled=True
     ).astype(f32)
     grad_gate = summed[:, :hid][None]
     grad_up = summed[:, hid : 2 * hid][None]
     grad_down = summed[:, 2 * hid :][None]
-    results = jnp.stack(
-        [
-            partial_out.reshape(2, window * zsize, CAP, width),
-            partial_grad.reshape(2, window * zsize, CAP, width),
-        ],
-        axis=2,
-    )
-    back = lax.ppermute(results[1].astype(jnp.bfloat16), "ec", [(0, 1), (1, 0)])
-    pair = (results[0] + back.astype(f32)).astype(jnp.bfloat16)
+    halves = results.reshape(2, window * zsize, 2, CAP, width)
+    back = lax.ppermute(halves[1].astype(jnp.bfloat16), "ec", [(0, 1), (1, 0)])
+    pair = (halves[0] + back.astype(f32)).astype(jnp.bfloat16)
     returned = lax.all_to_all(pair, ("ex", "ez"), split_axis=0, concat_axis=0, tiled=True)
     combined = jnp.sum(
         returned.reshape(window, zsize, 2, CAP, width).astype(f32), axis=1

time: 194 us -> 180 us (0.928)
  other arithmetic: 16.9 us -> 7.79 us
  local copies, waits for them, and re-layouts: 28.7 us -> 20.7 us
  matrix products: 16.9 us -> 20 us
    another operation x3 -> x1, local copies, waits for them, and re-layouts: 14.3 us -> 0.31 us  [expert_math(): jnp.stack([jnp.concatenate([zero, zero, hidden], axis=-1), jnp.concatenat...]
    unnamed x20 -> x10, local copies, waits for them, and re-layouts: 9.22 us -> 2.97 us
    convert_element_type x3 -> x2, other arithmetic: 9.26 us -> 3.11 us  [the longest x1 3.02 us: per_device(): pair = (halves[0] + back.astype(f32)).astype(jnp.bfloat16)]
    squeeze x0 -> x1, local copies, waits for them, and re-layouts: none -> 5.17 us  [per_device(): pair = (halves[0] + back.astype(f32)).astype(jnp.bfloat16)]
    slice x0 -> x3, local copies, waits for them, and re-layouts: none -> 4.46 us  [the longest x1 4.19 us: per_device(): pair = (halves[0] + back.astype(f32)).astype(jnp.bfloat16)]
    another operation x1 -> x2, other arithmetic: 4 us -> 0.09 us  [expert_math(): jnp.stack([jnp.concatenate([zero, zero, hidden], axis=-1), jnp.concatenat...]
    dot_general x9 -> x3, matrix products: 11.4 us -> 14.5 us  [the longest x1 5.67 us: expert_math(): term = lax.dot_general(flat, grad_side, tn, preferred_element_type=f32)]
    reshape x1, local copies, waits for them, and re-layouts: 2.94 us -> 0.1 us  [expert_math(): out_side = jnp.stack([jnp.concatenate([zero, zero, hidden], axis=-1), jnp...]
  transfers between devices with their start and end apart: 5 -> 5, of which waited for: 2 -> 2; matrix products, arithmetic and copies ran while one was open for 14% -> 15% of each run, Pallas kernels for 0% -> 0%
where the time goes in v7:
time: 180 us; the launch traced here: 178 us
  blocking collectives  49.4 us (27%)
  waiting for transfers between devices  45.9 us (26%)
  local copies, waits for them, and re-layouts  20.7 us (12%)
  starting transfers between devices  20.2 us (11%)
  matrix products  20 us (11%)
  between operations  14.2 us (8%)
  other arithmetic  7.79 us (4%)
    all_to_all x1, blocking collectives, per_device(): lax.all_to_all(pair, ('ex', 'ez'), split_axis=0, concat_axis=0, tiled=True)  49.4 us
    all_to_all x1, waiting for transfers between devices, per_device(): lax.all_to_all(outgoing, ('ex', 'ez'), split_axis=0, concat_axis=0, tiled...  42.5 us
    all_to_all x1, starting transfers between devices, per_device(): lax.all_to_all(outgoing, ('ex', 'ez'), split_axis=0, concat_axis=0, tiled...  13.7 us
    dot_general x1, matrix products, expert_math(): term = lax.dot_general(flat, grad_side, tn, preferred_element_type=f32)  5.67 us
    squeeze x1, local copies, waits for them, and re-layouts, per_device(): pair = (halves[0] + back.astype(f32)).astype(jnp.bfloat16)  5.17 us
    dot_general x1, matrix products, expert_math(): jnp.dot(rows.reshape(-1, rows.shape[-1]), w_all, preferred_element_type=f32)  4.94 us
    slice x1, local copies, waits for them, and re-layouts, per_device(): pair = (halves[0] + back.astype(f32)).astype(jnp.bfloat16)  4.19 us
    ppermute x1, starting transfers between devices, per_device(): partner = lax.ppermute(mine, 'ec', [(0, 1), (1, 0)])  4.14 us
  transfers between devices with their start and end apart: 5, of which 2 were waited for; matrix products, arithmetic and copies ran while one was open for 15% of the time, Pallas kernels for 0%

profile of v7, /device:TPU:1, one launch (start us, length us, event | category | flops | bytes accessed | tf_op | source)
XLA Modules:
  0.0 178.2 jit_solution(12371074728323747911)
XLA Ops:
  7.2 0.8 fusion.14
  8.0 0.7 select_reduce_fusion
  8.7 0.1 copy.42
  8.8 0.2 reduce_window_sum.11
  9.3 0.2 fusion.4
  9.5 1.4 fusion.5
  10.9 0.2 pad_maximum_fusion.2
  11.2 1.8 broadcast_in_dim.51
  13.0 13.7 %all-to-all-start = ((bf16[32,2,4,3584]{3,2,1,0:T(4,128)(2,1)}), bf16[32,2,4,3584]{3,2,1,0:T(4,128)(2,1)S(1)}, u32[]{:S(2)}, u32[]{:S(2)}) async-start(bf16[32,2,4,3584]{3,2,1,0:T(4,128)(2,1)} %bitcast.4), calls=%async_computation | async-start | bytes 3670016 | tf_op jit(solution)/shard_map/all_to_all | solution.py:77
  26.8 0.8 pad_maximum_fusion.1
  27.6 42.5 %all-to-all-done = bf16[32,2,4,3584]{3,2,1,0:T(4,128)(2,1)S(1)} async-done(((bf16[32,2,4,3584]{3,2,1,0:T(4,128)(2,1)}), bf16[32,2,4,3584]{3,2,1,0:T(4,128)(2,1)S(1)}, u32[]{:S(2)}, u32[]{:S(2)}) %all-to-all-start) | async-done | bytes 1835040 | tf_op jit(solution)/shard_map/all_to_all | solution.py:77
  70.1 1.9 %fusion.32 = (bf16[32,2,4,3584]{3,0,2,1:T(8,128)(2,1)S(1)}, bf16[64,2,4,3584]{3,0,2,1:T(8,128)(2,1)}) fusion(bf16[32,2,4,3584]{3,2,1,0:T(4,128)(2,1)S(1)} %all-to-all-done), kind=kLoop, calls=%fused_computation.65 | loop fusion | bytes 5505024 | tf_op jit(solution)/shard_map/all_to_all | solution.py:77
  72.0 4.1 %collective-permute-start = (bf16[32,2,4,3584]{3,0,2,1:T(8,128)(2,1)S(1)}, bf16[32,2,4,3584]{3,0,2,1:T(8,128)(2,1)S(1)}, u32[]{:S(2)}, u32[]{:S(2)}) collective-permute-start(bf16[32,2,4,3584]{3,0,2,1:T(8,128)(2,1)S(1)} %get-tuple-element.5), channel_id=1, source_target_pairs={{0,1},{1,0},{2,3},{3,2},{4,5},{5,4},{6,7},{7,6},{8,9},{9,8},{10,11... | collective-permute-start | bytes 5505032 | tf_op jit(solution)/shard_map/ppermute | solution.py:78
  76.1 3.4 %collective-permute-done = bf16[32,2,4,3584]{3,0,2,1:T(8,128)(2,1)S(1)} collective-permute-done((bf16[32,2,4,3584]{3,0,2,1:T(8,128)(2,1)S(1)}, bf16[32,2,4,3584]{3,0,2,1:T(8,128)(2,1)S(1)}, u32[]{:S(2)}, u32[]{:S(2)}) %collective-permute-start) | collective-permute-done | bytes 1835040 | tf_op jit(solution)/shard_map/ppermute | solution.py:78
  79.5 1.4 constant_dynamic-update-slice_fusion
  80.9 4.9 %fusion.6 = f32[64,2,4,384]{3,0,2,1:T(8,128)S(1)} fusion(bf16[64,2,4,3584]{3,0,2,1:T(8,128)(2,1)} %constant_dynamic-update-slice_fusion, bf16[3584,384]{1,0:T(8,128)(2,1)} %all-gather.3.cloned.1.call-done), kind=kOutput, calls=%fused_computation.13 | convolution fusion | flops 1409286144 | bytes 7208960 | tf_op jit(solution)/shard_map/dot_general | solution.py:34
  86.1 0.3 copy.50
  86.5 3.9 %fusion.34 = f32[512,3584]{1,0:T(8,128)S(1)} fusion(bf16[512,384]{1,0:T(8,128)(2,1)S(1)} %reshape.54, bf16[3584,384]{1,0:T(8,128)(2,1)} %all-gather.3.cloned.1.call-done), kind=kOutput, calls=%fused_computation.67 | convolution fusion | flops 1409286144 | bytes 10485760 | tf_op jit(solution)/shard_map/dot_general | solution.py:54
  90.4 2.9 %copy-done.1 = f32[512,3584]{1,0:T(8,128)} copy-done((f32[512,3584]{1,0:T(8,128)}, f32[512,3584]{1,0:T(8,128)S(1)}, u32[]{:S(2)}) %copy-start.1) | copy-done | bytes 7340056
  93.3 0.2 slice.76
  93.5 1.5 convert_element_type.65
  95.0 2.3 %collective-permute-start.1 = (bf16[32,2,4,3584]{3,2,1,0:T(4,128)(2,1)}, bf16[32,2,4,3584]{3,2,1,0:T(4,128)(2,1)S(1)}, u32[]{:S(2)}, u32[]{:S(2)}) collective-permute-start(bf16[32,2,4,3584]{3,2,1,0:T(4,128)(2,1)} %convert_element_type.65), channel_id=1, source_target_pairs={{0,1},{1,0},{2,3},{3,2},{4,5},{5,4},{6,7},{7,6},{8,9},{9,8},{10,11... | collective-permute-start | bytes 5505032 | tf_op jit(solution)/shard_map/ppermute | solution.py:88
  97.2 4.2 %slice.46 = f32[256,3584]{1,0:T(8,128)} slice(f32[512,3584]{1,0:T(8,128)} %copy-done.1), slice={[0:256], [0:3584]} | slice | bytes 7340032 | tf_op jit(solution)/shard_map/slice | solution.py:89
  101.4 5.7 %fusion = bf16[3584,384]{1,0:T(8,128)(2,1)} fusion(bf16[64,2,4,3584]{3,0,2,1:T(8,128)(2,1)} %constant_dynamic-update-slice_fusion, bf16[64,1,4,384]{3,0,2,1:T(8,128)(2,1)S(1)} %get-tuple-element.18, bf16[64,1,4,384]{3,0,2,1:T(8,128)(2,1)S(1)} %get-tuple-element.17), kind=kOutput, calls=%fused_computation.1 | convolution fusion | flops 1410859008 | bytes 6815744 | tf_op jit(solution)/shard_map/dot_general | solution.py:53
  107.1 5.2 %squeeze.34 = f32[32,2,4,3584]{3,2,1,0:T(4,128)} reshape(f32[256,3584]{1,0:T(8,128)} %slice.46) | data formatting | bytes 7340032 | tf_op jit(solution)/shard_map/squeeze | solution.py:89
  112.3 3.0 %add_convert_fusion = bf16[32,2,4,3584]{3,2,1,0:T(4,128)(2,1)S(1)} fusion(f32[32,2,4,3584]{3,2,1,0:T(4,128)} %squeeze.34, bf16[32,2,4,3584]{3,2,1,0:T(4,128)(2,1)S(1)} %collective-permute-done.1), kind=kLoop, calls=%fused_computation.12 | loop fusion | flops 2752512 | bytes 7340032 | tf_op jit(solution)/shard_map/convert_element_type | solution.py:89
  115.3 49.4 %all_to_all.10 = bf16[32,2,4,3584]{3,2,1,0:T(4,128)(2,1)S(1)} all-to-all(bf16[32,2,4,3584]{3,2,1,0:T(4,128)(2,1)S(1)} %add_convert_fusion), channel_id=1, replica_groups=mesh['dp'=8,'ex'=4,'ez'=8,'ec'=2] {'ex','ez'}, dimensions={0} | all-to-all | bytes 3670016 | tf_op jit(solution)/shard_map/all_to_all | solution.py:90
  164.7 0.8 bitcast_reduce_fusion
  165.6 1.9 %fusion.2 = bf16[128,3584]{1,0:T(8,128)(2,1)} fusion(bf16[4,1,4,3584]{3,2,1,0:T(4,128)(2,1)S(1)} %get-tuple-element.13, s32[128,4]{0,1:T(4,128)S(1)} %copy.43, pred[128,4]{0,1:T(4,128)(4,1)S(1)} %fusion.14), kind=kOutput, calls=%fused_computation.5 | convolution fusion | flops 88545280 | bytes 1034752 | tf_op jit(solution)/shard_map/tec,ecf->tf/dot_general | solution.py:96
  167.5 1.9 %fusion.1 = bf16[128,3584]{1,0:T(8,128)(2,1)} fusion(bf16[4,1,4,3584]{3,2,1,0:T(4,128)(2,1)S(1)} %get-tuple-element.14, f32[4,4]{0,1:T(4,128)S(1)} %get-tuple-element.16, s32[128,4]{0,1:T(4,128)S(1)} %copy.43, pred[128,4]{0,1:T(4,128)(4,1)S(1)} %fusion.14), kind=kOutput, calls=%fused_computation.4 | convolution fusion | flops 88547328 | bytes 1034816 | tf_op jit(solution)/shard_map/tec,ecf->tf/dot_general | solution.py:95
  169.5 1.0 convert_element_type.71
  170.5 0.9 slice_bitcast_fusion
  (30 shorter events, 0.9 us)
Async XLA Ops:
  7.2 2.1 %copy-start = (bf16[128,3584]{1,0:T(8,128)(2,1)S(1)}, bf16[128,3584]{1,0:T(8,128)(2,1)}, u32[]{:S(2)}) copy-start(bf16[128,3584]{1,0:T(8,128)(2,1)} %param.7) | copy-start | bytes 2752516
  11.2 15.6 %copy-start.2 = (bf16[1,448,128]{2,1,0:T(8,128)(2,1)S(1)}, bf16[1,448,128]{2,1,0:T(8,128)(2,1)}, u32[]{:S(2)}) copy-start(bf16[1,448,128]{2,1,0:T(8,128)(2,1)} %param.13) | copy-start | bytes 344068
  11.2 15.6 %copy-start.3 = (bf16[1,448,128]{2,1,0:T(8,128)(2,1)S(1)}, bf16[1,448,128]{2,1,0:T(8,128)(2,1)}, u32[]{:S(2)}) copy-start(bf16[1,448,128]{2,1,0:T(8,128)(2,1)} %param.12) | copy-start | bytes 344068
  11.2 15.6 %copy-start.4 = (bf16[1,448,128]{2,1,0:T(8,128)(2,1)S(1)}, bf16[1,448,128]{2,1,0:T(8,128)(2,1)}, u32[]{:S(2)}) copy-start(bf16[1,448,128]{2,1,0:T(8,128)(2,1)} %param.11) | copy-start | bytes 344068
  13.0 57.1 %all-to-all-start = ((bf16[32,2,4,3584]{3,2,1,0:T(4,128)(2,1)}), bf16[32,2,4,3584]{3,2,1,0:T(4,128)(2,1)S(1)}, u32[]{:S(2)}, u32[]{:S(2)}) async-start(bf16[32,2,4,3584]{3,2,1,0:T(4,128)(2,1)} %bitcast.4), calls=%async_computation | async-start | bytes 3670016 | tf_op jit(solution)/shard_map/all_to_all | solution.py:77
  26.7 54.2 %all-gather.3.cloned.1.call-start = ((), (), s32[]{:S(2)}) async-start(), calls=%async_computation.4 | async-start | bytes 3096576 | tf_op jit(solution)/shard_map/all_gather | solution.py:73
  27.6 141.9 %reduce-scatter.2.cloned.1.call-start = ((), (), s32[]{:S(2)}) async-start(), calls=%async_computation.3 | async-start | bytes 3096576 | tf_op jit(solution)/shard_map/reduce_scatter | solution.py:81
  72.0 7.5 %collective-permute-start = (bf16[32,2,4,3584]{3,0,2,1:T(8,128)(2,1)S(1)}, bf16[32,2,4,3584]{3,0,2,1:T(8,128)(2,1)S(1)}, u32[]{:S(2)}, u32[]{:S(2)}) collective-permute-start(bf16[32,2,4,3584]{3,0,2,1:T(8,128)(2,1)S(1)} %get-tuple-element.5), channel_id=1, source_target_pairs={{0,1},{1,0},{2,3},{3,2},{4,5},{5,4},{6,7},{7,6},{8,9},{9,8},{10,11... | collective-permute-start | bytes 5505032 | tf_op jit(solution)/shard_map/ppermute | solution.py:78
  90.4 3.0 %copy-start.1 = (f32[512,3584]{1,0:T(8,128)}, f32[512,3584]{1,0:T(8,128)S(1)}, u32[]{:S(2)}) copy-start(f32[512,3584]{1,0:T(8,128)S(1)} %fusion.34) | copy-start | bytes 22020100
  95.0 17.3 %collective-permute-start.1 = (bf16[32,2,4,3584]{3,2,1,0:T(4,128)(2,1)}, bf16[32,2,4,3584]{3,2,1,0:T(4,128)(2,1)S(1)}, u32[]{:S(2)}, u32[]{:S(2)}) collective-permute-start(bf16[32,2,4,3584]{3,2,1,0:T(4,128)(2,1)} %convert_element_type.65), channel_id=1, source_target_pairs={{0,1},{1,0},{2,3},{3,2},{4,5},{5,4},{6,7},{7,6},{8,9},{9,8},{10,11... | collective-permute-start | bytes 5505032 | tf_op jit(solution)/shard_map/ppermute | solution.py:88
Sparse Core Ops, SparseCore 0:
  30.2 44.7 all-gather.2
  107.3 40.2 reduce-scatter.1

commit v8 on v7

--- a/solution.py
+++ b/solution.py
@@ -31,7 +31,8 @@
     nt = (((1,), (1,)), ((), ()))
     tn = (((0,), (0,)), ((), ()))
     n = rows.shape[0]
-    pre = jnp.dot(rows.reshape(-1, rows.shape[-1]), w_all, preferred_element_type=f32)
+    flat = rows.reshape(-1, rows.shape[-1])
+    pre = jnp.dot(flat, w_all, preferred_element_type=f32)
     pre = pre.reshape(n, 2, -1, 3 * hid)
     gate_pre = pre[:, 0, :, :hid]
     up_pre = pre[:, 0, :, hid : 2 * hid]
@@ -49,10 +50,9 @@
         [jnp.concatenate([zero, zero, hidden], axis=-1), jnp.concatenate([d_gate, d_up, zero], axis=-1)],
         axis=1,
     ).reshape(-1, 3 * hid)
-    flat = rows.reshape(-1, rows.shape[-1])
     term = lax.dot_general(flat, grad_side, tn, preferred_element_type=f32)
     results = lax.dot_general(out_side, w_all, nt, preferred_element_type=f32)
-    return results.reshape(rows.shape), term
+    return results, term
 
 
 def per_device(tokens, out_cotangent, expert_ids, gate_fixed, w_gate, w_up, w_down):
@@ -68,11 +68,11 @@
     )
     picked = jnp.einsum("tec,tf->ecf", select_b, out_cotangent, preferred_element_type=f32)
     slot_cot = (picked * slot_gate[:, :, None]).astype(jnp.bfloat16)
-    payload = jnp.stack([slot_tokens, slot_cot], axis=1)
+    payload = jnp.concatenate([slot_tokens, slot_cot], axis=1)
     w_loc = jnp.concatenate([w_gate[0], w_up[0], w_down[0]], axis=1)
     w_all = lax.all_gather(w_loc, "dp", axis=0, tiled=False).reshape(-1, 3 * hid)
-    outgoing = jnp.broadcast_to(payload[:, None], (window, zsize, 2, CAP, width)).reshape(
-        window * zsize, 2, CAP, width
+    outgoing = jnp.broadcast_to(payload[:, None], (window, zsize, 2 * CAP, width)).reshape(
+        window * zsize, 2 * CAP, width
     )
     mine = lax.all_to_all(outgoing, ("ex", "ez"), split_axis=0, concat_axis=0, tiled=True)
     partner = lax.ppermute(mine, "ec", [(0, 1), (1, 0)])
@@ -84,13 +84,13 @@
     grad_gate = summed[:, :hid][None]
     grad_up = summed[:, hid : 2 * hid][None]
     grad_down = summed[:, 2 * hid :][None]
-    halves = results.reshape(2, window * zsize, 2, CAP, width)
+    halves = results.reshape(2, window * zsize, 2 * CAP, width)
     back = lax.ppermute(halves[1].astype(jnp.bfloat16), "ec", [(0, 1), (1, 0)])
     pair = (halves[0] + back.astype(f32)).astype(jnp.bfloat16)
     returned = lax.all_to_all(pair, ("ex", "ez"), split_axis=0, concat_axis=0, tiled=True)
     combined = jnp.sum(
-        returned.reshape(window, zsize, 2, CAP, width).astype(f32), axis=1
-    ).astype(jnp.bfloat16).astype(f32)
+        returned.reshape(window, zsize, 2 * CAP, width).astype(f32), axis=1
+    ).astype(jnp.bfloat16).astype(f32).reshape(window, 2, CAP, width)
     weighted = select * slot_gate[None, :, :]
     layer_out = jnp.einsum("tec,ecf->tf", weighted, combined[:, 0], precision=HIGH)
     token_grad = jnp.einsum("tec,ecf->tf", select, combined[:, 1], precision=HIGH)

time: 180 us -> 170 us (0.944)
  local copies, waits for them, and re-layouts: 20.7 us -> 12.8 us
    squeeze x1 -> x0, local copies, waits for them, and re-layouts: 5.17 us -> none  [per_device(): pair = (halves[0] + back.astype(f32)).astype(jnp.bfloat16)]
    slice x3 -> x0, local copies, waits for them, and re-layouts: 4.46 us -> none  [the longest x1 4.19 us: per_device(): pair = (halves[0] + back.astype(f32)).astype(jnp.bfloat16)]
    unnamed x10 -> x13, local copies, waits for them, and re-layouts: 2.97 us -> 4.99 us
    all_to_all x1 -> x0, local copies, waits for them, and re-layouts: 1.88 us -> none  [per_device(): lax.all_to_all(outgoing, ('ex', 'ez'), split_axis=0, concat_axis=0, tiled...]
  transfers between devices with their start and end apart: 5 -> 5, of which waited for: 2 -> 2; matrix products, arithmetic and copies ran while one was open for 15% -> 10% of each run, Pallas kernels for 0% -> 0%
where the time goes in v8:
time: 170 us; the launch traced here: 168 us
  blocking collectives  47.8 us (28%)
  waiting for transfers between devices  45.7 us (27%)
  starting transfers between devices  20.2 us (12%)
  matrix products  20.1 us (12%)
  between operations  14.3 us (8%)
  local copies, waits for them, and re-layouts  12.8 us (8%)
  other arithmetic  6.63 us (4%)
    all_to_all x1, blocking collectives, per_device(): lax.all_to_all(pair, ('ex', 'ez'), split_axis=0, concat_axis=0, tiled=True)  47.8 us
    all_to_all x1, waiting for transfers between devices, per_device(): lax.all_to_all(outgoing, ('ex', 'ez'), split_axis=0, concat_axis=0, tiled...  42.5 us
    all_to_all x1, starting transfers between devices, per_device(): lax.all_to_all(outgoing, ('ex', 'ez'), split_axis=0, concat_axis=0, tiled...  13.7 us
    dot_general x1, matrix products, expert_math(): term = lax.dot_general(flat, grad_side, tn, preferred_element_type=f32)  5.78 us
    unnamed x13, local copies, waits for them, and re-layouts  4.99 us
    dot_general x1, matrix products, expert_math(): pre = jnp.dot(flat, w_all, preferred_element_type=f32)  4.94 us
    ppermute x1, starting transfers between devices, per_device(): partner = lax.ppermute(mine, 'ec', [(0, 1), (1, 0)])  4.14 us
    dot_general x1, matrix products, expert_math(): results = lax.dot_general(out_side, w_all, nt, preferred_element_type=f32)  3.88 us
  transfers between devices with their start and end apart: 5, of which 2 were waited for; matrix products, arithmetic and copies ran while one was open for 10% of the time, Pallas kernels for 0%

profile of v8, /device:TPU:1, one launch (start us, length us, event | category | flops | bytes accessed | tf_op | source)
XLA Modules:
  0.0 167.5 jit_solution(11574277691568840878)
XLA Ops:
  7.2 0.8 fusion.12
  8.1 0.2 reduce_window_sum.11
  8.3 0.7 select_reduce_fusion
  9.3 0.2 convolution_convert_fusion.1
  9.5 1.4 fusion.2
  10.9 0.1 pad_maximum_fusion.3
  11.1 1.4 broadcast_in_dim.51
  12.5 13.7 %all-to-all-start = ((bf16[32,8,3584]{2,1,0:T(8,128)(2,1)}), bf16[32,8,3584]{2,1,0:T(8,128)(2,1)S(1)}, u32[]{:S(2)}, u32[]{:S(2)}) async-start(bf16[32,8,3584]{2,1,0:T(8,128)(2,1)} %bitcast.80), calls=%async_computation | async-start | bytes 3670016 | tf_op jit(solution)/shard_map/all_to_all | solution.py:77
  26.3 0.8 pad_maximum_fusion.2
  27.1 42.5 %all-to-all-done = bf16[32,8,3584]{2,1,0:T(8,128)(2,1)S(1)} async-done(((bf16[32,8,3584]{2,1,0:T(8,128)(2,1)}), bf16[32,8,3584]{2,1,0:T(8,128)(2,1)S(1)}, u32[]{:S(2)}, u32[]{:S(2)}) %all-to-all-start) | async-done | bytes 1835040 | tf_op jit(solution)/shard_map/all_to_all | solution.py:77
  69.6 4.1 %collective-permute-start = (bf16[32,8,3584]{2,1,0:T(8,128)(2,1)S(1)}, bf16[32,8,3584]{2,1,0:T(8,128)(2,1)S(1)}, u32[]{:S(2)}, u32[]{:S(2)}) collective-permute-start(bf16[32,8,3584]{2,1,0:T(8,128)(2,1)S(1)} %all-to-all-done), channel_id=1, source_target_pairs={{0,1},{1,0},{2,3},{3,2},{4,5},{5,4},{6,7},{7,6},{8,9},{9,8},{10,11... | collective-permute-start | bytes 5505032 | tf_op jit(solution)/shard_map/ppermute | solution.py:78
  73.8 0.1 constant_dynamic-update-slice_fusion.1
  73.9 3.2 %collective-permute-done = bf16[32,8,3584]{2,1,0:T(8,128)(2,1)S(1)} collective-permute-done((bf16[32,8,3584]{2,1,0:T(8,128)(2,1)S(1)}, bf16[32,8,3584]{2,1,0:T(8,128)(2,1)S(1)}, u32[]{:S(2)}, u32[]{:S(2)}) %collective-permute-start) | collective-permute-done | bytes 1835040 | tf_op jit(solution)/shard_map/ppermute | solution.py:78
  77.1 0.1 constant_dynamic-update-slice_fusion
  77.3 1.9 %copy-done.2 = bf16[64,8,3584]{2,1,0:T(8,128)(2,1)} copy-done((bf16[64,8,3584]{2,1,0:T(8,128)(2,1)}, bf16[64,8,3584]{2,1,0:T(8,128)(2,1)S(1)}, u32[]{:S(2)}) %copy-start.2) | copy-done | bytes 3670040
  79.2 2.8 %copy.46 = bf16[64,8,3584]{2,0,1:T(8,128)(2,1)} copy(bf16[64,8,3584]{2,1,0:T(8,128)(2,1)S(1)} %constant_dynamic-update-slice_fusion) | data formatting | bytes 7340032 | tf_op jit(solution)/shard_map/concatenate | solution.py:79
  82.0 4.9 %fusion.6 = f32[64,2,4,384]{3,0,2,1:T(8,128)S(1)} fusion(bf16[64,2,4,3584]{3,0,2,1:T(8,128)(2,1)} %bitcast.81, bf16[3584,384]{1,0:T(8,128)(2,1)} %all-gather.3.cloned.1.call-done), kind=kOutput, calls=%fused_computation.13 | convolution fusion | flops 1409286144 | bytes 7208960 | tf_op jit(solution)/shard_map/dot_general | solution.py:35
  87.2 0.3 copy.47
  87.6 3.9 %fusion.29 = f32[512,3584]{1,0:T(8,128)S(1)} fusion(bf16[512,384]{1,0:T(8,128)(2,1)S(1)} %reshape.61, bf16[3584,384]{1,0:T(8,128)(2,1)} %all-gather.3.cloned.1.call-done), kind=kOutput, calls=%fused_computation.63 | convolution fusion | flops 1409286144 | bytes 10485760 | tf_op jit(solution)/shard_map/dot_general | solution.py:54
  91.5 2.9 %copy-done.1 = f32[512,3584]{1,0:T(8,128)} copy-done((f32[512,3584]{1,0:T(8,128)}, f32[512,3584]{1,0:T(8,128)S(1)}, u32[]{:S(2)}) %copy-start.1) | copy-done | bytes 7340056
  94.4 1.4 fusion.8
  95.8 2.3 %collective-permute-start.1 = (bf16[32,8,3584]{2,1,0:T(8,128)(2,1)}, bf16[32,8,3584]{2,1,0:T(8,128)(2,1)S(1)}, u32[]{:S(2)}, u32[]{:S(2)}) collective-permute-start(bf16[32,8,3584]{2,1,0:T(8,128)(2,1)} %fusion.8), channel_id=1, source_target_pairs={{0,1},{1,0},{2,3},{3,2},{4,5},{5,4},{6,7},{7,6},{8,9},{9,8},{10,11... | collective-permute-start | bytes 5505032 | tf_op jit(solution)/shard_map/ppermute | solution.py:88
  98.1 0.3 copy.49
  98.5 5.8 %convolution_convert_fusion = bf16[3584,384]{1,0:T(8,128)(2,1)} fusion(bf16[512,384]{1,0:T(8,128)(2,1)S(1)} %reshape.65, bf16[64,8,3584]{2,1,0:T(8,128)(2,1)} %copy-done.2), kind=kOutput, calls=%fused_computation | convolution fusion | flops 1410662400 | bytes 6815744 | tf_op jit(solution)/shard_map/dot_general | solution.py:53
  104.3 2.4 %fusion.4 = bf16[32,8,3584]{2,1,0:T(8,128)(2,1)S(1)} fusion(f32[512,3584]{1,0:T(8,128)} %copy-done.1, bf16[32,8,3584]{2,1,0:T(8,128)(2,1)S(1)} %collective-permute-done.1), kind=kLoop, calls=%fused_computation.11 | loop fusion | flops 2752512 | bytes 7340032 | tf_op jit(solution)/shard_map/convert_element_type | solution.py:89
  106.8 47.8 %all_to_all.10 = bf16[32,8,3584]{2,1,0:T(8,128)(2,1)S(1)} all-to-all(bf16[32,8,3584]{2,1,0:T(8,128)(2,1)S(1)} %fusion.4), channel_id=1, replica_groups=mesh['dp'=8,'ex'=4,'ez'=8,'ec'=2] {'ex','ez'}, dimensions={0} | all-to-all | bytes 3670016 | tf_op jit(solution)/shard_map/all_to_all | solution.py:90
  154.6 0.2 bitcast_reduce_fusion
  154.8 0.1 copy.48
  155.0 1.9 %fusion.1 = bf16[128,3584]{1,0:T(8,128)(2,1)} fusion(bf16[4,2,4,3584]{3,0,2,1:T(4,128)(2,1)S(1)} %bitcast.82, s32[128,4]{0,1:T(4,128)S(1)} %copy.42, pred[128,4]{0,1:T(4,128)(4,1)S(1)} %fusion.12), kind=kOutput, calls=%fused_computation.4 | convolution fusion | flops 88545280 | bytes 1034752 | tf_op jit(solution)/shard_map/tec,ecf->tf/dot_general | solution.py:96
  156.9 1.9 %fusion = bf16[128,3584]{1,0:T(8,128)(2,1)} fusion(bf16[4,2,4,3584]{3,0,2,1:T(4,128)(2,1)S(1)} %bitcast.83, f32[4,4]{0,1:T(4,128)S(1)} %get-tuple-element.14, s32[128,4]{0,1:T(4,128)S(1)} %copy.42, pred[128,4]{0,1:T(4,128)(4,1)S(1)} %fusion.12), kind=kOutput, calls=%fused_computation.3 | convolution fusion | flops 88547328 | bytes 1036800 | tf_op jit(solution)/shard_map/tec,ecf->tf/dot_general | solution.py:95
  158.8 1.0 convert_element_type.71
  159.8 0.9 slice_bitcast_fusion.1
  (31 shorter events, 1.0 us)
Async XLA Ops:
  7.2 2.1 %copy-start = (bf16[128,3584]{1,0:T(8,128)(2,1)S(1)}, bf16[128,3584]{1,0:T(8,128)(2,1)}, u32[]{:S(2)}) copy-start(bf16[128,3584]{1,0:T(8,128)(2,1)} %param.7) | copy-start | bytes 2752516
  11.0 15.2 %copy-start.3 = (bf16[1,448,128]{2,1,0:T(8,128)(2,1)S(1)}, bf16[1,448,128]{2,1,0:T(8,128)(2,1)}, u32[]{:S(2)}) copy-start(bf16[1,448,128]{2,1,0:T(8,128)(2,1)} %param.13) | copy-start | bytes 344068
  11.1 15.2 %copy-start.4 = (bf16[1,448,128]{2,1,0:T(8,128)(2,1)S(1)}, bf16[1,448,128]{2,1,0:T(8,128)(2,1)}, u32[]{:S(2)}) copy-start(bf16[1,448,128]{2,1,0:T(8,128)(2,1)} %param.12) | copy-start | bytes 344068
  11.1 15.2 %copy-start.5 = (bf16[1,448,128]{2,1,0:T(8,128)(2,1)S(1)}, bf16[1,448,128]{2,1,0:T(8,128)(2,1)}, u32[]{:S(2)}) copy-start(bf16[1,448,128]{2,1,0:T(8,128)(2,1)} %param.11) | copy-start | bytes 344068
  12.5 57.1 %all-to-all-start = ((bf16[32,8,3584]{2,1,0:T(8,128)(2,1)}), bf16[32,8,3584]{2,1,0:T(8,128)(2,1)S(1)}, u32[]{:S(2)}, u32[]{:S(2)}) async-start(bf16[32,8,3584]{2,1,0:T(8,128)(2,1)} %bitcast.80), calls=%async_computation | async-start | bytes 3670016 | tf_op jit(solution)/shard_map/all_to_all | solution.py:77
  26.2 55.8 %all-gather.3.cloned.1.call-start = ((), (), s32[]{:S(2)}) async-start(), calls=%async_computation.4 | async-start | bytes 3096576 | tf_op jit(solution)/shard_map/all_gather | solution.py:73
  27.1 131.7 %reduce-scatter.2.cloned.1.call-start = ((), (), s32[]{:S(2)}) async-start(), calls=%async_computation.3 | async-start | bytes 3096576 | tf_op jit(solution)/shard_map/reduce_scatter | solution.py:81
  69.6 7.5 %collective-permute-start = (bf16[32,8,3584]{2,1,0:T(8,128)(2,1)S(1)}, bf16[32,8,3584]{2,1,0:T(8,128)(2,1)S(1)}, u32[]{:S(2)}, u32[]{:S(2)}) collective-permute-start(bf16[32,8,3584]{2,1,0:T(8,128)(2,1)S(1)} %all-to-all-done), channel_id=1, source_target_pairs={{0,1},{1,0},{2,3},{3,2},{4,5},{5,4},{6,7},{7,6},{8,9},{9,8},{10,11... | collective-permute-start | bytes 5505032 | tf_op jit(solution)/shard_map/ppermute | solution.py:78
  77.3 1.9 %copy-start.2 = (bf16[64,8,3584]{2,1,0:T(8,128)(2,1)}, bf16[64,8,3584]{2,1,0:T(8,128)(2,1)S(1)}, u32[]{:S(2)}) copy-start(bf16[64,8,3584]{2,1,0:T(8,128)(2,1)S(1)} %constant_dynamic-update-slice_fusion) | copy-start | bytes 11010052
  91.5 3.0 %copy-start.1 = (f32[512,3584]{1,0:T(8,128)}, f32[512,3584]{1,0:T(8,128)S(1)}, u32[]{:S(2)}) copy-start(f32[512,3584]{1,0:T(8,128)S(1)} %fusion.29) | copy-start | bytes 22020100
  95.8 8.5 %collective-permute-start.1 = (bf16[32,8,3584]{2,1,0:T(8,128)(2,1)}, bf16[32,8,3584]{2,1,0:T(8,128)(2,1)S(1)}, u32[]{:S(2)}, u32[]{:S(2)}) collective-permute-start(bf16[32,8,3584]{2,1,0:T(8,128)(2,1)} %fusion.8), channel_id=1, source_target_pairs={{0,1},{1,0},{2,3},{3,2},{4,5},{5,4},{6,7},{7,6},{8,9},{9,8},{10,11... | collective-permute-start | bytes 5505032 | tf_op jit(solution)/shard_map/ppermute | solution.py:88
Sparse Core Ops, SparseCore 0:
  29.7 44.7 all-gather.2
  104.5 40.3 reduce-scatter.1

commit v9 on v8

--- a/solution.py
+++ b/solution.py
@@ -25,18 +25,20 @@
     return (select, slot_gate)
 
 
-def expert_math(rows, w_all, hid):
+def expert_math(mine, partner, w_all, hid):
     f32 = jnp.float32
     bf16 = jnp.bfloat16
     nt = (((1,), (1,)), ((), ()))
     tn = (((0,), (0,)), ((), ()))
-    n = rows.shape[0]
-    flat = rows.reshape(-1, rows.shape[-1])
-    pre = jnp.dot(flat, w_all, preferred_element_type=f32)
-    pre = pre.reshape(n, 2, -1, 3 * hid)
-    gate_pre = pre[:, 0, :, :hid]
-    up_pre = pre[:, 0, :, hid : 2 * hid]
-    d_hidden = pre[:, 1, :, 2 * hid :]
+    n = mine.shape[0]
+    flat_m = mine.reshape(-1, mine.shape[-1])
+    flat_p = partner.reshape(-1, partner.shape[-1])
+    pre_m = jnp.dot(flat_m, w_all, preferred_element_type=f32)
+    pre_p = jnp.dot(flat_p, w_all, preferred_element_type=f32)
+    pre = jnp.stack([pre_m, pre_p], axis=0).reshape(2, n, 2, -1, 3 * hid)
+    gate_pre = pre[:, :, 0, :, :hid]
+    up_pre = pre[:, :, 0, :, hid : 2 * hid]
+    d_hidden = pre[:, :, 1, :, 2 * hid :]
     sig = jax.nn.sigmoid(gate_pre)
     act = gate_pre * sig
     hidden = (act * up_pre).astype(bf16)
@@ -45,14 +47,14 @@
     zero = jnp.zeros_like(hidden)
     tok_side = jnp.concatenate([d_gate, d_up, zero], axis=-1)
     cot_side = jnp.concatenate([zero, zero, hidden], axis=-1)
-    grad_side = jnp.stack([tok_side, cot_side], axis=1).reshape(-1, 3 * hid)
-    out_side = jnp.stack(
-        [jnp.concatenate([zero, zero, hidden], axis=-1), jnp.concatenate([d_gate, d_up, zero], axis=-1)],
-        axis=1,
-    ).reshape(-1, 3 * hid)
-    term = lax.dot_general(flat, grad_side, tn, preferred_element_type=f32)
-    results = lax.dot_general(out_side, w_all, nt, preferred_element_type=f32)
-    return results, term
+    grad_side = jnp.stack([tok_side, cot_side], axis=2).reshape(2, -1, 3 * hid)
+    out_side = jnp.stack([cot_side, tok_side], axis=2).reshape(2, -1, 3 * hid)
+    res_p = lax.dot_general(out_side[1], w_all, nt, preferred_element_type=f32)
+    res_m = lax.dot_general(out_side[0], w_all, nt, preferred_element_type=f32)
+    term = lax.dot_general(flat_m, grad_side[0], tn, preferred_element_type=f32) + lax.dot_general(
+        flat_p, grad_side[1], tn, preferred_element_type=f32
+    )
+    return res_m, res_p, term
 
 
 def per_device(tokens, out_cotangent, expert_ids, gate_fixed, w_gate, w_up, w_down):
@@ -76,17 +78,15 @@
     )
     mine = lax.all_to_all(outgoing, ("ex", "ez"), split_axis=0, concat_axis=0, tiled=True)
     partner = lax.ppermute(mine, "ec", [(0, 1), (1, 0)])
-    arrived = jnp.concatenate([mine, partner], axis=0)
-    results, term = expert_math(arrived, w_all, hid)
+    res_m, res_p, term = expert_math(mine, partner, w_all, hid)
     summed = lax.psum_scatter(
         term.astype(jnp.bfloat16), "dp", scatter_dimension=0, tiled=True
     ).astype(f32)
     grad_gate = summed[:, :hid][None]
     grad_up = summed[:, hid : 2 * hid][None]
     grad_down = summed[:, 2 * hid :][None]
-    halves = results.reshape(2, window * zsize, 2 * CAP, width)
-    back = lax.ppermute(halves[1].astype(jnp.bfloat16), "ec", [(0, 1), (1, 0)])
-    pair = (halves[0] + back.astype(f32)).astype(jnp.bfloat16)
+    back = lax.ppermute(res_p.astype(jnp.bfloat16), "ec", [(0, 1), (1, 0)])
+    pair = (res_m + back.astype(f32)).astype(jnp.bfloat16).reshape(window * zsize, 2 * CAP, width)
     returned = lax.all_to_all(pair, ("ex", "ez"), split_axis=0, concat_axis=0, tiled=True)
     combined = jnp.sum(
         returned.reshape(window, zsize, 2 * CAP, width).astype(f32), axis=1

time: 170 us -> 170 us (level)
  blocking collectives: 47.8 us -> 52.6 us
  waiting for transfers between devices: 45.7 us -> 42.5 us
  local copies, waits for them, and re-layouts: 12.8 us -> 9.61 us
  matrix products: 20.1 us -> 23.1 us
  other arithmetic: 6.63 us -> 4.26 us
  starting transfers between devices: 20.2 us -> 22 us
    unnamed x13 -> x12, local copies, waits for them, and re-layouts: 4.99 us -> 0.15 us
    all_to_all x1, blocking collectives: 47.8 us -> 52.6 us  [per_device(): lax.all_to_all(pair, ('ex', 'ez'), split_axis=0, concat_axis=0, tiled=True)]
    ppermute x1, waiting for transfers between devices: 3.24 us -> 0.01 us  [per_device(): partner = lax.ppermute(mine, 'ec', [(0, 1), (1, 0)])]
    dot_general x3 -> x6, matrix products: 14.6 us -> 17.6 us  [the longest x1 4.23 us: expert_math(): lax.dot_general(flat_p, grad_side[1], tn, preferred_element_type=f32)]
    concatenate x3 -> x1, local copies, waits for them, and re-layouts: 2.98 us -> 0.01 us  [expert_math(): tok_side = jnp.concatenate([d_gate, d_up, zero], axis=-1)]
    convert_element_type x2, other arithmetic: 2.53 us -> 0.16 us  [the longest x1 0.1 us: expert_math(): (d_hidden * up_pre * sig * (1.0 + gate_pre * (1.0 - sig))).astype(bf16)]
    ppermute x0 -> x1, local copies, waits for them, and re-layouts: none -> 2.19 us  [per_device(): partner = lax.ppermute(mine, 'ec', [(0, 1), (1, 0)])]
    squeeze x0 -> x4, local copies, waits for them, and re-layouts: none -> 1.81 us  [the longest x1 0.98 us: expert_math(): res_p = lax.dot_general(out_side[1], w_all, nt, preferred_element_type=f32)]
  transfers between devices with their start and end apart: 5 -> 5, of which waited for: 2 -> 1; matrix products, arithmetic and copies ran while one was open for 10% -> 12% of each run, Pallas kernels for 0% -> 0%
where the time goes in v9:
time: 170 us; the launch traced here: 168 us
  blocking collectives  52.6 us (31%)
  waiting for transfers between devices  42.5 us (25%)
  matrix products  23.1 us (14%)
  starting transfers between devices  22 us (13%)
  between operations  14.3 us (8%)
  local copies, waits for them, and re-layouts  9.61 us (6%)
  other arithmetic  4.26 us (3%)
    all_to_all x1, blocking collectives, per_device(): lax.all_to_all(pair, ('ex', 'ez'), split_axis=0, concat_axis=0, tiled=True)  52.6 us
    all_to_all x1, waiting for transfers between devices, per_device(): lax.all_to_all(outgoing, ('ex', 'ez'), split_axis=0, concat_axis=0, tiled...  42.5 us
    all_to_all x1, starting transfers between devices, per_device(): lax.all_to_all(outgoing, ('ex', 'ez'), split_axis=0, concat_axis=0, tiled...  13.8 us
    dot_general x1, matrix products, expert_math(): lax.dot_general(flat_p, grad_side[1], tn, preferred_element_type=f32)  4.23 us
    dot_general x1, matrix products, expert_math(): res_p = lax.dot_general(out_side[1], w_all, nt, preferred_element_type=f32)  4.17 us
    ppermute x1, starting transfers between devices, per_device(): partner = lax.ppermute(mine, 'ec', [(0, 1), (1, 0)])  4.14 us
    ppermute x1, starting transfers between devices, per_device(): back = lax.ppermute(res_p.astype(jnp.bfloat16), 'ec', [(0, 1), (1, 0)])  3.93 us
    dot_general x1, matrix products, expert_math(): res_m = lax.dot_general(out_side[0], w_all, nt, preferred_element_type=f32)  3.48 us
  transfers between devices with their start and end apart: 5, of which 1 were waited for; matrix products, arithmetic and copies ran while one was open for 12% of the time, Pallas kernels for 0%

profile of v9, /device:TPU:1, one launch (start us, length us, event | category | flops | bytes accessed | tf_op | source)
XLA Modules:
  0.0 168.3 jit_solution(13916053744409261873)
XLA Ops:
  7.2 0.8 fusion.24
  8.0 0.7 select_reduce_fusion
  8.7 0.1 copy.53
  8.8 0.2 reduce_window_sum.11
  9.3 0.2 convolution_convert_fusion.1
  9.5 1.4 fusion.3
  10.9 0.1 pad_maximum_fusion.1
  11.0 1.4 broadcast_in_dim.51
  12.4 13.8 %all-to-all-start = ((bf16[32,8,3584]{2,1,0:T(8,128)(2,1)}), bf16[32,8,3584]{2,1,0:T(8,128)(2,1)S(1)}, u32[]{:S(2)}, u32[]{:S(2)}) async-start(bf16[32,8,3584]{2,1,0:T(8,128)(2,1)} %bitcast.83), calls=%async_computation | async-start | bytes 3670016 | tf_op jit(solution)/shard_map/all_to_all | solution.py:79
  26.3 0.8 pad_maximum_fusion
  27.2 42.5 %all-to-all-done = bf16[32,8,3584]{2,1,0:T(8,128)(2,1)S(1)} async-done(((bf16[32,8,3584]{2,1,0:T(8,128)(2,1)}), bf16[32,8,3584]{2,1,0:T(8,128)(2,1)S(1)}, u32[]{:S(2)}, u32[]{:S(2)}) %all-to-all-start) | async-done | bytes 1835040 | tf_op jit(solution)/shard_map/all_to_all | solution.py:79
  69.7 4.1 %collective-permute-start = (bf16[32,8,3584]{2,1,0:T(8,128)(2,1)S(1)}, bf16[32,8,3584]{2,1,0:T(8,128)(2,1)}, u32[]{:S(2)}, u32[]{:S(2)}) collective-permute-start(bf16[32,8,3584]{2,1,0:T(8,128)(2,1)S(1)} %all-to-all-done), channel_id=1, source_target_pairs={{0,1},{1,0},{2,3},{3,2},{4,5},{5,4},{6,7},{7,6},{8,9},{9,8},{10,11... | collective-permute-start | bytes 5505032 | tf_op jit(solution)/shard_map/ppermute | solution.py:80
  73.8 1.8 %copy.58 = bf16[32,8,3584]{2,0,1:T(8,128)(2,1)} copy(bf16[32,8,3584]{2,1,0:T(8,128)(2,1)S(1)} %all-to-all-done) | data formatting | bytes 3670016 | tf_op jit(solution)/shard_map/all_to_all | solution.py:79
  75.6 3.5 %fusion.12 = f32[1,32,2,4,384]{4,1,3,2,0:T(8,128)S(1)} fusion(bf16[32,2,4,3584]{3,0,2,1:T(8,128)(2,1)} %bitcast.84, bf16[3584,384]{1,0:T(8,128)(2,1)} %all-gather.3.cloned.1.call-done), kind=kOutput, calls=%fused_computation.20 | convolution fusion | flops 704643072 | bytes 4980736 | tf_op jit(solution)/shard_map/dot_general | solution.py:36
  79.1 2.2 %copy.59 = bf16[32,8,3584]{2,0,1:T(8,128)(2,1)S(1)} copy(bf16[32,8,3584]{2,1,0:T(8,128)(2,1)} %collective-permute-done) | data formatting | bytes 3670016 | tf_op jit(solution)/shard_map/ppermute | solution.py:80
  81.3 0.1 copy-done.1
  81.4 1.1 fusion.15
  82.8 0.8 copy.63
  83.6 1.0 squeeze.43
  84.6 4.2 %convolution_convert_fusion = bf16[256,3584]{1,0:T(8,128)(2,1)} fusion(bf16[256,384]{1,0:T(8,128)(2,1)S(1)} %squeeze.43, bf16[3584,384]{1,0:T(8,128)(2,1)} %all-gather.3.cloned.1.call-done), kind=kOutput, calls=%fused_computation.2 | convolution fusion | flops 705560576 | bytes 4784128 | tf_op jit(solution)/shard_map/dot_general | solution.py:52
  88.8 3.9 %collective-permute-start.1 = (bf16[256,3584]{1,0:T(8,128)(2,1)}, bf16[256,3584]{1,0:T(8,128)(2,1)}, u32[]{:S(2)}, u32[]{:S(2)}) collective-permute-start(bf16[256,3584]{1,0:T(8,128)(2,1)} %convolution_convert_fusion), channel_id=1, source_target_pairs={{0,1},{1,0},{2,3},{3,2},{4,5},{5,4},{6,7},{7,6},{8,9},{9,8},{10,11... | collective-permute-start | bytes 5505032 | tf_op jit(solution)/shard_map/ppermute | solution.py:88
  92.8 0.7 squeeze.47
  93.7 1.1 fusion.10
  94.9 4.2 %fusion = bf16[3584,384]{1,0:T(8,128)(2,1)} fusion(f32[3584,384]{1,0:T(8,128)S(1)} %fusion.10, bf16[256,384]{1,0:T(8,128)(2,1)S(1)} %copy-done.2, bf16[32,8,3584]{2,1,0:T(8,128)(2,1)} %collective-permute-done), kind=kOutput, calls=%fused_computation.1 | convolution fusion | flops 707395584 | bytes 10289152 | tf_op jit(solution)/shard_map/dot_general | solution.py:54
  99.3 3.5 %fusion.8 = bf16[32,8,3584]{2,1,0:T(8,128)(2,1)S(1)} fusion(bf16[256,3584]{1,0:T(8,128)(2,1)} %collective-permute-done.1, bf16[256,384]{1,0:T(8,128)(2,1)S(1)} %squeeze.42, bf16[3584,384]{1,0:T(8,128)(2,1)} %all-gather.3.cloned.1.call-done), kind=kOutput, calls=%fused_computation.15 | convolution fusion | flops 707395584 | bytes 6619136 | tf_op jit(solution)/shard_map/dot_general | solution.py:53
  102.8 52.6 %all_to_all.10 = bf16[32,8,3584]{2,1,0:T(8,128)(2,1)S(1)} all-to-all(bf16[32,8,3584]{2,1,0:T(8,128)(2,1)S(1)} %fusion.8), channel_id=1, replica_groups=mesh['dp'=8,'ex'=4,'ez'=8,'ec'=2] {'ex','ez'}, dimensions={0} | all-to-all | bytes 3670016 | tf_op jit(solution)/shard_map/all_to_all | solution.py:90
  155.4 0.2 bitcast_reduce_fusion
  155.6 0.1 copy.64
  155.8 1.9 %fusion.2 = bf16[128,3584]{1,0:T(8,128)(2,1)} fusion(bf16[4,2,4,3584]{3,0,2,1:T(4,128)(2,1)S(1)} %bitcast.86, s32[128,4]{0,1:T(4,128)S(1)} %copy.54, pred[128,4]{0,1:T(4,128)(4,1)S(1)} %fusion.24), kind=kOutput, calls=%fused_computation.6 | convolution fusion | flops 88545280 | bytes 1034752 | tf_op jit(solution)/shard_map/tec,ecf->tf/dot_general | solution.py:96
  157.7 1.9 %fusion.1 = bf16[128,3584]{1,0:T(8,128)(2,1)} fusion(bf16[4,2,4,3584]{3,0,2,1:T(4,128)(2,1)S(1)} %bitcast.87, f32[4,4]{0,1:T(4,128)S(1)} %get-tuple-element.19, s32[128,4]{0,1:T(4,128)S(1)} %copy.54, pred[128,4]{0,1:T(4,128)(4,1)S(1)} %fusion.24), kind=kOutput, calls=%fused_computation.5 | convolution fusion | flops 88547328 | bytes 1036800 | tf_op jit(solution)/shard_map/tec,ecf->tf/dot_general | solution.py:95
  159.6 1.0 convert_element_type.70
  160.6 0.9 slice_bitcast_fusion
  (36 shorter events, 1.2 us)
Async XLA Ops:
  7.2 2.1 %copy-start = (bf16[128,3584]{1,0:T(8,128)(2,1)S(1)}, bf16[128,3584]{1,0:T(8,128)(2,1)}, u32[]{:S(2)}) copy-start(bf16[128,3584]{1,0:T(8,128)(2,1)} %param.7) | copy-start | bytes 2752516
  12.4 13.9 %copy-start.3 = (bf16[1,448,128]{2,1,0:T(8,128)(2,1)S(1)}, bf16[1,448,128]{2,1,0:T(8,128)(2,1)}, u32[]{:S(2)}) copy-start(bf16[1,448,128]{2,1,0:T(8,128)(2,1)} %param.13) | copy-start | bytes 344068
  12.4 13.9 %copy-start.4 = (bf16[1,448,128]{2,1,0:T(8,128)(2,1)S(1)}, bf16[1,448,128]{2,1,0:T(8,128)(2,1)}, u32[]{:S(2)}) copy-start(bf16[1,448,128]{2,1,0:T(8,128)(2,1)} %param.12) | copy-start | bytes 344068
  12.4 13.9 %copy-start.5 = (bf16[1,448,128]{2,1,0:T(8,128)(2,1)S(1)}, bf16[1,448,128]{2,1,0:T(8,128)(2,1)}, u32[]{:S(2)}) copy-start(bf16[1,448,128]{2,1,0:T(8,128)(2,1)} %param.11) | copy-start | bytes 344068
  12.4 57.3 %all-to-all-start = ((bf16[32,8,3584]{2,1,0:T(8,128)(2,1)}), bf16[32,8,3584]{2,1,0:T(8,128)(2,1)S(1)}, u32[]{:S(2)}, u32[]{:S(2)}) async-start(bf16[32,8,3584]{2,1,0:T(8,128)(2,1)} %bitcast.83), calls=%async_computation | async-start | bytes 3670016 | tf_op jit(solution)/shard_map/all_to_all | solution.py:79
  26.3 49.3 %all-gather.3.cloned.1.call-start = ((), (), s32[]{:S(2)}) async-start(), calls=%async_computation.4 | async-start | bytes 3096576 | tf_op jit(solution)/shard_map/all_gather | solution.py:75
  27.1 132.5 %reduce-scatter.2.cloned.1.call-start = ((), (), s32[]{:S(2)}) async-start(), calls=%async_computation.3 | async-start | bytes 3096576 | tf_op jit(solution)/shard_map/reduce_scatter | solution.py:82
  69.7 9.4 %collective-permute-start = (bf16[32,8,3584]{2,1,0:T(8,128)(2,1)S(1)}, bf16[32,8,3584]{2,1,0:T(8,128)(2,1)}, u32[]{:S(2)}, u32[]{:S(2)}) collective-permute-start(bf16[32,8,3584]{2,1,0:T(8,128)(2,1)S(1)} %all-to-all-done), channel_id=1, source_target_pairs={{0,1},{1,0},{2,3},{3,2},{4,5},{5,4},{6,7},{7,6},{8,9},{9,8},{10,11... | collective-permute-start | bytes 5505032 | tf_op jit(solution)/shard_map/ppermute | solution.py:80
  79.1 2.3 %copy-start.1 = (bf16[3584,384]{1,0:T(8,128)(2,1)S(1)}, bf16[3584,384]{1,0:T(8,128)(2,1)}, u32[]{:S(2)}) copy-start(bf16[3584,384]{1,0:T(8,128)(2,1)} %all-gather.3.cloned.1.call-done) | copy-start | bytes 8257540
  88.8 10.5 %collective-permute-start.1 = (bf16[256,3584]{1,0:T(8,128)(2,1)}, bf16[256,3584]{1,0:T(8,128)(2,1)}, u32[]{:S(2)}, u32[]{:S(2)}) collective-permute-start(bf16[256,3584]{1,0:T(8,128)(2,1)} %convolution_convert_fusion), channel_id=1, source_target_pairs={{0,1},{1,0},{2,3},{3,2},{4,5},{5,4},{6,7},{7,6},{8,9},{9,8},{10,11... | collective-permute-start | bytes 5505032 | tf_op jit(solution)/shard_map/ppermute | solution.py:88
  93.7 1.2 copy-start.2
Sparse Core Ops, SparseCore 0:
  29.8 44.7 all-gather.2
  99.3 41.7 reduce-scatter.1

commit v10 on v9

v10 whole, which is shorter than its diff:
```python
import jax
import jax.numpy as jnp
from jax import lax
from jax.sharding import Mesh
from jax.sharding import PartitionSpec as P

SPLIT = 16
CAP = 4


SCALE = 2.0 ** (-16)
HIGH = lax.Precision.HIGHEST


def routing(ids, gates, window, capacity):
    wanted = jnp.arange(window, dtype=jnp.int32)
    hits = ids[:, :, None] == wanted[None, None, :]
    member = jnp.any(hits, axis=1)
    weight = jnp.sum(jnp.where(hits, gates[:, :, None], 0), axis=1).astype(jnp.float32) * SCALE
    rank = jnp.cumsum(member.astype(jnp.int32), axis=0) - 1
    slots = jnp.arange(capacity, dtype=jnp.int32)
    pick = jnp.logical_and(member[:, :, None], rank[:, :, None] == slots[None, None, :])
    select = jnp.where(pick, 1.0, 0.0).astype(jnp.float32)
    slot_gate = jnp.sum(select * weight[:, :, None], axis=0)
    return (select, slot_gate)


def expert_math(mine, w_two, hid):
    f32 = jnp.float32
    bf16 = jnp.bfloat16
    nt = (((1,), (1,)), ((), ()))
    tn = (((0,), (0,)), ((), ()))
    n = mine.shape[0]
    flat = mine.reshape(-1, mine.shape[-1])
    pre = jnp.dot(flat, w_two, preferred_element_type=f32).reshape(n, 2, -1, 2, 3 * hid)
    gate_pre = pre[:, 0, :, :, :hid]
    up_pre = pre[:, 0, :, :, hid : 2 * hid]
    d_hidden = pre[:, 1, :, :, 2 * hid :]
    sig = jax.nn.sigmoid(gate_pre)
    act = gate_pre * sig
    hidden = (act * up_pre).astype(bf16)
    d_gate = (d_hidden * up_pre * sig * (1.0 + gate_pre * (1.0 - sig))).astype(bf16)
    d_up = (d_hidden * act).astype(bf16)
    zero = jnp.zeros_like(hidden)
    tok_side = jnp.concatenate([d_gate, d_up, zero], axis=-1)
    cot_side = jnp.concatenate([zero, zero, hidden], axis=-1)
    grad_side = jnp.stack([tok_side, cot_side], axis=1).reshape(-1, 2 * 3 * hid)
    out_side = jnp.stack([cot_side, tok_side], axis=1).reshape(-1, 2 * 3 * hid)
    results = lax.dot_general(out_side, w_two, nt, preferred_element_type=f32)
    term = lax.dot_general(flat, grad_side, tn, preferred_element_type=f32)
    return results, term.reshape(term.shape[0], 2, 3 * hid)


def per_device(tokens, out_cotangent, expert_ids, gate_fixed, w_gate, w_up, w_down):
    window = lax.axis_size("ex")
    zsize = lax.axis_size("ez")
    hid = w_gate.shape[2]
    f32 = jnp.float32
    core = lax.axis_index("ec")
    swap = [(0, 1), (1, 0)]
    w_loc = jnp.concatenate([w_gate[0], w_up[0], w_down[0]], axis=1)
    w_all = lax.all_gather(w_loc, "dp", axis=0, tiled=False).reshape(-1, 3 * hid)
    w_other = lax.ppermute(w_all, "ec", swap)
    w_pair = jnp.stack([w_all, w_other], axis=1)
    w_pair = jnp.where(core == 0, w_pair, w_pair[:, ::-1])
    w_two = w_pair.reshape(-1, 2 * 3 * hid)
    select, slot_gate = routing(expert_ids, gate_fixed, window, CAP)
    select_b = select.astype(jnp.bfloat16)
    slot_tokens = jnp.einsum("tec,tf->ecf", select_b, tokens, preferred_element_type=f32).astype(
        jnp.bfloat16
    )
    picked = jnp.einsum("tec,tf->ecf", select_b, out_cotangent, preferred_element_type=f32)
    slot_cot = (picked * slot_gate[:, :, None]).astype(jnp.bfloat16)
    payload = jnp.concatenate([slot_tokens, slot_cot], axis=1)
    width = payload.shape[-1]
    outgoing = jnp.broadcast_to(payload[:, None], (window, zsize, 2 * CAP, width)).reshape(
        window * zsize, 2 * CAP, width
    )
    mine = lax.all_to_all(outgoing, ("ex", "ez"), split_axis=0, concat_axis=0, tiled=True)
    results, term = expert_math(mine, w_two, hid)
    own = jnp.where(core == 0, term[:, 0], term[:, 1])
    other = jnp.where(core == 0, term[:, 1], term[:, 0])
    got = lax.ppermute(other.astype(jnp.bfloat16), "ec", swap)
    chip_term = own + got.astype(f32)
    summed = lax.psum_scatter(
        chip_term.astype(jnp.bfloat16), "dp", scatter_dimension=0, tiled=True
    ).astype(f32)
    grad_gate = summed[:, :hid][None]
    grad_up = summed[:, hid : 2 * hid][None]
    grad_down = summed[:, 2 * hid :][None]
    pair = results.astype(jnp.bfloat16).reshape(window * zsize, 2 * CAP, width)
    returned = lax.all_to_all(pair, ("ex", "ez"), split_axis=0, concat_axis=0, tiled=True)
    combined = jnp.sum(
        returned.reshape(window, zsize, 2 * CAP, width).astype(f32), axis=1
    ).astype(jnp.bfloat16).reshape(window, 2, CAP, width)
    weighted = select * slot_gate[None, :, :]
    layer_out = jnp.einsum("tec,ecf->tf", weighted, combined[:, 0].astype(f32), precision=HIGH)
    token_grad = jnp.einsum("tec,ecf->tf", select_b, combined[:, 1], preferred_element_type=f32)
    return (
        layer_out.astype(jnp.bfloat16),
        token_grad.astype(jnp.bfloat16),
        grad_gate,
        grad_up,
        grad_down,
    )


def solution(mesh):
    n_dp = mesh.shape["dp"]
    n_exp = mesh.shape["expert"]
    devices = mesh.devices.reshape(n_dp, n_exp // SPLIT, SPLIT // 2, 2)
    grid = Mesh(devices, ("dp", "ex", "ez", "ec"))
    tok = P(("dp", "ex", "ez", "ec"), None)
    wsp = P(("ex", "ez", "ec"), "dp", None)
    return jax.shard_map(
        per_device,
        mesh=grid,
        in_specs=(tok, tok, tok, tok, wsp, wsp, wsp),
        out_specs=(tok, tok, wsp, wsp, wsp),
        check_vma=False,
    )
```

time: 170 us -> 165 us (0.971)
  the two profiles are of different devices: /device:TPU:1 before, /device:TPU:8 now
where the time goes in v10:
time: 165 us
  blocking collectives  54.1 us (33%)
  waiting for transfers between devices  43.2 us (26%)
  starting transfers between devices  17.1 us (10%)
  between operations  14.2 us (9%)
  matrix products  12.4 us (8%)
  other arithmetic  12.2 us (7%)
  local copies, waits for them, and re-layouts  11.6 us (7%)
    all_to_all x1, blocking collectives, per_device(): lax.all_to_all(pair, ('ex', 'ez'), split_axis=0, concat_axis=0, tiled=True)  54.1 us
    all_gather x1, waiting for transfers between devices, per_device(): lax.all_gather(w_loc, 'dp', axis=0, tiled=False).reshape(-1, 3 * hid)  33.3 us
    all_to_all x1, starting transfers between devices, per_device(): lax.all_to_all(outgoing, ('ex', 'ez'), split_axis=0, concat_axis=0, tiled...  13.2 us
    ppermute x1, waiting for transfers between devices, per_device(): got = lax.ppermute(other.astype(jnp.bfloat16), 'ec', swap)  5.06 us
    all_to_all x1, waiting for transfers between devices, per_device(): lax.all_to_all(outgoing, ('ex', 'ez'), split_axis=0, concat_axis=0, tiled...  4.85 us
    all_gather x1, local copies, waits for them, and re-layouts, per_device(): lax.all_gather(w_loc, 'dp', axis=0, tiled=False).reshape(-1, 3 * hid)  4.57 us
    dot_general x1, matrix products, expert_math(): results = lax.dot_general(out_side, w_two, nt, preferred_element_type=f32)  4.15 us
  transfers between devices with their start and end apart: 5, of which 3 were waited for; matrix products, arithmetic and copies ran while one was open for 11% of the time, Pallas kernels for 0%

profile of v10, /device:TPU:8, one launch (start us, length us, event | category | flops | bytes accessed | tf_op | source)
XLA Modules:
  0.0 164.8 jit_solution(5300833779511031895)
XLA Ops:
  7.2 1.9 %pad_maximum_fusion.3 = bf16[448,384]{1,0:T(8,128)(2,1)} fusion(bf16[448,128]{1,0:T(8,128)(2,1)} %bitcast.114, bf16[448,128]{1,0:T(8,128)(2,1)} %bitcast.115, bf16[448,128]{1,0:T(8,128)(2,1)} %bitcast.116), kind=kLoop, calls=%fused_computation.24 | loop fusion | flops 1032192 | bytes 688128 | tf_op jit(solution)/shard_map/concatenate | solution.py:61
  9.1 0.7 fusion.13
  10.2 0.7 select_reduce_fusion
  11.4 1.4 fusion.6
  12.9 1.4 broadcast_in_dim.51
  14.3 13.2 %all-to-all-start = ((bf16[32,8,3584]{2,1,0:T(8,128)(2,1)}), bf16[32,8,3584]{2,1,0:T(8,128)(2,1)S(1)}, u32[]{:S(2)}, u32[]{:S(2)}) async-start(bf16[32,8,3584]{2,1,0:T(8,128)(2,1)} %bitcast.104), calls=%async_computation | async-start | bytes 3670016 | tf_op jit(solution)/shard_map/all_to_all | solution.py:79
  27.5 33.3 %all-gather.3.cloned.1.call-done = bf16[3584,384]{1,0:T(8,128)(2,1)} async-done(((bf16[448,384]{1,0:T(8,128)(2,1)}), bf16[3584,384]{1,0:T(8,128)(2,1)}) %all-gather.3.cloned.1.call-update) | async-done | bytes 2752528 | tf_op jit(solution)/shard_map/all_gather | solution.py:62
  60.8 4.6 %copy.57 = bf16[3584,384]{0,1:T(8,128)(2,1)} copy(bf16[3584,384]{1,0:T(8,128)(2,1)} %all-gather.3.cloned.1.call-done) | data formatting | bytes 5505024 | tf_op jit(solution)/shard_map/all_gather | solution.py:62
  65.4 1.9 %collective-permute-start = (bf16[3584,384]{0,1:T(8,128)(2,1)}, bf16[3584,384]{0,1:T(8,128)(2,1)}, u32[]{:S(2)}, u32[]{:S(2)}) collective-permute-start(bf16[3584,384]{0,1:T(8,128)(2,1)} %copy.57), channel_id=1, source_target_pairs={{0,1},{1,0},{2,3},{3,2},{4,5},{5,4},{6,7},{7,6},{8,9},{9,8},{10,11... | collective-permute-start | bytes 8257544 | tf_op jit(solution)/shard_map/ppermute | solution.py:63
  67.3 4.8 %all-to-all-done = bf16[32,8,3584]{2,1,0:T(8,128)(2,1)S(1)} async-done(((bf16[32,8,3584]{2,1,0:T(8,128)(2,1)}), bf16[32,8,3584]{2,1,0:T(8,128)(2,1)S(1)}, u32[]{:S(2)}, u32[]{:S(2)}) %all-to-all-start) | async-done | bytes 1835040 | tf_op jit(solution)/shard_map/all_to_all | solution.py:79
  72.2 0.5 copy.56
  72.7 1.2 copy-done.1
  73.9 2.3 %pad_maximum_fusion = bf16[3584,2,384]{0,2,1:T(8,128)(2,1)S(1)} fusion(bf16[3584,1,384]{0,2,1:T(8,128)(2,1)} %bitcast.10, bf16[3584,1,384]{0,2,1:T(8,128)(2,1)S(1)} %bitcast.103), kind=kLoop, calls=%fused_computation.1 | loop fusion | flops 2752512 | bytes 11010048 | tf_op jit(solution)/shard_map/stack | solution.py:64
  76.2 1.1 reverse_select_fusion
  77.3 1.6 fusion
  78.9 0.8 copy-done.2
  79.8 0.8 pad_maximum_fusion.2
  80.6 0.3 copy.61
  81.2 1.6 fusion.8
  82.8 0.5 fusion.7
  83.3 1.9 %collective-permute-start.1 = (bf16[3584,384]{1,0:T(8,128)(2,1)S(1)}, bf16[3584,384]{1,0:T(8,128)(2,1)S(1)}, u32[]{:S(2)}, u32[]{:S(2)}) collective-permute-start(bf16[3584,384]{1,0:T(8,128)(2,1)S(1)} %fusion.7), channel_id=1, source_target_pairs={{0,1},{1,0},{2,3},{3,2},{4,5},{5,4},{6,7},{7,6},{8,9},{9,8},{10,11... | collective-permute-start | bytes 8257544 | tf_op jit(solution)/shard_map/ppermute | solution.py:83
  85.3 5.1 %collective-permute-done.1 = bf16[3584,384]{1,0:T(8,128)(2,1)S(1)} collective-permute-done((bf16[3584,384]{1,0:T(8,128)(2,1)S(1)}, bf16[3584,384]{1,0:T(8,128)(2,1)S(1)}, u32[]{:S(2)}, u32[]{:S(2)}) %collective-permute-start.1) | collective-permute-done | bytes 2752544 | tf_op jit(solution)/shard_map/ppermute | solution.py:83
  90.3 2.4 %fusion.2 = bf16[3584,384]{1,0:T(8,128)(2,1)} fusion(bf16[3584,384]{1,0:T(8,128)(2,1)S(1)} %collective-permute-done.1, f32[3584,2,384]{2,0,1:T(8,128)S(1)} %fusion.8, pred[]{:T(512)S(6)} %eq.37), kind=kLoop, calls=%fused_computation.5 | loop fusion | flops 5505024 | bytes 16515073 | tf_op jit(solution)/shard_map/convert_element_type | solution.py:86
  92.8 1.0 copy-done.3
  93.8 0.3 copy.59
  94.1 4.1 %fusion.3 = bf16[32,8,3584]{2,1,0:T(8,128)(2,1)S(1)} fusion(bf16[256,768]{1,0:T(8,128)(2,1)S(1)} %bitcast.111, bf16[3584,768]{0,1:T(8,128)(2,1)} %bitcast.105), kind=kOutput, calls=%fused_computation.8 | convolution fusion | flops 1410203648 | bytes 7733248 | tf_op jit(solution)/shard_map/dot_general | solution.py:49
  98.3 54.1 %all_to_all.10 = bf16[32,8,3584]{2,1,0:T(8,128)(2,1)S(1)} all-to-all(bf16[32,8,3584]{2,1,0:T(8,128)(2,1)S(1)} %fusion.3), channel_id=1, replica_groups=mesh['dp'=8,'ex'=4,'ez'=8,'ec'=2] {'ex','ez'}, dimensions={0} | all-to-all | bytes 3670016 | tf_op jit(solution)/shard_map/all_to_all | solution.py:92
  152.4 0.2 bitcast_reduce_fusion
  152.8 1.4 fusion.5
  154.2 1.9 %fusion.4 = bf16[128,3584]{1,0:T(8,128)(2,1)} fusion(bf16[4,2,4,3584]{3,0,2,1:T(4,128)(2,1)S(1)} %bitcast.113, f32[4,4]{0,1:T(4,128)S(1)} %get-tuple-element.14, s32[128,4]{0,1:T(4,128)S(1)} %copy.52, pred[128,4]{0,1:T(4,128)(4,1)S(1)} %fusion.13), kind=kOutput, calls=%fused_computation.11 | convolution fusion | flops 88547328 | bytes 1036800 | tf_op jit(solution)/shard_map/tec,ecf->tf/dot_general | solution.py:97
  156.1 1.0 convert_element_type.74
  157.1 0.9 slice_bitcast_fusion
  (29 shorter events, 1.6 us)
Async XLA Ops:
  7.2 4.0 %copy-start = (bf16[128,3584]{1,0:T(8,128)(2,1)S(1)}, bf16[128,3584]{1,0:T(8,128)(2,1)}, u32[]{:S(2)}) copy-start(bf16[128,3584]{1,0:T(8,128)(2,1)} %param.7) | copy-start | bytes 2752516
  7.2 53.6 %all-gather.3.cloned.1.call-start = ((), (), s32[]{:S(2)}) async-start(), calls=%async_computation.4 | async-start | bytes 3096576 | tf_op jit(solution)/shard_map/all_gather | solution.py:62
  14.3 57.9 %all-to-all-start = ((bf16[32,8,3584]{2,1,0:T(8,128)(2,1)}), bf16[32,8,3584]{2,1,0:T(8,128)(2,1)S(1)}, u32[]{:S(2)}, u32[]{:S(2)}) async-start(bf16[32,8,3584]{2,1,0:T(8,128)(2,1)} %bitcast.104), calls=%async_computation | async-start | bytes 3670016 | tf_op jit(solution)/shard_map/all_to_all | solution.py:79
  27.5 128.6 %reduce-scatter.2.cloned.1.call-start = ((), (), s32[]{:S(2)}) async-start(), calls=%async_computation.3 | async-start | bytes 3096576 | tf_op jit(solution)/shard_map/reduce_scatter | solution.py:85
  65.4 7.3 %collective-permute-start = (bf16[3584,384]{0,1:T(8,128)(2,1)}, bf16[3584,384]{0,1:T(8,128)(2,1)}, u32[]{:S(2)}, u32[]{:S(2)}) collective-permute-start(bf16[3584,384]{0,1:T(8,128)(2,1)} %copy.57), channel_id=1, source_target_pairs={{0,1},{1,0},{2,3},{3,2},{4,5},{5,4},{6,7},{7,6},{8,9},{9,8},{10,11... | collective-permute-start | bytes 8257544 | tf_op jit(solution)/shard_map/ppermute | solution.py:63
  72.2 1.8 %copy-start.1 = (bf16[3584,384]{0,1:T(8,128)(2,1)S(1)}, bf16[3584,384]{0,1:T(8,128)(2,1)}, u32[]{:S(2)}) copy-start(bf16[3584,384]{0,1:T(8,128)(2,1)} %copy.57) | copy-start | bytes 8257540
  77.3 2.4 %copy-start.2 = (bf16[3584,2,384]{0,2,1:T(8,128)(2,1)}, bf16[3584,2,384]{0,2,1:T(8,128)(2,1)S(1)}, u32[]{:S(2)}) copy-start(bf16[3584,2,384]{0,2,1:T(8,128)(2,1)S(1)} %reverse_select_fusion) | copy-start | bytes 16515076
  83.3 7.0 %collective-permute-start.1 = (bf16[3584,384]{1,0:T(8,128)(2,1)S(1)}, bf16[3584,384]{1,0:T(8,128)(2,1)S(1)}, u32[]{:S(2)}, u32[]{:S(2)}) collective-permute-start(bf16[3584,384]{1,0:T(8,128)(2,1)S(1)} %fusion.7), channel_id=1, source_target_pairs={{0,1},{1,0},{2,3},{3,2},{4,5},{5,4},{6,7},{7,6},{8,9},{9,8},{10,11... | collective-permute-start | bytes 8257544 | tf_op jit(solution)/shard_map/ppermute | solution.py:83
  92.8 1.0 copy-start.3
Sparse Core Ops, SparseCore 0:
  10.7 50.0 all-gather.2
  92.9 43.5 reduce-scatter.1

commit v11 on v10

--- a/solution.py
+++ b/solution.py
@@ -78,12 +78,9 @@
     )
     mine = lax.all_to_all(outgoing, ("ex", "ez"), split_axis=0, concat_axis=0, tiled=True)
     results, term = expert_math(mine, w_two, hid)
-    own = jnp.where(core == 0, term[:, 0], term[:, 1])
-    other = jnp.where(core == 0, term[:, 1], term[:, 0])
-    got = lax.ppermute(other.astype(jnp.bfloat16), "ec", swap)
-    chip_term = own + got.astype(f32)
+    by_core = jnp.transpose(term, (1, 0, 2)).reshape(-1, 3 * hid)
     summed = lax.psum_scatter(
-        chip_term.astype(jnp.bfloat16), "dp", scatter_dimension=0, tiled=True
+        by_core.astype(jnp.bfloat16), ("ec", "dp"), scatter_dimension=0, tiled=True
     ).astype(f32)
     grad_gate = summed[:, :hid][None]
     grad_up = summed[:, hid : 2 * hid][None]

time: 165 us -> 174 us (1.055)
  the two profiles are of different devices: /device:TPU:8 before, /device:TPU:1 now
where the time goes in v11:
time: 174 us; the launch traced here: 173 us
  waiting for transfers between devices  54.7 us (31%)
  blocking collectives  50.9 us (29%)
  starting transfers between devices  18.8 us (11%)
  matrix products  15.8 us (9%)
  between operations  14.2 us (8%)
  local copies, waits for them, and re-layouts  10.2 us (6%)
  other arithmetic  8.53 us (5%)
    all_to_all x1, blocking collectives, per_device(): lax.all_to_all(pair, ('ex', 'ez'), split_axis=0, concat_axis=0, tiled=True)  50.9 us
    all_gather x1, waiting for transfers between devices, per_device(): lax.all_gather(w_loc, 'dp', axis=0, tiled=False).reshape(-1, 3 * hid)  31.3 us
    reduce_scatter x1, waiting for transfers between devices, per_device(): lax.psum_scatter(by_core.astype(jnp.bfloat16), ('ec', 'dp'), scatter_dime...  18.9 us
    all_to_all x1, starting transfers between devices, per_device(): lax.all_to_all(outgoing, ('ex', 'ez'), split_axis=0, concat_axis=0, tiled...  13.7 us
    dot_general x1, matrix products, expert_math(): term = lax.dot_general(flat, grad_side, tn, preferred_element_type=f32)  5.1 us
    ppermute x1, starting transfers between devices, per_device(): w_other = lax.ppermute(w_all, 'ec', swap)  4.99 us
    all_gather x1, local copies, waits for them, and re-layouts, per_device(): lax.all_gather(w_loc, 'dp', axis=0, tiled=False).reshape(-1, 3 * hid)  4.57 us
    dot_general x1, matrix products, expert_math(): results = lax.dot_general(out_side, w_two, nt, preferred_element_type=f32)  4.15 us
  transfers between devices with their start and end apart: 4, of which 4 were waited for; matrix products, arithmetic and copies ran while one was open for 11% of the time, Pallas kernels for 0%

profile of v11, /device:TPU:1, one launch (start us, length us, event | category | flops | bytes accessed | tf_op | source)
XLA Modules:
  0.0 173.1 jit_solution(9209183932882900820)
XLA Ops:
  7.2 1.9 %pad_maximum_fusion.3 = bf16[448,384]{1,0:T(8,128)(2,1)} fusion(bf16[448,128]{1,0:T(8,128)(2,1)} %bitcast.112, bf16[448,128]{1,0:T(8,128)(2,1)} %bitcast.113, bf16[448,128]{1,0:T(8,128)(2,1)} %bitcast.114), kind=kLoop, calls=%fused_computation.20 | loop fusion | flops 1032192 | bytes 688128 | tf_op jit(solution)/shard_map/concatenate | solution.py:61
  9.1 0.7 fusion.10
  9.9 0.2 reduce_window_sum.11
  10.2 0.7 select_reduce_fusion
  11.1 0.2 convolution_convert_fusion.2
  11.4 1.4 fusion.5
  12.8 0.1 pad_maximum_fusion.4
  12.9 1.4 broadcast_in_dim.51
  14.3 13.7 %all-to-all-start = ((bf16[32,8,3584]{2,1,0:T(8,128)(2,1)}), bf16[32,8,3584]{2,1,0:T(8,128)(2,1)S(1)}, u32[]{:S(2)}, u32[]{:S(2)}) async-start(bf16[32,8,3584]{2,1,0:T(8,128)(2,1)} %bitcast.102), calls=%async_computation | async-start | bytes 3670016 | tf_op jit(solution)/shard_map/all_to_all | solution.py:79
  28.1 31.3 %all-gather.3.cloned.1.call-done = bf16[3584,384]{1,0:T(8,128)(2,1)} async-done(((bf16[448,384]{1,0:T(8,128)(2,1)}), bf16[3584,384]{1,0:T(8,128)(2,1)}) %all-gather.3.cloned.1.call-update) | async-done | bytes 2752528 | tf_op jit(solution)/shard_map/all_gather | solution.py:62
  59.4 4.6 %copy.57 = bf16[3584,384]{0,1:T(8,128)(2,1)} copy(bf16[3584,384]{1,0:T(8,128)(2,1)} %all-gather.3.cloned.1.call-done) | data formatting | bytes 5505024 | tf_op jit(solution)/shard_map/all_gather | solution.py:62
  64.0 5.0 %collective-permute-start = (bf16[3584,384]{0,1:T(8,128)(2,1)}, bf16[3584,384]{0,1:T(8,128)(2,1)}, u32[]{:S(2)}, u32[]{:S(2)}) collective-permute-start(bf16[3584,384]{0,1:T(8,128)(2,1)} %copy.57), channel_id=1, source_target_pairs={{0,1},{1,0},{2,3},{3,2},{4,5},{5,4},{6,7},{7,6},{8,9},{9,8},{10,11... | collective-permute-start | bytes 8257544 | tf_op jit(solution)/shard_map/ppermute | solution.py:63
  69.0 2.4 %all-to-all-done = bf16[32,8,3584]{2,1,0:T(8,128)(2,1)S(1)} async-done(((bf16[32,8,3584]{2,1,0:T(8,128)(2,1)}), bf16[32,8,3584]{2,1,0:T(8,128)(2,1)S(1)}, u32[]{:S(2)}, u32[]{:S(2)}) %all-to-all-start) | async-done | bytes 1835040 | tf_op jit(solution)/shard_map/all_to_all | solution.py:79
  71.4 0.5 copy.56
  72.0 2.0 %collective-permute-done = bf16[3584,384]{0,1:T(8,128)(2,1)} collective-permute-done((bf16[3584,384]{0,1:T(8,128)(2,1)}, bf16[3584,384]{0,1:T(8,128)(2,1)}, u32[]{:S(2)}, u32[]{:S(2)}) %collective-permute-start) | collective-permute-done | bytes 2752544 | tf_op jit(solution)/shard_map/ppermute | solution.py:63
  74.0 2.3 %pad_maximum_fusion = bf16[3584,2,384]{0,2,1:T(8,128)(2,1)S(1)} fusion(bf16[3584,1,384]{0,2,1:T(8,128)(2,1)} %bitcast.10, bf16[3584,1,384]{0,2,1:T(8,128)(2,1)S(1)} %bitcast.101), kind=kLoop, calls=%fused_computation.2 | loop fusion | flops 2752512 | bytes 11010048 | tf_op jit(solution)/shard_map/stack | solution.py:64
  76.3 1.1 reverse_select_fusion
  77.4 1.6 fusion
  79.0 0.8 copy-done.2
  80.0 0.3 copy.61
  80.4 0.9 copy.62
  81.3 5.1 %convolution_convert_fusion = bf16[3584,2,384]{2,0,1:T(8,128)(2,1)} fusion(bf16[2,384,256]{2,1,0:T(8,128)(2,1)} %bitcast.108, bf16[32,8,3584]{2,1,0:T(8,128)(2,1)S(1)} %all-to-all-done), kind=kOutput, calls=%fused_computation.1 | convolution fusion | flops 1412038656 | bytes 7733248 | tf_op jit(solution)/shard_map/dot_general | solution.py:50
  86.4 0.3 copy.59
  86.8 4.1 %fusion.2 = bf16[32,8,3584]{2,1,0:T(8,128)(2,1)S(1)} fusion(bf16[256,768]{1,0:T(8,128)(2,1)S(1)} %bitcast.109, bf16[3584,768]{0,1:T(8,128)(2,1)} %bitcast.103), kind=kOutput, calls=%fused_computation.6 | convolution fusion | flops 1410203648 | bytes 7733248 | tf_op jit(solution)/shard_map/dot_general | solution.py:49
  90.9 50.9 %all_to_all.10 = bf16[32,8,3584]{2,1,0:T(8,128)(2,1)S(1)} all-to-all(bf16[32,8,3584]{2,1,0:T(8,128)(2,1)S(1)} %fusion.2), channel_id=1, replica_groups=mesh['dp'=8,'ex'=4,'ez'=8,'ec'=2] {'ex','ez'}, dimensions={0} | all-to-all | bytes 3670016 | tf_op jit(solution)/shard_map/all_to_all | solution.py:89
  141.9 0.2 bitcast_reduce_fusion
  142.1 0.1 copy.60
  142.2 1.4 fusion.4
  143.6 1.9 %fusion.3 = bf16[128,3584]{1,0:T(8,128)(2,1)} fusion(bf16[4,2,4,3584]{3,0,2,1:T(4,128)(2,1)S(1)} %bitcast.111, f32[4,4]{0,1:T(4,128)S(1)} %get-tuple-element.14, s32[128,4]{0,1:T(4,128)S(1)} %copy.52, pred[128,4]{0,1:T(4,128)(4,1)S(1)} %fusion.10), kind=kOutput, calls=%fused_computation.9 | convolution fusion | flops 88547328 | bytes 1036800 | tf_op jit(solution)/shard_map/tec,ecf->tf/dot_general | solution.py:94
  145.6 18.9 %reduce-scatter.2.cloned.1.call-done = bf16[448,384]{1,0:T(8,128)(2,1)} async-done(((bf16[7168,384]{1,0:T(8,128)(2,1)}), bf16[448,384]{1,0:T(8,128)(2,1)}) %reduce-scatter.2.cloned.1.call-update) | async-done | bytes 344080 | tf_op jit(solution)/shard_map/reduce_scatter | solution.py:82
  164.4 1.0 convert_element_type.70
  165.4 0.9 slice_bitcast_fusion
  (23 shorter events, 0.8 us)
Async XLA Ops:
  7.2 4.0 %copy-start = (bf16[128,3584]{1,0:T(8,128)(2,1)S(1)}, bf16[128,3584]{1,0:T(8,128)(2,1)}, u32[]{:S(2)}) copy-start(bf16[128,3584]{1,0:T(8,128)(2,1)} %param.7) | copy-start | bytes 2752516
  7.2 52.2 %all-gather.3.cloned.1.call-start = ((), (), s32[]{:S(2)}) async-start(), calls=%async_computation.4 | async-start | bytes 3096576 | tf_op jit(solution)/shard_map/all_gather | solution.py:62
  14.3 57.1 %all-to-all-start = ((bf16[32,8,3584]{2,1,0:T(8,128)(2,1)}), bf16[32,8,3584]{2,1,0:T(8,128)(2,1)S(1)}, u32[]{:S(2)}, u32[]{:S(2)}) async-start(bf16[32,8,3584]{2,1,0:T(8,128)(2,1)} %bitcast.102), calls=%async_computation | async-start | bytes 3670016 | tf_op jit(solution)/shard_map/all_to_all | solution.py:79
  28.0 136.4 %reduce-scatter.2.cloned.1.call-start = ((), (), s32[]{:S(2)}) async-start(), calls=%async_computation.3 | async-start | bytes 5849088 | tf_op jit(solution)/shard_map/reduce_scatter | solution.py:82
  64.0 10.0 %collective-permute-start = (bf16[3584,384]{0,1:T(8,128)(2,1)}, bf16[3584,384]{0,1:T(8,128)(2,1)}, u32[]{:S(2)}, u32[]{:S(2)}) collective-permute-start(bf16[3584,384]{0,1:T(8,128)(2,1)} %copy.57), channel_id=1, source_target_pairs={{0,1},{1,0},{2,3},{3,2},{4,5},{5,4},{6,7},{7,6},{8,9},{9,8},{10,11... | collective-permute-start | bytes 8257544 | tf_op jit(solution)/shard_map/ppermute | solution.py:63
  71.4 2.6 %copy-start.1 = (bf16[3584,384]{0,1:T(8,128)(2,1)S(1)}, bf16[3584,384]{0,1:T(8,128)(2,1)}, u32[]{:S(2)}) copy-start(bf16[3584,384]{0,1:T(8,128)(2,1)} %copy.57) | copy-start | bytes 8257540
  77.4 2.4 %copy-start.2 = (bf16[3584,2,384]{0,2,1:T(8,128)(2,1)}, bf16[3584,2,384]{0,2,1:T(8,128)(2,1)S(1)}, u32[]{:S(2)}) copy-start(bf16[3584,2,384]{0,2,1:T(8,128)(2,1)S(1)} %reverse_select_fusion) | copy-start | bytes 16515076
Sparse Core Ops, SparseCore 0:
  10.7 48.6 all-gather.2
  86.5 77.8 reduce-scatter.1

commit v12 on v11

--- a/solution.py
+++ b/solution.py
@@ -47,8 +47,7 @@
     grad_side = jnp.stack([tok_side, cot_side], axis=1).reshape(-1, 2 * 3 * hid)
     out_side = jnp.stack([cot_side, tok_side], axis=1).reshape(-1, 2 * 3 * hid)
     results = lax.dot_general(out_side, w_two, nt, preferred_element_type=f32)
-    term = lax.dot_general(flat, grad_side, tn, preferred_element_type=f32)
-    return results, term.reshape(term.shape[0], 2, 3 * hid)
+    return results, grad_side.reshape(-1, 2, 3 * hid)
 
 
 def per_device(tokens, out_cotangent, expert_ids, gate_fixed, w_gate, w_up, w_down):
@@ -77,10 +76,17 @@
         window * zsize, 2 * CAP, width
     )
     mine = lax.all_to_all(outgoing, ("ex", "ez"), split_axis=0, concat_axis=0, tiled=True)
-    results, term = expert_math(mine, w_two, hid)
-    by_core = jnp.transpose(term, (1, 0, 2)).reshape(-1, 3 * hid)
+    partner = lax.ppermute(mine, "ec", swap)
+    results, grad_side = expert_math(mine, w_two, hid)
+    own_side = jnp.where(core == 0, grad_side[:, 0], grad_side[:, 1])
+    other_side = jnp.where(core == 0, grad_side[:, 1], grad_side[:, 0])
+    got_side = lax.ppermute(other_side, "ec", swap)
+    tn = (((0,), (0,)), ((), ()))
+    chip_term = lax.dot_general(
+        mine.reshape(-1, width), own_side, tn, preferred_element_type=f32
+    ) + lax.dot_general(partner.reshape(-1, width), got_side, tn, preferred_element_type=f32)
     summed = lax.psum_scatter(
-        by_core.astype(jnp.bfloat16), ("ec", "dp"), scatter_dimension=0, tiled=True
+        chip_term.astype(jnp.bfloat16), "dp", scatter_dimension=0, tiled=True
     ).astype(f32)
     grad_gate = summed[:, :hid][None]
     grad_up = summed[:, hid : 2 * hid][None]

time: 174 us -> 159 us (0.914)
  the two profiles are of different devices: /device:TPU:1 before, /device:TPU:64 now
where the time goes in v12:
time: 159 us; the launch traced here: 158 us
  blocking collectives  54.4 us (34%)
  waiting for transfers between devices  37.4 us (24%)
  starting transfers between devices  19 us (12%)
  matrix products  14.6 us (9%)
  between operations  14.3 us (9%)
  other arithmetic  9.45 us (6%)
  local copies, waits for them, and re-layouts  9.25 us (6%)
    all_to_all x1, blocking collectives, per_device(): lax.all_to_all(pair, ('ex', 'ez'), split_axis=0, concat_axis=0, tiled=True)  54.4 us
    all_gather x1, waiting for transfers between devices, per_device(): lax.all_gather(w_loc, 'dp', axis=0, tiled=False).reshape(-1, 3 * hid)  33.3 us
    all_to_all x1, starting transfers between devices, per_device(): lax.all_to_all(outgoing, ('ex', 'ez'), split_axis=0, concat_axis=0, tiled...  12.6 us
    all_gather x1, local copies, waits for them, and re-layouts, per_device(): lax.all_gather(w_loc, 'dp', axis=0, tiled=False).reshape(-1, 3 * hid)  4.58 us
    dot_general x1, matrix products, expert_math(): results = lax.dot_general(out_side, w_two, nt, preferred_element_type=f32)  4.15 us
    all_to_all x1, waiting for transfers between devices, per_device(): lax.all_to_all(outgoing, ('ex', 'ez'), split_axis=0, concat_axis=0, tiled...  4.02 us
  transfers between devices with their start and end apart: 6, of which 2 were waited for; matrix products, arithmetic and copies ran while one was open for 16% of the time, Pallas kernels for 0%

profile of v12, /device:TPU:64, one launch (start us, length us, event | category | flops | bytes accessed | tf_op | source)
XLA Modules:
  0.0 158.4 jit_solution(12303720792165122666)
XLA Ops:
  7.2 1.9 %pad_maximum_fusion.3 = bf16[448,384]{1,0:T(8,128)(2,1)} fusion(bf16[448,128]{1,0:T(8,128)(2,1)} %bitcast.109, bf16[448,128]{1,0:T(8,128)(2,1)} %bitcast.110, bf16[448,128]{1,0:T(8,128)(2,1)} %bitcast.111), kind=kLoop, calls=%fused_computation.25 | loop fusion | flops 1032192 | bytes 688128 | tf_op jit(solution)/shard_map/concatenate | solution.py:60
  9.1 0.7 fusion.15
  9.9 0.2 reduce_window_sum.11
  10.2 0.7 select_reduce_fusion
  11.1 0.2 convolution_convert_fusion.1
  11.4 1.4 fusion.6
  12.9 1.4 broadcast_in_dim.51
  14.3 12.6 %all-to-all-start = ((bf16[32,8,3584]{2,1,0:T(8,128)(2,1)}), bf16[32,8,3584]{2,1,0:T(8,128)(2,1)S(1)}, u32[]{:S(2)}, u32[]{:S(2)}) async-start(bf16[32,8,3584]{2,1,0:T(8,128)(2,1)} %bitcast.100), calls=%async_computation | async-start | bytes 3670016 | tf_op jit(solution)/shard_map/all_to_all | solution.py:78
  26.9 33.3 %all-gather.3.cloned.1.call-done = bf16[3584,384]{1,0:T(8,128)(2,1)} async-done(((bf16[448,384]{1,0:T(8,128)(2,1)}), bf16[3584,384]{1,0:T(8,128)(2,1)}) %all-gather.3.cloned.1.call-update) | async-done | bytes 2752528 | tf_op jit(solution)/shard_map/all_gather | solution.py:61
  60.3 4.6 %copy.52 = bf16[3584,384]{0,1:T(8,128)(2,1)} copy(bf16[3584,384]{1,0:T(8,128)(2,1)} %all-gather.3.cloned.1.call-done) | data formatting | bytes 5505024 | tf_op jit(solution)/shard_map/all_gather | solution.py:61
  64.8 1.9 %collective-permute-start = (bf16[3584,384]{0,1:T(8,128)(2,1)}, bf16[3584,384]{0,1:T(8,128)(2,1)}, u32[]{:S(2)}, u32[]{:S(2)}) collective-permute-start(bf16[3584,384]{0,1:T(8,128)(2,1)} %copy.52), channel_id=1, source_target_pairs={{0,1},{1,0},{2,3},{3,2},{4,5},{5,4},{6,7},{7,6},{8,9},{9,8},{10,11... | collective-permute-start | bytes 8257544 | tf_op jit(solution)/shard_map/ppermute | solution.py:62
  66.8 4.0 %all-to-all-done = bf16[32,8,3584]{2,1,0:T(8,128)(2,1)S(1)} async-done(((bf16[32,8,3584]{2,1,0:T(8,128)(2,1)}), bf16[32,8,3584]{2,1,0:T(8,128)(2,1)S(1)}, u32[]{:S(2)}, u32[]{:S(2)}) %all-to-all-start) | async-done | bytes 1835040 | tf_op jit(solution)/shard_map/all_to_all | solution.py:78
  70.8 0.5 copy.51
  71.4 2.1 %collective-permute-start.1 = (bf16[32,8,3584]{2,1,0:T(8,128)(2,1)S(1)}, bf16[32,8,3584]{2,1,0:T(8,128)(2,1)S(1)}, u32[]{:S(2)}, u32[]{:S(2)}) collective-permute-start(bf16[32,8,3584]{2,1,0:T(8,128)(2,1)S(1)} %all-to-all-done), channel_id=1, source_target_pairs={{0,1},{1,0},{2,3},{3,2},{4,5},{5,4},{6,7},{7,6},{8,9},{9,8},{10,11... | collective-permute-start | bytes 5505032 | tf_op jit(solution)/shard_map/ppermute | solution.py:79
  73.4 2.3 %pad_maximum_fusion = bf16[3584,2,384]{0,2,1:T(8,128)(2,1)S(1)} fusion(bf16[3584,1,384]{0,2,1:T(8,128)(2,1)} %bitcast.10, bf16[3584,1,384]{0,2,1:T(8,128)(2,1)S(1)} %bitcast.99), kind=kLoop, calls=%fused_computation.3 | loop fusion | flops 2752512 | bytes 11010048 | tf_op jit(solution)/shard_map/stack | solution.py:63
  75.7 1.1 reverse_select_fusion
  76.8 1.6 %fusion.1 = f32[32,2,4,2,384]{4,0,3,2,1:T(8,128)S(1)} fusion(bf16[32,2,4,3584,1]{3,0,4,2,1:T(8,128)(2,1)S(1)} %bitcast.103, bf16[3584,2,384]{0,2,1:T(8,128)(2,1)S(1)} %reverse_select_fusion), kind=kOutput, calls=%fused_computation.4 | convolution fusion | flops 1409286144 | bytes 8126464 | tf_op jit(solution)/shard_map/dot_general | solution.py:35
  78.4 0.8 copy-done.2
  79.4 0.3 copy.56
  79.7 0.9 broadcast_select_fusion
  80.7 2.4 %collective-permute-start.2 = (bf16[256,384]{1,0:T(8,128)(2,1)S(1)}, bf16[256,384]{1,0:T(8,128)(2,1)S(1)}, u32[]{:S(2)}, u32[]{:S(2)}) collective-permute-start(bf16[256,384]{1,0:T(8,128)(2,1)S(1)} %bitcast.108), channel_id=1, source_target_pairs={{0,1},{1,0},{2,3},{3,2},{4,5},{5,4},{6,7},{7,6},{8,9},{9,8},{10,11... | collective-permute-start | bytes 589832 | tf_op jit(solution)/shard_map/ppermute | solution.py:83
  83.1 1.1 fusion.8
  84.3 2.7 %fusion = bf16[3584,384]{1,0:T(8,128)(2,1)} fusion(f32[3584,384]{1,0:T(8,128)S(1)} %fusion.8, bf16[256,384]{1,0:T(8,128)(2,1)S(1)} %collective-permute-done.2, bf16[32,8,3584]{2,1,0:T(8,128)(2,1)S(1)} %collective-permute-done.1), kind=kOutput, calls=%fused_computation.2 | convolution fusion | flops 707395584 | bytes 10289152 | tf_op jit(solution)/shard_map/dot_general | solution.py:87
  87.0 0.3 copy.54
  87.4 4.1 %fusion.3 = bf16[32,8,3584]{2,1,0:T(8,128)(2,1)S(1)} fusion(bf16[256,768]{1,0:T(8,128)(2,1)S(1)} %bitcast.105, bf16[3584,768]{0,1:T(8,128)(2,1)} %bitcast.101), kind=kOutput, calls=%fused_computation.7 | convolution fusion | flops 1410203648 | bytes 7733248 | tf_op jit(solution)/shard_map/dot_general | solution.py:49
  91.6 54.4 %all_to_all.10 = bf16[32,8,3584]{2,1,0:T(8,128)(2,1)S(1)} all-to-all(bf16[32,8,3584]{2,1,0:T(8,128)(2,1)S(1)} %fusion.3), channel_id=1, replica_groups=mesh['dp'=8,'ex'=4,'ez'=8,'ec'=2] {'ex','ez'}, dimensions={0} | all-to-all | bytes 3670016 | tf_op jit(solution)/shard_map/all_to_all | solution.py:95
  146.0 0.2 bitcast_reduce_fusion
  146.2 0.1 copy.55
  146.3 1.4 fusion.5
  147.7 1.9 %fusion.4 = bf16[128,3584]{1,0:T(8,128)(2,1)} fusion(bf16[4,2,4,3584]{3,0,2,1:T(4,128)(2,1)S(1)} %bitcast.107, f32[4,4]{0,1:T(4,128)S(1)} %get-tuple-element.16, s32[128,4]{0,1:T(4,128)S(1)} %copy.47, pred[128,4]{0,1:T(4,128)(4,1)S(1)} %fusion.15), kind=kOutput, calls=%fused_computation.10 | convolution fusion | flops 88547328 | bytes 1036800 | tf_op jit(solution)/shard_map/tec,ecf->tf/dot_general | solution.py:100
  149.7 1.0 convert_element_type.62
  150.7 0.9 slice_bitcast_fusion
  (28 shorter events, 0.9 us)
Async XLA Ops:
  7.2 4.0 %copy-start = (bf16[128,3584]{1,0:T(8,128)(2,1)S(1)}, bf16[128,3584]{1,0:T(8,128)(2,1)}, u32[]{:S(2)}) copy-start(bf16[128,3584]{1,0:T(8,128)(2,1)} %param.7) | copy-start | bytes 2752516
  7.2 53.1 %all-gather.3.cloned.1.call-start = ((), (), s32[]{:S(2)}) async-start(), calls=%async_computation.4 | async-start | bytes 3096576 | tf_op jit(solution)/shard_map/all_gather | solution.py:61
  14.3 56.5 %all-to-all-start = ((bf16[32,8,3584]{2,1,0:T(8,128)(2,1)}), bf16[32,8,3584]{2,1,0:T(8,128)(2,1)S(1)}, u32[]{:S(2)}, u32[]{:S(2)}) async-start(bf16[32,8,3584]{2,1,0:T(8,128)(2,1)} %bitcast.100), calls=%async_computation | async-start | bytes 3670016 | tf_op jit(solution)/shard_map/all_to_all | solution.py:78
  26.9 122.8 %reduce-scatter.2.cloned.1.call-start = ((), (), s32[]{:S(2)}) async-start(), calls=%async_computation.3 | async-start | bytes 3096576 | tf_op jit(solution)/shard_map/reduce_scatter | solution.py:88
  64.8 8.6 %collective-permute-start = (bf16[3584,384]{0,1:T(8,128)(2,1)}, bf16[3584,384]{0,1:T(8,128)(2,1)}, u32[]{:S(2)}, u32[]{:S(2)}) collective-permute-start(bf16[3584,384]{0,1:T(8,128)(2,1)} %copy.52), channel_id=1, source_target_pairs={{0,1},{1,0},{2,3},{3,2},{4,5},{5,4},{6,7},{7,6},{8,9},{9,8},{10,11... | collective-permute-start | bytes 8257544 | tf_op jit(solution)/shard_map/ppermute | solution.py:62
  70.8 2.6 %copy-start.1 = (bf16[3584,384]{0,1:T(8,128)(2,1)S(1)}, bf16[3584,384]{0,1:T(8,128)(2,1)}, u32[]{:S(2)}) copy-start(bf16[3584,384]{0,1:T(8,128)(2,1)} %copy.52) | copy-start | bytes 8257540
  71.4 12.9 %collective-permute-start.1 = (bf16[32,8,3584]{2,1,0:T(8,128)(2,1)S(1)}, bf16[32,8,3584]{2,1,0:T(8,128)(2,1)S(1)}, u32[]{:S(2)}, u32[]{:S(2)}) collective-permute-start(bf16[32,8,3584]{2,1,0:T(8,128)(2,1)S(1)} %all-to-all-done), channel_id=1, source_target_pairs={{0,1},{1,0},{2,3},{3,2},{4,5},{5,4},{6,7},{7,6},{8,9},{9,8},{10,11... | collective-permute-start | bytes 5505032 | tf_op jit(solution)/shard_map/ppermute | solution.py:79
  76.8 2.4 %copy-start.2 = (bf16[3584,2,384]{0,2,1:T(8,128)(2,1)}, bf16[3584,2,384]{0,2,1:T(8,128)(2,1)S(1)}, u32[]{:S(2)}) copy-start(bf16[3584,2,384]{0,2,1:T(8,128)(2,1)S(1)} %reverse_select_fusion) | copy-start | bytes 16515076
  80.7 3.6 %collective-permute-start.2 = (bf16[256,384]{1,0:T(8,128)(2,1)S(1)}, bf16[256,384]{1,0:T(8,128)(2,1)S(1)}, u32[]{:S(2)}, u32[]{:S(2)}) collective-permute-start(bf16[256,384]{1,0:T(8,128)(2,1)S(1)} %bitcast.108), channel_id=1, source_target_pairs={{0,1},{1,0},{2,3},{3,2},{4,5},{5,4},{6,7},{7,6},{8,9},{9,8},{10,11... | collective-permute-start | bytes 589832 | tf_op jit(solution)/shard_map/ppermute | solution.py:83
Sparse Core Ops, SparseCore 0:
  10.7 49.5 all-gather.2
  87.2 44.8 reduce-scatter.1

commit v13 on v12

--- a/solution.py
+++ b/solution.py
@@ -25,17 +25,18 @@
     return (select, slot_gate)
 
 
-def expert_math(mine, w_two, hid):
+def expert_math(mine, w_own, w_other, hid):
     f32 = jnp.float32
     bf16 = jnp.bfloat16
     nt = (((1,), (1,)), ((), ()))
-    tn = (((0,), (0,)), ((), ()))
     n = mine.shape[0]
     flat = mine.reshape(-1, mine.shape[-1])
-    pre = jnp.dot(flat, w_two, preferred_element_type=f32).reshape(n, 2, -1, 2, 3 * hid)
-    gate_pre = pre[:, 0, :, :, :hid]
-    up_pre = pre[:, 0, :, :, hid : 2 * hid]
-    d_hidden = pre[:, 1, :, :, 2 * hid :]
+    pre_a = jnp.dot(flat, w_own, preferred_element_type=f32)
+    pre_b = jnp.dot(flat, w_other, preferred_element_type=f32)
+    pre = jnp.stack([pre_a, pre_b], axis=0).reshape(2, n, 2, -1, 3 * hid)
+    gate_pre = pre[:, :, 0, :, :hid]
+    up_pre = pre[:, :, 0, :, hid : 2 * hid]
+    d_hidden = pre[:, :, 1, :, 2 * hid :]
     sig = jax.nn.sigmoid(gate_pre)
     act = gate_pre * sig
     hidden = (act * up_pre).astype(bf16)
@@ -44,10 +45,12 @@
     zero = jnp.zeros_like(hidden)
     tok_side = jnp.concatenate([d_gate, d_up, zero], axis=-1)
     cot_side = jnp.concatenate([zero, zero, hidden], axis=-1)
-    grad_side = jnp.stack([tok_side, cot_side], axis=1).reshape(-1, 2 * 3 * hid)
-    out_side = jnp.stack([cot_side, tok_side], axis=1).reshape(-1, 2 * 3 * hid)
-    results = lax.dot_general(out_side, w_two, nt, preferred_element_type=f32)
-    return results, grad_side.reshape(-1, 2, 3 * hid)
+    grad_side = jnp.stack([tok_side, cot_side], axis=2).reshape(2, -1, 3 * hid)
+    out_side = jnp.stack([cot_side, tok_side], axis=2).reshape(2, -1, 3 * hid)
+    results = lax.dot_general(out_side[0], w_own, nt, preferred_element_type=f32) + lax.dot_general(
+        out_side[1], w_other, nt, preferred_element_type=f32
+    )
+    return results, grad_side[0], grad_side[1]
 
 
 def per_device(tokens, out_cotangent, expert_ids, gate_fixed, w_gate, w_up, w_down):
@@ -55,14 +58,10 @@
     zsize = lax.axis_size("ez")
     hid = w_gate.shape[2]
     f32 = jnp.float32
-    core = lax.axis_index("ec")
     swap = [(0, 1), (1, 0)]
     w_loc = jnp.concatenate([w_gate[0], w_up[0], w_down[0]], axis=1)
     w_all = lax.all_gather(w_loc, "dp", axis=0, tiled=False).reshape(-1, 3 * hid)
     w_other = lax.ppermute(w_all, "ec", swap)
-    w_pair = jnp.stack([w_all, w_other], axis=1)
-    w_pair = jnp.where(core == 0, w_pair, w_pair[:, ::-1])
-    w_two = w_pair.reshape(-1, 2 * 3 * hid)
     select, slot_gate = routing(expert_ids, gate_fixed, window, CAP)
     select_b = select.astype(jnp.bfloat16)
     slot_tokens = jnp.einsum("tec,tf->ecf", select_b, tokens, preferred_element_type=f32).astype(
@@ -77,9 +76,7 @@
     )
     mine = lax.all_to_all(outgoing, ("ex", "ez"), split_axis=0, concat_axis=0, tiled=True)
     partner = lax.ppermute(mine, "ec", swap)
-    results, grad_side = expert_math(mine, w_two, hid)
-    own_side = jnp.where(core == 0, grad_side[:, 0], grad_side[:, 1])
-    other_side = jnp.where(core == 0, grad_side[:, 1], grad_side[:, 0])
+    results, own_side, other_side = expert_math(mine, w_all, w_other, hid)
     got_side = lax.ppermute(other_side, "ec", swap)
     tn = (((0,), (0,)), ((), ()))
     chip_term = lax.dot_general(

time: 159 us -> 159 us (level)
  the two profiles are of different devices: /device:TPU:64 before, /device:TPU:40 now
where the time goes in v13:
time: 159 us; the launch traced here: 158 us
  blocking collectives  51 us (32%)
  waiting for transfers between devices  42.7 us (27%)
  matrix products  21.1 us (13%)
  starting transfers between devices  19.6 us (12%)
  between operations  14.3 us (9%)
  other arithmetic  5.27 us (3%)
  local copies, waits for them, and re-layouts  4.51 us (3%)
    all_to_all x1, blocking collectives, per_device(): lax.all_to_all(pair, ('ex', 'ez'), split_axis=0, concat_axis=0, tiled=True)  51 us
    all_gather x1, waiting for transfers between devices, per_device(): lax.all_gather(w_loc, 'dp', axis=0, tiled=False).reshape(-1, 3 * hid)  31.1 us
    all_to_all x1, starting transfers between devices, per_device(): lax.all_to_all(outgoing, ('ex', 'ez'), split_axis=0, concat_axis=0, tiled...  13.2 us
    all_to_all x1, waiting for transfers between devices, per_device(): lax.all_to_all(outgoing, ('ex', 'ez'), split_axis=0, concat_axis=0, tiled...  11.6 us
    dot_general x1, matrix products, per_device(): lax.dot_general(partner.reshape(-1, width), got_side, tn, preferred_eleme...  4.18 us
  transfers between devices with their start and end apart: 6, of which 2 were waited for; matrix products, arithmetic and copies ran while one was open for 14% of the time, Pallas kernels for 0%

profile of v13, /device:TPU:40, one launch (start us, length us, event | category | flops | bytes accessed | tf_op | source)
XLA Modules:
  0.0 158.5 jit_solution(9870680483545604585)
XLA Ops:
  7.2 1.9 %pad_maximum_fusion = bf16[448,384]{1,0:T(8,128)(2,1)} fusion(bf16[448,128]{1,0:T(8,128)(2,1)} %bitcast.90, bf16[448,128]{1,0:T(8,128)(2,1)} %bitcast.91, bf16[448,128]{1,0:T(8,128)(2,1)} %bitcast.92), kind=kLoop, calls=%fused_computation.28 | loop fusion | flops 1032192 | bytes 688128 | tf_op jit(solution)/shard_map/concatenate | solution.py:62
  9.1 0.7 fusion.25
  9.8 0.1 copy.51
  9.9 0.2 reduce_window_sum.11
  10.2 0.7 select_reduce_fusion
  11.1 0.2 convolution_convert_fusion
  11.4 1.4 fusion.5
  12.8 0.1 pad_maximum_fusion.1
  12.9 1.4 broadcast_in_dim.51
  14.3 13.2 %all-to-all-start = ((bf16[32,8,3584]{2,1,0:T(8,128)(2,1)}), bf16[32,8,3584]{2,1,0:T(8,128)(2,1)S(1)}, u32[]{:S(2)}, u32[]{:S(2)}) async-start(bf16[32,8,3584]{2,1,0:T(8,128)(2,1)} %bitcast.85), calls=%async_computation | async-start | bytes 3670016 | tf_op jit(solution)/shard_map/all_to_all | solution.py:77
  27.5 31.1 %all-gather.3.cloned.1.call-done = bf16[3584,384]{1,0:T(8,128)(2,1)} async-done(((bf16[448,384]{1,0:T(8,128)(2,1)}), bf16[3584,384]{1,0:T(8,128)(2,1)}) %all-gather.3.cloned.1.call-update) | async-done | bytes 2752528 | tf_op jit(solution)/shard_map/all_gather | solution.py:63
  58.6 1.9 %collective-permute-start = (bf16[3584,384]{1,0:T(8,128)(2,1)}, bf16[3584,384]{1,0:T(8,128)(2,1)}, u32[]{:S(2)}, u32[]{:S(2)}) collective-permute-start(bf16[3584,384]{1,0:T(8,128)(2,1)} %all-gather.3.cloned.1.call-done), channel_id=1, source_target_pairs={{0,1},{1,0},{2,3},{3,2},{4,5},{5,4},{6,7},{7,6},{8,9},{9,8},{10,11... | collective-permute-start | bytes 8257544 | tf_op jit(solution)/shard_map/ppermute | solution.py:64
  60.5 11.6 %all-to-all-done = bf16[32,8,3584]{2,1,0:T(8,128)(2,1)S(1)} async-done(((bf16[32,8,3584]{2,1,0:T(8,128)(2,1)}), bf16[32,8,3584]{2,1,0:T(8,128)(2,1)S(1)}, u32[]{:S(2)}, u32[]{:S(2)}) %all-to-all-start) | async-done | bytes 1835040 | tf_op jit(solution)/shard_map/all_to_all | solution.py:77
  72.2 0.5 copy.56
  72.7 2.1 %collective-permute-start.1 = (bf16[32,8,3584]{2,1,0:T(8,128)(2,1)S(1)}, bf16[32,8,3584]{2,1,0:T(8,128)(2,1)}, u32[]{:S(2)}, u32[]{:S(2)}) collective-permute-start(bf16[32,8,3584]{2,1,0:T(8,128)(2,1)S(1)} %all-to-all-done), channel_id=1, source_target_pairs={{0,1},{1,0},{2,3},{3,2},{4,5},{5,4},{6,7},{7,6},{8,9},{9,8},{10,11... | collective-permute-start | bytes 5505032 | tf_op jit(solution)/shard_map/ppermute | solution.py:78
  74.8 1.1 fusion.13
  75.9 2.9 %fusion.16 = f32[1,32,2,4,384]{4,1,3,2,0:T(8,128)S(1)} fusion(bf16[32,2,4,3584]{3,0,2,1:T(8,128)(2,1)S(1)} %bitcast.87, bf16[3584,384]{1,0:T(8,128)(2,1)} %collective-permute-done), kind=kOutput, calls=%fused_computation.21 | convolution fusion | flops 704643072 | bytes 4980736 | tf_op jit(solution)/shard_map/dot_general | solution.py:35
  79.2 0.7 squeeze.46
  80.1 2.4 %collective-permute-start.2 = (bf16[256,384]{1,0:T(8,128)(2,1)S(1)}, bf16[256,384]{1,0:T(8,128)(2,1)S(1)}, u32[]{:S(2)}, u32[]{:S(2)}) collective-permute-start(bf16[256,384]{1,0:T(8,128)(2,1)S(1)} %squeeze.47), channel_id=1, source_target_pairs={{0,1},{1,0},{2,3},{3,2},{4,5},{5,4},{6,7},{7,6},{8,9},{9,8},{10,11... | collective-permute-start | bytes 589832 | tf_op jit(solution)/shard_map/ppermute | solution.py:80
  82.6 2.1 %fusion.11 = f32[3584,384]{1,0:T(8,128)S(1)} fusion(bf16[256,384]{1,0:T(8,128)(2,1)} %squeeze.46, bf16[32,8,3584]{2,1,0:T(8,128)(2,1)S(1)} %all-to-all-done), kind=kOutput, calls=%fused_computation.17 | convolution fusion | flops 704643072 | bytes 7536640 | tf_op jit(solution)/shard_map/dot_general | solution.py:82
  84.6 4.2 %fusion = bf16[3584,384]{1,0:T(8,128)(2,1)} fusion(f32[3584,384]{1,0:T(8,128)S(1)} %fusion.11, bf16[256,384]{1,0:T(8,128)(2,1)S(1)} %collective-permute-done.2, bf16[32,8,3584]{2,1,0:T(8,128)(2,1)} %collective-permute-done.1), kind=kOutput, calls=%fused_computation.1 | convolution fusion | flops 707395584 | bytes 10289152 | tf_op jit(solution)/shard_map/dot_general | solution.py:84
  88.9 0.1 copy.59
  89.0 0.1 copy.60
  89.2 2.9 %fusion.40 = f32[256,3584]{1,0:T(8,128)S(1)} fusion(bf16[256,384]{1,0:T(8,128)(2,1)S(1)} %squeeze.42, bf16[3584,384]{1,0:T(8,128)(2,1)} %all-gather.3.cloned.1.call-done), kind=kOutput, calls=%fused_computation.70 | convolution fusion | flops 704643072 | bytes 6619136 | tf_op jit(solution)/shard_map/dot_general | solution.py:50
  92.1 2.9 %fusion.2 = bf16[32,8,3584]{2,1,0:T(8,128)(2,1)S(1)} fusion(f32[256,3584]{1,0:T(8,128)S(1)} %fusion.40, bf16[256,384]{1,0:T(8,128)(2,1)S(1)} %squeeze.43, bf16[3584,384]{1,0:T(8,128)(2,1)} %collective-permute-done), kind=kOutput, calls=%fused_computation.4 | convolution fusion | flops 706478080 | bytes 8454144 | tf_op jit(solution)/shard_map/dot_general | solution.py:50
  95.0 51.0 %all_to_all.10 = bf16[32,8,3584]{2,1,0:T(8,128)(2,1)S(1)} all-to-all(bf16[32,8,3584]{2,1,0:T(8,128)(2,1)S(1)} %fusion.2), channel_id=1, replica_groups=mesh['dp'=8,'ex'=4,'ez'=8,'ec'=2] {'ex','ez'}, dimensions={0} | all-to-all | bytes 3670016 | tf_op jit(solution)/shard_map/all_to_all | solution.py:92
  146.1 0.2 bitcast_reduce_fusion
  146.3 0.1 copy.61
  146.4 1.4 fusion.4
  147.8 1.9 %fusion.3 = bf16[128,3584]{1,0:T(8,128)(2,1)} fusion(bf16[4,2,4,3584]{3,0,2,1:T(4,128)(2,1)S(1)} %bitcast.89, f32[4,4]{0,1:T(4,128)S(1)} %get-tuple-element.19, s32[128,4]{0,1:T(4,128)S(1)} %copy.52, pred[128,4]{0,1:T(4,128)(4,1)S(1)} %fusion.25), kind=kOutput, calls=%fused_computation.7 | convolution fusion | flops 88547328 | bytes 1036800 | tf_op jit(solution)/shard_map/tec,ecf->tf/dot_general | solution.py:97
  149.8 1.0 convert_element_type.62
  150.8 0.9 slice_bitcast_fusion
  (29 shorter events, 1.1 us)
Async XLA Ops:
  7.2 4.0 %copy-start = (bf16[128,3584]{1,0:T(8,128)(2,1)S(1)}, bf16[128,3584]{1,0:T(8,128)(2,1)}, u32[]{:S(2)}) copy-start(bf16[128,3584]{1,0:T(8,128)(2,1)} %param.7) | copy-start | bytes 2752516
  7.2 51.4 %all-gather.3.cloned.1.call-start = ((), (), s32[]{:S(2)}) async-start(), calls=%async_computation.4 | async-start | bytes 3096576 | tf_op jit(solution)/shard_map/all_gather | solution.py:63
  14.3 57.9 %all-to-all-start = ((bf16[32,8,3584]{2,1,0:T(8,128)(2,1)}), bf16[32,8,3584]{2,1,0:T(8,128)(2,1)S(1)}, u32[]{:S(2)}, u32[]{:S(2)}) async-start(bf16[32,8,3584]{2,1,0:T(8,128)(2,1)} %bitcast.85), calls=%async_computation | async-start | bytes 3670016 | tf_op jit(solution)/shard_map/all_to_all | solution.py:77
  27.5 122.3 %reduce-scatter.2.cloned.1.call-start = ((), (), s32[]{:S(2)}) async-start(), calls=%async_computation.3 | async-start | bytes 3096576 | tf_op jit(solution)/shard_map/reduce_scatter | solution.py:85
  58.6 17.3 %collective-permute-start = (bf16[3584,384]{1,0:T(8,128)(2,1)}, bf16[3584,384]{1,0:T(8,128)(2,1)}, u32[]{:S(2)}, u32[]{:S(2)}) collective-permute-start(bf16[3584,384]{1,0:T(8,128)(2,1)} %all-gather.3.cloned.1.call-done), channel_id=1, source_target_pairs={{0,1},{1,0},{2,3},{3,2},{4,5},{5,4},{6,7},{7,6},{8,9},{9,8},{10,11... | collective-permute-start | bytes 8257544 | tf_op jit(solution)/shard_map/ppermute | solution.py:64
  72.2 2.6 %copy-start.1 = (bf16[3584,384]{1,0:T(8,128)(2,1)S(1)}, bf16[3584,384]{1,0:T(8,128)(2,1)}, u32[]{:S(2)}) copy-start(bf16[3584,384]{1,0:T(8,128)(2,1)} %all-gather.3.cloned.1.call-done) | copy-start | bytes 8257540
  72.7 11.9 %collective-permute-start.1 = (bf16[32,8,3584]{2,1,0:T(8,128)(2,1)S(1)}, bf16[32,8,3584]{2,1,0:T(8,128)(2,1)}, u32[]{:S(2)}, u32[]{:S(2)}) collective-permute-start(bf16[32,8,3584]{2,1,0:T(8,128)(2,1)S(1)} %all-to-all-done), channel_id=1, source_target_pairs={{0,1},{1,0},{2,3},{3,2},{4,5},{5,4},{6,7},{7,6},{8,9},{9,8},{10,11... | collective-permute-start | bytes 5505032 | tf_op jit(solution)/shard_map/ppermute | solution.py:78
  80.1 4.5 %collective-permute-start.2 = (bf16[256,384]{1,0:T(8,128)(2,1)S(1)}, bf16[256,384]{1,0:T(8,128)(2,1)S(1)}, u32[]{:S(2)}, u32[]{:S(2)}) collective-permute-start(bf16[256,384]{1,0:T(8,128)(2,1)S(1)} %squeeze.47), channel_id=1, source_target_pairs={{0,1},{1,0},{2,3},{3,2},{4,5},{5,4},{6,7},{7,6},{8,9},{9,8},{10,11... | collective-permute-start | bytes 589832 | tf_op jit(solution)/shard_map/ppermute | solution.py:80
Sparse Core Ops, SparseCore 0:
  10.7 47.8 all-gather.2
  89.0 42.1 reduce-scatter.1

commit v14 on v12

--- a/solution.py
+++ b/solution.py
@@ -55,13 +55,11 @@
     zsize = lax.axis_size("ez")
     hid = w_gate.shape[2]
     f32 = jnp.float32
-    core = lax.axis_index("ec")
     swap = [(0, 1), (1, 0)]
     w_loc = jnp.concatenate([w_gate[0], w_up[0], w_down[0]], axis=1)
     w_all = lax.all_gather(w_loc, "dp", axis=0, tiled=False).reshape(-1, 3 * hid)
     w_other = lax.ppermute(w_all, "ec", swap)
     w_pair = jnp.stack([w_all, w_other], axis=1)
-    w_pair = jnp.where(core == 0, w_pair, w_pair[:, ::-1])
     w_two = w_pair.reshape(-1, 2 * 3 * hid)
     select, slot_gate = routing(expert_ids, gate_fixed, window, CAP)
     select_b = select.astype(jnp.bfloat16)
@@ -78,8 +76,8 @@
     mine = lax.all_to_all(outgoing, ("ex", "ez"), split_axis=0, concat_axis=0, tiled=True)
     partner = lax.ppermute(mine, "ec", swap)
     results, grad_side = expert_math(mine, w_two, hid)
-    own_side = jnp.where(core == 0, grad_side[:, 0], grad_side[:, 1])
-    other_side = jnp.where(core == 0, grad_side[:, 1], grad_side[:, 0])
+    own_side = grad_side[:, 0]
+    other_side = grad_side[:, 1]
     got_side = lax.ppermute(other_side, "ec", swap)
     tn = (((0,), (0,)), ((), ()))
     chip_term = lax.dot_general(

time: 159 us -> 157 us (0.987)
    dot_general x1, matrix products: 4.15 us -> 1.59 us  [expert_math(): results = lax.dot_general(out_side, w_two, nt, preferred_element_type=f32)]
    select_n x2 -> x0, other arithmetic: 1.98 us -> none  [the longest x1 1.07 us: per_device(): w_pair = jnp.where(core == 0, w_pair, w_pair[:, ::-1])]
    dot_general x1, matrix products: 1.61 us -> 3.39 us  [expert_math(): jnp.dot(flat, w_two, preferred_element_type=f32)]
where the time goes in v14:
time: 157 us; the launch traced here: 156 us
  blocking collectives  54.2 us (35%)
  waiting for transfers between devices  37.4 us (24%)
  starting transfers between devices  19.2 us (12%)
  between operations  14.3 us (9%)
  matrix products  13.8 us (9%)
  local copies, waits for them, and re-layouts  9.02 us (6%)
  other arithmetic  8.3 us (5%)
    all_to_all x1, blocking collectives, per_device(): lax.all_to_all(pair, ('ex', 'ez'), split_axis=0, concat_axis=0, tiled=True)  54.2 us
    all_gather x1, waiting for transfers between devices, per_device(): lax.all_gather(w_loc, 'dp', axis=0, tiled=False).reshape(-1, 3 * hid)  33.3 us
    all_to_all x1, starting transfers between devices, per_device(): lax.all_to_all(outgoing, ('ex', 'ez'), split_axis=0, concat_axis=0, tiled...  12.6 us
    all_gather x1, local copies, waits for them, and re-layouts, per_device(): lax.all_gather(w_loc, 'dp', axis=0, tiled=False).reshape(-1, 3 * hid)  4.57 us
    all_to_all x1, waiting for transfers between devices, per_device(): lax.all_to_all(outgoing, ('ex', 'ez'), split_axis=0, concat_axis=0, tiled...  4.07 us
    dot_general x1, matrix products, expert_math(): jnp.dot(flat, w_two, preferred_element_type=f32)  3.39 us
  transfers between devices with their start and end apart: 6, of which 2 were waited for; matrix products, arithmetic and copies ran while one was open for 16% of the time, Pallas kernels for 0%

profile of v14, /device:TPU:64, one launch (start us, length us, event | category | flops | bytes accessed | tf_op | source)
XLA Modules:
  0.0 156.2 jit_solution(8604186943643258050)
XLA Ops:
  7.2 1.9 %pad_maximum_fusion.3 = bf16[448,384]{1,0:T(8,128)(2,1)} fusion(bf16[448,128]{1,0:T(8,128)(2,1)} %bitcast.110, bf16[448,128]{1,0:T(8,128)(2,1)} %bitcast.111, bf16[448,128]{1,0:T(8,128)(2,1)} %bitcast.112), kind=kLoop, calls=%fused_computation.22 | loop fusion | flops 1032192 | bytes 688128 | tf_op jit(solution)/shard_map/concatenate | solution.py:59
  9.1 0.7 fusion.15
  9.8 0.1 copy.46
  9.9 0.2 reduce_window_sum.11
  10.2 0.7 select_reduce_fusion
  11.1 0.2 convolution_convert_fusion.1
  11.4 1.4 fusion.6
  12.8 0.1 pad_maximum_fusion.4
  12.9 1.4 broadcast_in_dim.51
  14.3 12.6 %all-to-all-start = ((bf16[32,8,3584]{2,1,0:T(8,128)(2,1)}), bf16[32,8,3584]{2,1,0:T(8,128)(2,1)S(1)}, u32[]{:S(2)}, u32[]{:S(2)}) async-start(bf16[32,8,3584]{2,1,0:T(8,128)(2,1)} %bitcast.101), calls=%async_computation | async-start | bytes 3670016 | tf_op jit(solution)/shard_map/all_to_all | solution.py:76
  26.9 33.3 %all-gather.3.cloned.1.call-done = bf16[3584,384]{1,0:T(8,128)(2,1)} async-done(((bf16[448,384]{1,0:T(8,128)(2,1)}), bf16[3584,384]{1,0:T(8,128)(2,1)}) %all-gather.3.cloned.1.call-update) | async-done | bytes 2752528 | tf_op jit(solution)/shard_map/all_gather | solution.py:60
  60.3 4.6 %copy.52 = bf16[3584,384]{0,1:T(8,128)(2,1)} copy(bf16[3584,384]{1,0:T(8,128)(2,1)} %all-gather.3.cloned.1.call-done) | data formatting | bytes 5505024 | tf_op jit(solution)/shard_map/all_gather | solution.py:60
  64.8 1.9 %collective-permute-start = (bf16[3584,384]{0,1:T(8,128)(2,1)}, bf16[3584,384]{0,1:T(8,128)(2,1)}, u32[]{:S(2)}, u32[]{:S(2)}) collective-permute-start(bf16[3584,384]{0,1:T(8,128)(2,1)} %copy.52), channel_id=1, source_target_pairs={{0,1},{1,0},{2,3},{3,2},{4,5},{5,4},{6,7},{7,6},{8,9},{9,8},{10,11... | collective-permute-start | bytes 8257544 | tf_op jit(solution)/shard_map/ppermute | solution.py:61
  66.7 4.1 %all-to-all-done = bf16[32,8,3584]{2,1,0:T(8,128)(2,1)S(1)} async-done(((bf16[32,8,3584]{2,1,0:T(8,128)(2,1)}), bf16[32,8,3584]{2,1,0:T(8,128)(2,1)S(1)}, u32[]{:S(2)}, u32[]{:S(2)}) %all-to-all-start) | async-done | bytes 1835040 | tf_op jit(solution)/shard_map/all_to_all | solution.py:76
  70.8 2.2 %collective-permute-start.1 = (bf16[32,8,3584]{2,1,0:T(8,128)(2,1)S(1)}, bf16[32,8,3584]{2,1,0:T(8,128)(2,1)S(1)}, u32[]{:S(2)}, u32[]{:S(2)}) collective-permute-start(bf16[32,8,3584]{2,1,0:T(8,128)(2,1)S(1)} %all-to-all-done), channel_id=1, source_target_pairs={{0,1},{1,0},{2,3},{3,2},{4,5},{5,4},{6,7},{7,6},{8,9},{9,8},{10,11... | collective-permute-start | bytes 5505032 | tf_op jit(solution)/shard_map/ppermute | solution.py:77
  73.0 0.5 copy.51
  73.6 3.4 %fusion.1 = f32[32,2,4,2,384]{4,0,3,2,1:T(8,128)S(1)} fusion(bf16[32,2,4,3584,1]{3,0,4,2,1:T(8,128)(2,1)S(1)} %bitcast.104, bf16[3584,1,384]{0,2,1:T(8,128)(2,1)} %bitcast.10, bf16[3584,1,384]{0,2,1:T(8,128)(2,1)S(1)} %bitcast.100), kind=kOutput, calls=%fused_computation.3 | convolution fusion | flops 1420296192 | bytes 8126464 | tf_op jit(solution)/shard_map/dot_general | solution.py:35
  77.2 0.3 copy.56
  77.5 0.5 fusion.29
  78.1 2.4 %collective-permute-start.2 = (bf16[256,384]{1,0:T(8,128)(2,1)S(1)}, bf16[256,384]{1,0:T(8,128)(2,1)S(1)}, u32[]{:S(2)}, u32[]{:S(2)}) collective-permute-start(bf16[256,384]{1,0:T(8,128)(2,1)S(1)} %bitcast.109), channel_id=1, source_target_pairs={{0,1},{1,0},{2,3},{3,2},{4,5},{5,4},{6,7},{7,6},{8,9},{9,8},{10,11... | collective-permute-start | bytes 589832 | tf_op jit(solution)/shard_map/ppermute | solution.py:81
  80.6 1.1 fusion.8
  81.7 2.7 %fusion = bf16[3584,384]{1,0:T(8,128)(2,1)} fusion(f32[3584,384]{1,0:T(8,128)S(1)} %fusion.8, bf16[256,384]{1,0:T(8,128)(2,1)S(1)} %collective-permute-done.2, bf16[32,8,3584]{2,1,0:T(8,128)(2,1)S(1)} %collective-permute-done.1), kind=kOutput, calls=%fused_computation.1 | convolution fusion | flops 707395584 | bytes 10289152 | tf_op jit(solution)/shard_map/dot_general | solution.py:85
  84.4 0.3 copy.54
  84.8 3.1 %pad_maximum_fusion = bf16[3584,2,384]{0,2,1:T(8,128)(2,1)S(1)} fusion(bf16[3584,1,384]{0,2,1:T(8,128)(2,1)} %bitcast.10, bf16[3584,1,384]{0,2,1:T(8,128)(2,1)} %bitcast.99), kind=kLoop, calls=%fused_computation.2 | loop fusion | flops 2752512 | bytes 11010048 | tf_op jit(solution)/shard_map/stack | solution.py:62
  87.9 1.6 %fusion.3 = bf16[32,8,3584]{2,1,0:T(8,128)(2,1)S(1)} fusion(bf16[256,768]{1,0:T(8,128)(2,1)S(1)} %bitcast.106, bf16[3584,768]{0,1:T(8,128)(2,1)S(1)} %bitcast.102), kind=kOutput, calls=%fused_computation.6 | convolution fusion | flops 1410203648 | bytes 7733248 | tf_op jit(solution)/shard_map/dot_general | solution.py:49
  89.5 54.2 %all_to_all.10 = bf16[32,8,3584]{2,1,0:T(8,128)(2,1)S(1)} all-to-all(bf16[32,8,3584]{2,1,0:T(8,128)(2,1)S(1)} %fusion.3), channel_id=1, replica_groups=mesh['dp'=8,'ex'=4,'ez'=8,'ec'=2] {'ex','ez'}, dimensions={0} | all-to-all | bytes 3670016 | tf_op jit(solution)/shard_map/all_to_all | solution.py:93
  143.7 0.2 bitcast_reduce_fusion
  144.0 0.1 copy.55
  144.1 1.4 fusion.5
  145.5 1.9 %fusion.4 = bf16[128,3584]{1,0:T(8,128)(2,1)} fusion(bf16[4,2,4,3584]{3,0,2,1:T(4,128)(2,1)S(1)} %bitcast.108, f32[4,4]{0,1:T(4,128)S(1)} %get-tuple-element.16, s32[128,4]{0,1:T(4,128)S(1)} %copy.47, pred[128,4]{0,1:T(4,128)(4,1)S(1)} %fusion.15), kind=kOutput, calls=%fused_computation.9 | convolution fusion | flops 88547328 | bytes 1036800 | tf_op jit(solution)/shard_map/tec,ecf->tf/dot_general | solution.py:98
  147.4 1.0 convert_element_type.62
  148.5 0.9 slice_bitcast_fusion
  (25 shorter events, 0.7 us)
Async XLA Ops:
  7.2 4.0 %copy-start = (bf16[128,3584]{1,0:T(8,128)(2,1)S(1)}, bf16[128,3584]{1,0:T(8,128)(2,1)}, u32[]{:S(2)}) copy-start(bf16[128,3584]{1,0:T(8,128)(2,1)} %param.7) | copy-start | bytes 2752516
  7.2 53.1 %all-gather.3.cloned.1.call-start = ((), (), s32[]{:S(2)}) async-start(), calls=%async_computation.4 | async-start | bytes 3096576 | tf_op jit(solution)/shard_map/all_gather | solution.py:60
  14.3 56.5 %all-to-all-start = ((bf16[32,8,3584]{2,1,0:T(8,128)(2,1)}), bf16[32,8,3584]{2,1,0:T(8,128)(2,1)S(1)}, u32[]{:S(2)}, u32[]{:S(2)}) async-start(bf16[32,8,3584]{2,1,0:T(8,128)(2,1)} %bitcast.101), calls=%async_computation | async-start | bytes 3670016 | tf_op jit(solution)/shard_map/all_to_all | solution.py:76
  26.9 120.6 %reduce-scatter.2.cloned.1.call-start = ((), (), s32[]{:S(2)}) async-start(), calls=%async_computation.3 | async-start | bytes 3096576 | tf_op jit(solution)/shard_map/reduce_scatter | solution.py:86
  64.8 8.7 %collective-permute-start = (bf16[3584,384]{0,1:T(8,128)(2,1)}, bf16[3584,384]{0,1:T(8,128)(2,1)}, u32[]{:S(2)}, u32[]{:S(2)}) collective-permute-start(bf16[3584,384]{0,1:T(8,128)(2,1)} %copy.52), channel_id=1, source_target_pairs={{0,1},{1,0},{2,3},{3,2},{4,5},{5,4},{6,7},{7,6},{8,9},{9,8},{10,11... | collective-permute-start | bytes 8257544 | tf_op jit(solution)/shard_map/ppermute | solution.py:61
  70.8 2.8 %copy-start.1 = (bf16[3584,384]{0,1:T(8,128)(2,1)S(1)}, bf16[3584,384]{0,1:T(8,128)(2,1)}, u32[]{:S(2)}) copy-start(bf16[3584,384]{0,1:T(8,128)(2,1)} %copy.52) | copy-start | bytes 8257540
  70.8 10.9 %collective-permute-start.1 = (bf16[32,8,3584]{2,1,0:T(8,128)(2,1)S(1)}, bf16[32,8,3584]{2,1,0:T(8,128)(2,1)S(1)}, u32[]{:S(2)}, u32[]{:S(2)}) collective-permute-start(bf16[32,8,3584]{2,1,0:T(8,128)(2,1)S(1)} %all-to-all-done), channel_id=1, source_target_pairs={{0,1},{1,0},{2,3},{3,2},{4,5},{5,4},{6,7},{7,6},{8,9},{9,8},{10,11... | collective-permute-start | bytes 5505032 | tf_op jit(solution)/shard_map/ppermute | solution.py:77
  78.1 3.6 %collective-permute-start.2 = (bf16[256,384]{1,0:T(8,128)(2,1)S(1)}, bf16[256,384]{1,0:T(8,128)(2,1)S(1)}, u32[]{:S(2)}, u32[]{:S(2)}) collective-permute-start(bf16[256,384]{1,0:T(8,128)(2,1)S(1)} %bitcast.109), channel_id=1, source_target_pairs={{0,1},{1,0},{2,3},{3,2},{4,5},{5,4},{6,7},{7,6},{8,9},{9,8},{10,11... | collective-permute-start | bytes 589832 | tf_op jit(solution)/shard_map/ppermute | solution.py:81
Sparse Core Ops, SparseCore 0:
  10.7 49.5 all-gather.2
  84.6 44.8 reduce-scatter.1

commit v15 on v14

--- a/solution.py
+++ b/solution.py
@@ -95,7 +95,9 @@
         returned.reshape(window, zsize, 2 * CAP, width).astype(f32), axis=1
     ).astype(jnp.bfloat16).reshape(window, 2, CAP, width)
     weighted = select * slot_gate[None, :, :]
-    layer_out = jnp.einsum("tec,ecf->tf", weighted, combined[:, 0].astype(f32), precision=HIGH)
+    layer_out = jnp.einsum(
+        "tec,ecf->tf", weighted, combined[:, 0].astype(f32), precision=lax.Precision.HIGH
+    )
     token_grad = jnp.einsum("tec,ecf->tf", select_b, combined[:, 1], preferred_element_type=f32)
     return (
         layer_out.astype(jnp.bfloat16),

time: 157 us -> 157 us (level)
  no operation moved by 1% of the time
where the time goes in v15:
time: 157 us; the launch traced here: 156 us
  blocking collectives  54.2 us (35%)
  waiting for transfers between devices  37.4 us (24%)
  starting transfers between devices  19.2 us (12%)
  between operations  14.3 us (9%)
  matrix products  13.5 us (9%)
  local copies, waits for them, and re-layouts  9.02 us (6%)
  other arithmetic  8.3 us (5%)
    all_to_all x1, blocking collectives, per_device(): lax.all_to_all(pair, ('ex', 'ez'), split_axis=0, concat_axis=0, tiled=True)  54.2 us
    all_gather x1, waiting for transfers between devices, per_device(): lax.all_gather(w_loc, 'dp', axis=0, tiled=False).reshape(-1, 3 * hid)  33.3 us
    all_to_all x1, starting transfers between devices, per_device(): lax.all_to_all(outgoing, ('ex', 'ez'), split_axis=0, concat_axis=0, tiled...  12.6 us
    all_gather x1, local copies, waits for them, and re-layouts, per_device(): lax.all_gather(w_loc, 'dp', axis=0, tiled=False).reshape(-1, 3 * hid)  4.57 us
    all_to_all x1, waiting for transfers between devices, per_device(): lax.all_to_all(outgoing, ('ex', 'ez'), split_axis=0, concat_axis=0, tiled...  4.07 us
    dot_general x1, matrix products, expert_math(): jnp.dot(flat, w_two, preferred_element_type=f32)  3.39 us
  transfers between devices with their start and end apart: 6, of which 2 were waited for; matrix products, arithmetic and copies ran while one was open for 16% of the time, Pallas kernels for 0%

profile of v15, /device:TPU:64, one launch (start us, length us, event | category | flops | bytes accessed | tf_op | source)
XLA Modules:
  0.0 155.9 jit_solution(15340039957294404625)
XLA Ops:
  7.2 1.9 %pad_maximum_fusion.3 = bf16[448,384]{1,0:T(8,128)(2,1)} fusion(bf16[448,128]{1,0:T(8,128)(2,1)} %bitcast.110, bf16[448,128]{1,0:T(8,128)(2,1)} %bitcast.111, bf16[448,128]{1,0:T(8,128)(2,1)} %bitcast.112), kind=kLoop, calls=%fused_computation.22 | loop fusion | flops 1032192 | bytes 688128 | tf_op jit(solution)/shard_map/concatenate | solution.py:59
  9.1 0.7 fusion.15
  9.8 0.1 copy.46
  9.9 0.2 reduce_window_sum.11
  10.2 0.7 select_reduce_fusion
  11.1 0.2 convolution_convert_fusion.1
  11.4 1.4 fusion.6
  12.8 0.1 pad_maximum_fusion.4
  12.9 1.4 broadcast_in_dim.51
  14.3 12.6 %all-to-all-start = ((bf16[32,8,3584]{2,1,0:T(8,128)(2,1)}), bf16[32,8,3584]{2,1,0:T(8,128)(2,1)S(1)}, u32[]{:S(2)}, u32[]{:S(2)}) async-start(bf16[32,8,3584]{2,1,0:T(8,128)(2,1)} %bitcast.101), calls=%async_computation | async-start | bytes 3670016 | tf_op jit(solution)/shard_map/all_to_all | solution.py:76
  26.9 33.3 %all-gather.3.cloned.1.call-done = bf16[3584,384]{1,0:T(8,128)(2,1)} async-done(((bf16[448,384]{1,0:T(8,128)(2,1)}), bf16[3584,384]{1,0:T(8,128)(2,1)}) %all-gather.3.cloned.1.call-update) | async-done | bytes 2752528 | tf_op jit(solution)/shard_map/all_gather | solution.py:60
  60.3 4.6 %copy.52 = bf16[3584,384]{0,1:T(8,128)(2,1)} copy(bf16[3584,384]{1,0:T(8,128)(2,1)} %all-gather.3.cloned.1.call-done) | data formatting | bytes 5505024 | tf_op jit(solution)/shard_map/all_gather | solution.py:60
  64.8 1.9 %collective-permute-start = (bf16[3584,384]{0,1:T(8,128)(2,1)}, bf16[3584,384]{0,1:T(8,128)(2,1)}, u32[]{:S(2)}, u32[]{:S(2)}) collective-permute-start(bf16[3584,384]{0,1:T(8,128)(2,1)} %copy.52), channel_id=1, source_target_pairs={{0,1},{1,0},{2,3},{3,2},{4,5},{5,4},{6,7},{7,6},{8,9},{9,8},{10,11... | collective-permute-start | bytes 8257544 | tf_op jit(solution)/shard_map/ppermute | solution.py:61
  66.7 4.1 %all-to-all-done = bf16[32,8,3584]{2,1,0:T(8,128)(2,1)S(1)} async-done(((bf16[32,8,3584]{2,1,0:T(8,128)(2,1)}), bf16[32,8,3584]{2,1,0:T(8,128)(2,1)S(1)}, u32[]{:S(2)}, u32[]{:S(2)}) %all-to-all-start) | async-done | bytes 1835040 | tf_op jit(solution)/shard_map/all_to_all | solution.py:76
  70.8 2.2 %collective-permute-start.1 = (bf16[32,8,3584]{2,1,0:T(8,128)(2,1)S(1)}, bf16[32,8,3584]{2,1,0:T(8,128)(2,1)S(1)}, u32[]{:S(2)}, u32[]{:S(2)}) collective-permute-start(bf16[32,8,3584]{2,1,0:T(8,128)(2,1)S(1)} %all-to-all-done), channel_id=1, source_target_pairs={{0,1},{1,0},{2,3},{3,2},{4,5},{5,4},{6,7},{7,6},{8,9},{9,8},{10,11... | collective-permute-start | bytes 5505032 | tf_op jit(solution)/shard_map/ppermute | solution.py:77
  73.0 0.5 copy.51
  73.6 3.4 %fusion.1 = f32[32,2,4,2,384]{4,0,3,2,1:T(8,128)S(1)} fusion(bf16[32,2,4,3584,1]{3,0,4,2,1:T(8,128)(2,1)S(1)} %bitcast.104, bf16[3584,1,384]{0,2,1:T(8,128)(2,1)} %bitcast.10, bf16[3584,1,384]{0,2,1:T(8,128)(2,1)S(1)} %bitcast.100), kind=kOutput, calls=%fused_computation.3 | convolution fusion | flops 1420296192 | bytes 8126464 | tf_op jit(solution)/shard_map/dot_general | solution.py:35
  77.2 0.3 copy.56
  77.5 0.5 fusion.29
  78.1 2.4 %collective-permute-start.2 = (bf16[256,384]{1,0:T(8,128)(2,1)S(1)}, bf16[256,384]{1,0:T(8,128)(2,1)S(1)}, u32[]{:S(2)}, u32[]{:S(2)}) collective-permute-start(bf16[256,384]{1,0:T(8,128)(2,1)S(1)} %bitcast.109), channel_id=1, source_target_pairs={{0,1},{1,0},{2,3},{3,2},{4,5},{5,4},{6,7},{7,6},{8,9},{9,8},{10,11... | collective-permute-start | bytes 589832 | tf_op jit(solution)/shard_map/ppermute | solution.py:81
  80.6 1.1 fusion.8
  81.7 2.7 %fusion = bf16[3584,384]{1,0:T(8,128)(2,1)} fusion(f32[3584,384]{1,0:T(8,128)S(1)} %fusion.8, bf16[256,384]{1,0:T(8,128)(2,1)S(1)} %collective-permute-done.2, bf16[32,8,3584]{2,1,0:T(8,128)(2,1)S(1)} %collective-permute-done.1), kind=kOutput, calls=%fused_computation.1 | convolution fusion | flops 707395584 | bytes 10289152 | tf_op jit(solution)/shard_map/dot_general | solution.py:85
  84.4 0.3 copy.54
  84.8 3.1 %pad_maximum_fusion = bf16[3584,2,384]{0,2,1:T(8,128)(2,1)S(1)} fusion(bf16[3584,1,384]{0,2,1:T(8,128)(2,1)} %bitcast.10, bf16[3584,1,384]{0,2,1:T(8,128)(2,1)} %bitcast.99), kind=kLoop, calls=%fused_computation.2 | loop fusion | flops 2752512 | bytes 11010048 | tf_op jit(solution)/shard_map/stack | solution.py:62
  87.9 1.6 %fusion.3 = bf16[32,8,3584]{2,1,0:T(8,128)(2,1)S(1)} fusion(bf16[256,768]{1,0:T(8,128)(2,1)S(1)} %bitcast.106, bf16[3584,768]{0,1:T(8,128)(2,1)S(1)} %bitcast.102), kind=kOutput, calls=%fused_computation.6 | convolution fusion | flops 1410203648 | bytes 7733248 | tf_op jit(solution)/shard_map/dot_general | solution.py:49
  89.5 54.2 %all_to_all.10 = bf16[32,8,3584]{2,1,0:T(8,128)(2,1)S(1)} all-to-all(bf16[32,8,3584]{2,1,0:T(8,128)(2,1)S(1)} %fusion.3), channel_id=1, replica_groups=mesh['dp'=8,'ex'=4,'ez'=8,'ec'=2] {'ex','ez'}, dimensions={0} | all-to-all | bytes 3670016 | tf_op jit(solution)/shard_map/all_to_all | solution.py:93
  143.7 0.2 bitcast_reduce_fusion
  144.0 0.1 copy.55
  144.1 1.4 fusion.5
  145.5 1.7 %fusion.4 = bf16[128,3584]{1,0:T(8,128)(2,1)} fusion(bf16[4,2,4,3584]{3,0,2,1:T(4,128)(2,1)S(1)} %bitcast.108, f32[4,4]{0,1:T(4,128)S(1)} %get-tuple-element.16, s32[128,4]{0,1:T(4,128)S(1)} %copy.47, pred[128,4]{0,1:T(4,128)(4,1)S(1)} %fusion.15), kind=kOutput, calls=%fused_computation.9 | convolution fusion | flops 44507136 | bytes 1036800 | tf_op jit(solution)/shard_map/tec,ecf->tf/dot_general | solution.py:98
  147.2 1.0 convert_element_type.62
  148.2 0.9 slice_bitcast_fusion
  (25 shorter events, 0.7 us)
Async XLA Ops:
  7.2 4.0 %copy-start = (bf16[128,3584]{1,0:T(8,128)(2,1)S(1)}, bf16[128,3584]{1,0:T(8,128)(2,1)}, u32[]{:S(2)}) copy-start(bf16[128,3584]{1,0:T(8,128)(2,1)} %param.7) | copy-start | bytes 2752516
  7.2 53.1 %all-gather.3.cloned.1.call-start = ((), (), s32[]{:S(2)}) async-start(), calls=%async_computation.4 | async-start | bytes 3096576 | tf_op jit(solution)/shard_map/all_gather | solution.py:60
  14.3 56.5 %all-to-all-start = ((bf16[32,8,3584]{2,1,0:T(8,128)(2,1)}), bf16[32,8,3584]{2,1,0:T(8,128)(2,1)S(1)}, u32[]{:S(2)}, u32[]{:S(2)}) async-start(bf16[32,8,3584]{2,1,0:T(8,128)(2,1)} %bitcast.101), calls=%async_computation | async-start | bytes 3670016 | tf_op jit(solution)/shard_map/all_to_all | solution.py:76
  26.9 120.3 %reduce-scatter.2.cloned.1.call-start = ((), (), s32[]{:S(2)}) async-start(), calls=%async_computation.3 | async-start | bytes 3096576 | tf_op jit(solution)/shard_map/reduce_scatter | solution.py:86
  64.8 8.7 %collective-permute-start = (bf16[3584,384]{0,1:T(8,128)(2,1)}, bf16[3584,384]{0,1:T(8,128)(2,1)}, u32[]{:S(2)}, u32[]{:S(2)}) collective-permute-start(bf16[3584,384]{0,1:T(8,128)(2,1)} %copy.52), channel_id=1, source_target_pairs={{0,1},{1,0},{2,3},{3,2},{4,5},{5,4},{6,7},{7,6},{8,9},{9,8},{10,11... | collective-permute-start | bytes 8257544 | tf_op jit(solution)/shard_map/ppermute | solution.py:61
  70.8 2.8 %copy-start.1 = (bf16[3584,384]{0,1:T(8,128)(2,1)S(1)}, bf16[3584,384]{0,1:T(8,128)(2,1)}, u32[]{:S(2)}) copy-start(bf16[3584,384]{0,1:T(8,128)(2,1)} %copy.52) | copy-start | bytes 8257540
  70.8 10.9 %collective-permute-start.1 = (bf16[32,8,3584]{2,1,0:T(8,128)(2,1)S(1)}, bf16[32,8,3584]{2,1,0:T(8,128)(2,1)S(1)}, u32[]{:S(2)}, u32[]{:S(2)}) collective-permute-start(bf16[32,8,3584]{2,1,0:T(8,128)(2,1)S(1)} %all-to-all-done), channel_id=1, source_target_pairs={{0,1},{1,0},{2,3},{3,2},{4,5},{5,4},{6,7},{7,6},{8,9},{9,8},{10,11... | collective-permute-start | bytes 5505032 | tf_op jit(solution)/shard_map/ppermute | solution.py:77
  78.1 3.6 %collective-permute-start.2 = (bf16[256,384]{1,0:T(8,128)(2,1)S(1)}, bf16[256,384]{1,0:T(8,128)(2,1)S(1)}, u32[]{:S(2)}, u32[]{:S(2)}) collective-permute-start(bf16[256,384]{1,0:T(8,128)(2,1)S(1)} %bitcast.109), channel_id=1, source_target_pairs={{0,1},{1,0},{2,3},{3,2},{4,5},{5,4},{6,7},{7,6},{8,9},{9,8},{10,11... | collective-permute-start | bytes 589832 | tf_op jit(solution)/shard_map/ppermute | solution.py:81
Sparse Core Ops, SparseCore 0:
  10.7 49.5 all-gather.2
  84.6 44.8 reduce-scatter.1
